TPU v7x, 128 devices: a whole 4x4x4 slice. The times are simulated.
128 devices in a mesh: lat: 8 (over z, y_hi), lon: 16 (over x, y_lo, core).
Axes of the slice: x: 4, y: 4 (y_hi: 2, y_lo: 2; y = y_hi * 2 + y_lo), z: 4, core: 2. Of those that a mesh axis runs over, the one named last changes fastest.
Arguments:
- tracer: float32 [10, 768, 2048], P(None, 'lat', 'lon'), may hold values from -6 to 6
- velocity: float32 [10, 768, 2048], P(None, 'lat', 'lon'), may hold values from -6 to 6
- tracer_adjoint: float32 [10, 768, 2048], P(None, 'lat', 'lon'), may hold values from -6 to 6
- velocity_adjoint: float32 [10, 768, 2048], P(None, 'lat', 'lon'), may hold values from -6 to 6
- sea_mask: int32 [10, 768, 2048], P(None, 'lat', 'lon'), may hold values from 0 to 1, as said below
- face_east: float32 [768, 2048], P('lat', 'lon'), may hold values from 0.03 to 0.2
- face_north: float32 [768, 2048], P('lat', 'lon'), may hold values from 0.03 to 0.2
- viscosity: float32 [768, 2048], P('lat', 'lon'), may hold values from 0.1 to 0.7
- conv_first: float32 [3, 32, 20], replicated, may hold values from -0.75 to 0.75
- conv_middle: float32 [3, 32, 32], replicated, may hold values from -0.625 to 0.625
- conv_last: float32 [3, 20, 32], replicated, may hold values from -0.625 to 0.625
Outputs:
- tracer_grad: float32 [10, 768, 2048], P(None, 'lat', 'lon')
- velocity_grad: float32 [10, 768, 2048], P(None, 'lat', 'lon')
- first_grad: float32 [3, 32, 20], replicated
- middle_grad: float32 [3, 32, 32], replicated
- last_grad: float32 [3, 20, 32], replicated
Inputs may be any that keep to these rules, and one draw needn't show every extreme that they name: `sea_mask`: in each column a cell is sea from the top level down to the column's depth and land below it; a depth may be zero (a land column).
All inputs are finite; a program needn't handle non-finite values.
Results may differ from a plain program's by a relative error of at most 0.00015.
Values sent between devices are 32-bit elements; how exact they have to be, the bound alone decides.
No kernel may reach another device: no remote copies, remote signals or barrier semaphores. Data moves between devices by JAX's collectives and lax.ppermute only.
A program may use at most 128 MiB of HBM per device.

v0:
```python
import math

import jax
import jax.numpy as jnp
from jax import lax
from jax.sharding import PartitionSpec as P

KW = 3


highest = lax.Precision.HIGH


def edges(block):
    def ring(axis, step):
        count = lax.axis_size(axis)
        return [(i, (i + step) % count) for i in range(count)]

    below = lax.ppermute(block[..., -1:, :], "lat", ring("lat", 1))
    above = lax.ppermute(block[..., :1, :], "lat", ring("lat", -1))
    left = lax.ppermute(block[..., :, -1:], "lon", ring("lon", 1))
    right = lax.ppermute(block[..., :, :1], "lon", ring("lon", -1))
    return below, above, left, right


def shifted(block, halo):
    below, above, left, right = halo
    east = jnp.concatenate([block[..., :, 1:], right], axis=-1)
    west = jnp.concatenate([left, block[..., :, :-1]], axis=-1)
    north = jnp.concatenate([block[..., 1:, :], above], axis=-2)
    south = jnp.concatenate([below, block[..., :-1, :]], axis=-2)
    return east, west, north, south


def laplace(values, value_halo, sea, sea_near, face_east, face_west, face_north, face_south):
    east, west, north, south = shifted(values, value_halo)
    sea_east, sea_west, sea_north, sea_south = sea_near
    summed = face_east * sea * sea_east * (east - values)
    summed = summed + face_west * sea_west * sea * (west - values)
    summed = summed + face_north * sea * sea_north * (north - values)
    summed = summed + face_south * sea_south * sea * (south - values)
    return summed


def row_inside(step):
    index = lax.axis_index("lat") + step
    return ((index >= 0) & (index < lax.axis_size("lat"))).astype(jnp.float32)


def lon_roll(values, step):
    if step == 1:
        return jnp.concatenate([jnp.roll(values[..., -1:], 1, axis=0), values[..., :-1]], axis=-1)
    if step == -1:
        return jnp.concatenate([values[..., 1:], jnp.roll(values[..., :1], -1, axis=0)], axis=-1)
    return values


def stack_taps(values):
    return jnp.concatenate([lon_roll(values, 1), values, lon_roll(values, -1)], axis=1)


def unstack_taps(stacked, channels):
    first = lon_roll(stacked[:, :channels], -1)
    middle = stacked[:, channels : 2 * channels]
    last = lon_roll(stacked[:, 2 * channels :], 1)
    return first + middle + last


def flat_kernel(kernel):
    taps, outs, ins = kernel.shape
    return kernel.transpose(1, 0, 2).reshape(outs, taps * ins)


def kernel_of(flat, taps):
    outs, width = flat.shape
    return flat.reshape(outs, taps, width // taps).transpose(1, 0, 2)


def apply(flat, stacked):
    return jnp.einsum("oc,scml->soml", flat, stacked, precision=highest)


def network_vjp(weights, values, adjoint):
    flats = [flat_kernel(weight) for weight in weights]
    taps = weights[0].shape[0]
    in_stack = stack_taps(values)
    first = jnp.tanh(apply(flats[0], in_stack))
    first_stack = stack_taps(first)
    second = jnp.tanh(apply(flats[1], first_stack))
    second_stack = stack_taps(second)
    last_grad = jnp.einsum("soml,scml->oc", adjoint, second_stack, precision=highest)
    back = jnp.einsum("oc,soml->scml", flats[2], adjoint, precision=highest)
    second_delta = unstack_taps(back, second.shape[1]) * (1.0 - second * second)
    middle_grad = jnp.einsum("soml,scml->oc", second_delta, first_stack, precision=highest)
    back = jnp.einsum("oc,soml->scml", flats[1], second_delta, precision=highest)
    first_delta = unstack_taps(back, first.shape[1]) * (1.0 - first * first)
    first_grad = jnp.einsum("soml,scml->oc", first_delta, in_stack, precision=highest)
    back = jnp.einsum("oc,soml->scml", flats[0], first_delta, precision=highest)
    input_grad = unstack_taps(back, values.shape[1])
    grads = (kernel_of(first_grad, taps), kernel_of(middle_grad, taps), kernel_of(last_grad, taps))
    return grads, input_grad


LANES = 128


def butterfly_sum(values, axes):
    for axis in axes:
        size = lax.axis_size(axis)
        stride = 1
        while stride < size:
            pairs = [(i, i ^ stride) for i in range(size)]
            values = values + lax.ppermute(values, axis, pairs)
            stride *= 2
    return values


def pack(parts):
    flat = jnp.concatenate([part.reshape(-1) for part in parts])
    rows = -(-flat.shape[0] // LANES)
    flat = jnp.pad(flat, (0, rows * LANES - flat.shape[0]))
    return flat.reshape(rows, LANES)


def unpack(total, parts):
    total = total.reshape(-1)
    out, start = [], 0
    for part in parts:
        out.append(total[start : start + part.size].reshape(part.shape))
        start += part.size
    return out


def on_device(
    tracer,
    velocity,
    tracer_adjoint,
    velocity_adjoint,
    sea_mask,
    face_east,
    face_north,
    viscosity,
    conv_first,
    conv_middle,
    conv_last,
):
    levels = tracer.shape[0]
    tile_rows = tracer.shape[1]
    tile_cols = tracer.shape[2]
    sea_cells = sea_mask.astype(jnp.float32)
    planes = jnp.concatenate(
        [tracer_adjoint, velocity_adjoint, sea_cells, face_east[None], face_north[None]], axis=0
    )
    plane_halo = edges(planes)
    weights = (conv_first, conv_middle, conv_last)
    inputs = jnp.concatenate([tracer, velocity], axis=0)
    masked_adjoint = jnp.concatenate(
        [tracer_adjoint * sea_cells, velocity_adjoint * sea_cells], axis=0
    )
    stacked = jnp.concatenate([inputs, masked_adjoint], axis=0)
    blocks = lax.axis_size("lon")
    chunks = stacked.reshape(stacked.shape[0], tile_rows // blocks, blocks, tile_cols)
    band = lax.all_to_all(chunks.transpose(2, 0, 1, 3), "lon", split_axis=0, concat_axis=0, tiled=True)
    weight_grads, band_grad = network_vjp(weights, band[:, : 2 * levels], band[:, 2 * levels :])
    packed = pack(weight_grads)
    packed, plane_halo = lax.optimization_barrier((packed, plane_halo))
    summed = unpack(butterfly_sum(packed, ("lon", "lat")), weight_grads)
    returned = lax.all_to_all(band_grad, "lon", split_axis=0, concat_axis=0, tiled=True)
    input_grad = returned.transpose(1, 2, 0, 3).reshape(2 * levels, tile_rows, tile_cols)
    below, above, left, right = plane_halo
    below = below * row_inside(-1)
    above = above * row_inside(1)

    def part(lo, hi):
        return tuple(piece[lo:hi] for piece in (below, above, left, right))

    sea_near = shifted(sea_cells, part(2 * levels, 3 * levels))
    face_west = jnp.concatenate([left[3 * levels], face_east[:, :-1]], axis=-1)
    face_south = jnp.concatenate([below[3 * levels + 1], face_north[:-1, :]], axis=-2)
    faces = (face_east, face_west, face_north, face_south)
    tracer_term = laplace(tracer_adjoint, part(0, levels), sea_cells, sea_near, *faces)
    first_laplace = laplace(velocity_adjoint, part(levels, 2 * levels), sea_cells, sea_near, *faces)
    scaled = viscosity * first_laplace
    viscous_term = laplace(scaled, edges(scaled), sea_cells, sea_near, *faces)
    scale = 1.0 / math.sqrt(tile_rows * lax.axis_size("lat") * tile_cols * lax.axis_size("lon"))
    tracer_grad = tracer_adjoint + tracer_term + input_grad[:levels]
    velocity_grad = velocity_adjoint - viscous_term + input_grad[levels:]
    return (tracer_grad, velocity_grad, summed[0] * scale, summed[1] * scale, summed[2] * scale)


def solution(mesh):
    return jax.shard_map(
        on_device,
        mesh=mesh,
        in_specs=(
            P(None, "lat", "lon"),
            P(None, "lat", "lon"),
            P(None, "lat", "lon"),
            P(None, "lat", "lon"),
            P(None, "lat", "lon"),
            P("lat", "lon"),
            P("lat", "lon"),
            P("lat", "lon"),
            P(),
            P(),
            P(),
        ),
        out_specs=(P(None, "lat", "lon"), P(None, "lat", "lon"), P(), P(), P()),
        check_vma=False,
    )
```

profile of v0, /device:TPU:1, one launch (start us, length us, event | category | flops | bytes accessed | tf_op | source)
XLA Modules:
  0.0 154.4 jit_solution(5531603626910962924)
XLA Ops:
  6.0 2.4 %copy.169 = f32[40,6,16,128]{3,0,1,2:T(8,128)} copy(f32[40,6,16,128]{3,2,1,0:T(8,128)S(1)} %bitcast.76) | data formatting | bytes 3932160 | tf_op jit(solution)/shard_map/reshape | solution.py:162
  8.4 6.9 %all-to-all-start = ((f32[16,40,6,128]{3,1,2,0:T(8,128)}), f32[16,40,6,128]{3,1,2,0:T(8,128)S(1)}, u32[]{:S(2)}, u32[]{:S(2)}) async-start(f32[16,40,6,128]{3,1,2,0:T(8,128)} %bitcast.75), calls=%async_computation | async-start | bytes 3932160 | tf_op jit(solution)/shard_map/all_to_all | solution.py:163
  18.2 2.6 %collective-permute-start = (f32[32,1,128]{2,1,0:T(1,128)}, f32[32,1,128]{2,1,0:T(1,128)}, u32[]{:S(2)}, u32[]{:S(2)}) collective-permute-start(f32[32,1,128]{2,1,0:T(1,128)} %get-tuple-element.64), channel_id=1, source_target_pairs={{0,16},{16,32},{32,48},{48,64},{64,80},{80,96},{96,112},{112,0},{1... | collective-permute-start | bytes 49160 | tf_op jit(solution)/shard_map/ppermute | solution.py:19
  20.8 3.5 %collective-permute-start.1 = (f32[32,1,128]{2,1,0:T(1,128)}, f32[32,1,128]{2,1,0:T(1,128)}, u32[]{:S(2)}, u32[]{:S(2)}) collective-permute-start(f32[32,1,128]{2,1,0:T(1,128)} %get-tuple-element.63), channel_id=1, source_target_pairs={{0,112},{16,0},{32,16},{48,32},{64,48},{80,64},{96,80},{112,96},{1... | collective-permute-start | bytes 49160 | tf_op jit(solution)/shard_map/ppermute | solution.py:20
  24.3 4.2 %fusion.78 = (f32[32,96,1]{2,1,0:T(8,128)}, f32[32,96,1]{2,1,0:T(8,128)}) fusion(f32[32,96,128]{2,1,0:T(8,128)} %bitcast_dynamic-update-slice_fusion), kind=kLoop, calls=%fused_computation.110 | loop fusion | bytes 49152 | tf_op jit(solution)/shard_map/slice | solution.py:22
  28.4 2.5 %copy.121 = f32[32,96,1]{1,0,2:T(8,128)} copy(f32[32,96,1]{2,1,0:T(8,128)} %get-tuple-element.62) | data formatting | bytes 24576 | tf_op jit(solution)/shard_map/slice | solution.py:21
  32.3 2.5 %copy.122 = f32[32,96,1]{1,0,2:T(8,128)} copy(f32[32,96,1]{2,1,0:T(8,128)} %get-tuple-element.61) | data formatting | bytes 24576 | tf_op jit(solution)/shard_map/slice | solution.py:22
  47.5 2.7 %convolution_bitcast_fusion.1 = f32[16,96,6,128]{3,1,2,0:T(8,128)S(1)} fusion(f32[20,96,1,1]{1,0,2,3:T(8,128)} %reshape.78, f32[16,40,6,128]{3,1,2,0:T(8,128)S(1)} %all-to-all-done), kind=kOutput, calls=%fused_computation.10 | convolution fusion | flops 141557760 | bytes 5905920 | tf_op jit(solution)/shard_map/oc,soml->scml/dot_general | solution.py:92
  57.0 4.0 %fusion.9 = (f32[16,32,6,128]{3,1,2,0:T(8,128)S(1)}, f32[16,32,6,128]{3,1,2,0:T(8,128)S(1)}) fusion(f32[16,96,6,128]{3,1,2,0:T(8,128)S(1)} %convolution_bitcast_fusion.1, f32[1,32,6,1]{3,1,2,0:T(8,128)S(1)} %get-tuple-element.42, f32[15,32,6,1]{3,1,2,0:T(8,128)S(1)} %get-tuple-element.44, f32[16,32,6,127]{3,1,2,0:T(8,128)S(1)} %get-tuple-element.46, ...), kind=kOutput, calls=%fused_computation.19 | convolution fusion | flops 237109248 | bytes 12595200 | tf_op jit(solution)/shard_map/oc,scml->soml/dot_general | solution.py:80
  62.2 2.3 %fusion.19 = f32[32,96]{1,0:T(8,128)S(1)} fusion(f32[16,32,6,128]{3,1,2,0:T(8,128)S(1)} %get-tuple-element.116, f32[1,32,6,1]{3,1,2,0:T(8,128)S(1)} %get-tuple-element.72, f32[15,32,6,1]{3,1,2,0:T(8,128)S(1)} %get-tuple-element.74, f32[16,32,6,127]{3,1,2,0:T(8,128)S(1)} %get-tuple-element.76, f32[16,32,6,128]{3,1,2,0:T(8,128)S(1)} %tanh_bitcast_fusion.1, ...), kind=kOutput, calls=%fused_computation.28 | convolution fusion | flops 233570304 | bytes 6303744 | tf_op jit(solution)/shard_map/soml,scml->oc/dot_general | solution.py:94
  64.5 2.0 %convolution_bitcast_fusion = f32[16,96,6,128]{3,1,2,0:T(8,128)S(1)} fusion(f32[16,32,6,128]{3,1,2,0:T(8,128)S(1)} %get-tuple-element.116, f32[32,96,1,1]{1,0,2,3:T(8,128)S(1)} %reshape.80), kind=kOutput, calls=%fused_computation.9 | convolution fusion | flops 226492416 | bytes 6303744 | tf_op jit(solution)/shard_map/oc,soml->scml/dot_general | solution.py:95
  66.7 2.6 %fusion.66 = (f32[15,32,6,1]{3,1,2,0:T(8,128)}, f32[15,32,6,1]{3,1,2,0:T(8,128)}) fusion(f32[16,96,6,128]{3,1,2,0:T(8,128)S(1)} %convolution_bitcast_fusion), kind=kLoop, calls=%fused_computation.98 | loop fusion | bytes 46080 | tf_op jit(solution)/shard_map/jit(_roll_static)/slice | solution.py:52
  69.6 2.2 %fusion.67 = (f32[16,32,6,127]{3,1,2,0:T(8,128)}, f32[16,32,6,127]{3,1,2,0:T(8,128)}) fusion(f32[16,96,6,128]{3,1,2,0:T(8,128)S(1)} %convolution_bitcast_fusion), kind=kLoop, calls=%fused_computation.99 | loop fusion | bytes 6242304 | tf_op jit(solution)/shard_map/slice | solution.py:52
  71.8 2.4 %fusion.24 = f32[20,96]{1,0:T(8,128)S(1)} fusion(f32[16,20,6,128]{3,1,2,0:T(8,128)S(1)} %get-tuple-element.53, f32[1,32,6,1]{3,1,2,0:T(8,128)S(1)} %get-tuple-element.66, f32[15,32,6,1]{3,1,2,0:T(8,128)S(1)} %get-tuple-element.68, f32[16,32,6,127]{3,1,2,0:T(8,128)S(1)} %get-tuple-element.70, f32[16,32,6,128]{3,1,2,0:T(8,128)S(1)} %get-tuple-element.117, ...), kind=kOutput, calls=%fused_computation.29 | convolution fusion | flops 148635648 | bytes 5709312 | tf_op jit(solution)/shard_map/soml,scml->oc/dot_general | solution.py:91
  74.5 4.5 %fusion.7 = f32[16,32,6,128]{3,1,2,0:T(8,128)S(1)} fusion(f32[16,96,6,128]{3,1,2,0:T(8,128)} %copy-done, f32[1,32,6,1]{3,1,2,0:T(8,128)S(1)} %get-tuple-element.36, f32[15,32,6,1]{3,1,2,0:T(8,128)} %get-tuple-element.38, f32[16,32,6,127]{3,1,2,0:T(8,128)} %get-tuple-element.40, f32[16,32,6,127]{3,1,2,0:T(8,128)} %get-tuple-element.39, ...), kind=kLoop, calls=%fused_computation.16 | loop fusion | flops 3538944 | bytes 7864320 | tf_op jit(solution)/shard_map/mul | solution.py:96
  82.7 4.7 %convolution_bitcast_fusion.2 = f32[16,60,6,128]{3,1,2,0:T(8,128)} fusion(f32[16,32,6,128]{3,1,2,0:T(8,128)} %copy-done.6, f32[32,60]{0,1:T(8,128)S(1)} %copy-done.35), kind=kOutput, calls=%fused_computation.13 | convolution fusion | flops 141557760 | bytes 4529664 | tf_op jit(solution)/shard_map/oc,soml->scml/dot_general | solution.py:98
  93.1 2.2 %fusion.73 = (f32[16,20,6,127]{3,1,2,0:T(8,128)S(1)}, f32[16,20,6,127]{3,1,2,0:T(8,128)S(1)}) fusion(f32[16,60,6,128]{3,1,2,0:T(8,128)} %convolution_bitcast_fusion.2), kind=kLoop, calls=%fused_computation.105 | loop fusion | bytes 3901440 | tf_op jit(solution)/shard_map/slice | solution.py:52
  95.3 3.0 %collective-permute-start.8 = (f32[54,128]{1,0:T(8,128)S(1)}, f32[54,128]{1,0:T(8,128)S(1)}, u32[]{:S(2)}, u32[]{:S(2)}) collective-permute-start(f32[54,128]{1,0:T(8,128)S(1)} %maximum_bitcast_fusion), channel_id=1, source_target_pairs={{0,1},{1,0},{2,3},{3,2},{4,5},{5,4},{6,7},{7,6},{8,9},{9,8},{10,11... | collective-permute-start | bytes 82952 | tf_op jit(solution)/shard_map/ppermute | solution.py:113
  98.5 3.3 %fusion.44 = (f32[10,96,128]{2,1,0:T(8,128)S(1)}, f32[10,96,128]{2,1,0:T(8,128)S(1)}, f32[10,96,128]{2,1,0:T(8,128)}, f32[10,96,128]{2,1,0:T(8,128)}, f32[10,96,128]{2,1,0:T(8,128)}) fusion(f32[10,96,128]{2,1,0:T(8,128)S(1)} %copy-done.1, f32[10,96,1]{2,1,0:T(8,128)S(1)} %copy-done.22, f32[10,96,127]{2,1,0:T(8,128)S(1)} %copy-done.14, ...), kind=kLoop, calls=%fused_computation.54 | loop fusion | flops 3563520 | bytes 7618560 | tf_op jit(solution)/shard_map/mul | solution.py:183
  102.5 2.6 %collective-permute-done.9 = f32[54,128]{1,0:T(8,128)S(1)} collective-permute-done((f32[54,128]{1,0:T(8,128)S(1)}, f32[54,128]{1,0:T(8,128)S(1)}, u32[]{:S(2)}, u32[]{:S(2)}) %collective-permute-start.9) | collective-permute-done | bytes 27680 | tf_op jit(solution)/shard_map/ppermute | solution.py:113
  113.1 7.5 %all-to-all-start.1 = ((f32[16,20,6,128]{3,1,2,0:T(8,128)}), f32[16,20,6,128]{3,1,2,0:T(8,128)S(1)}, u32[]{:S(2)}, u32[]{:S(2)}) async-start(f32[16,20,6,128]{3,1,2,0:T(8,128)} %fusion.12), calls=%async_computation.1 | async-start | bytes 2359296 | tf_op jit(solution)/shard_map/all_to_all | solution.py:168
  123.7 3.4 %collective-permute-start.14 = (f32[54,128]{1,0:T(8,128)S(1)}, f32[54,128]{1,0:T(8,128)S(1)}, u32[]{:S(2)}, u32[]{:S(2)}) collective-permute-start(f32[54,128]{1,0:T(8,128)S(1)} %add.106), channel_id=1, source_target_pairs={{0,64},{16,80},{32,96},{48,112},{64,0},{80,16},{96,32},{112,48},{1... | collective-permute-start | bytes 82952 | tf_op jit(solution)/shard_map/ppermute | solution.py:113
  141.7 6.7 %collective-permute-done.4 = f32[10,96,1]{2,1,0:T(8,128)} collective-permute-done((f32[10,96,1]{2,1,0:T(8,128)}, f32[10,96,1]{2,1,0:T(8,128)}, u32[]{:S(2)}, u32[]{:S(2)}) %collective-permute-start.4) | collective-permute-done | bytes 3872 | tf_op jit(solution)/shard_map/ppermute | solution.py:22
  151.8 2.6 %fusion.53 = f32[10,96,128]{2,1,0:T(8,128)} fusion(f32[10,96,128]{2,1,0:T(8,128)S(1)} %copy-done.1, f32[10,96,128]{2,1,0:T(8,128)S(1)} %copy-done.11, f32[10,96,128]{2,1,0:T(8,128)S(1)} %get-tuple-element.30, f32[10,96,1]{2,1,0:T(8,128)} %collective-permute-done.4, f32[10,96,127]{2,1,0:T(8,128)S(1)} %copy-done.28, f32[10,96,128]{2,1,0:T(8,128)S(1)} %copy-done.10, ...), kind=kLoop, calls=%fused_computation.67 | loop fusion | flops 2088960 | bytes 5898240 | tf_op jit(solution)/shard_map/add | solution.py:187
  (183 shorter events, 69.5 us)
Async XLA Ops:
  8.4 7.0 %copy-start.34 = (f32[96,128]{1,0:T(8,128)S(1)}, f32[96,128]{1,0:T(8,128)}, u32[]{:S(2)}) copy-start(f32[96,128]{1,0:T(8,128)} %param.16) | copy-start | bytes 147460
  8.4 7.6 %copy-start.33 = (f32[96,128]{1,0:T(8,128)S(1)}, f32[96,128]{1,0:T(8,128)}, u32[]{:S(2)}) copy-start(f32[96,128]{1,0:T(8,128)} %param.17) | copy-start | bytes 147460
  8.4 39.2 %all-to-all-start = ((f32[16,40,6,128]{3,1,2,0:T(8,128)}), f32[16,40,6,128]{3,1,2,0:T(8,128)S(1)}, u32[]{:S(2)}, u32[]{:S(2)}) async-start(f32[16,40,6,128]{3,1,2,0:T(8,128)} %bitcast.75), calls=%async_computation | async-start | bytes 3932160 | tf_op jit(solution)/shard_map/all_to_all | solution.py:163
  18.2 63.8 %collective-permute-start = (f32[32,1,128]{2,1,0:T(1,128)}, f32[32,1,128]{2,1,0:T(1,128)}, u32[]{:S(2)}, u32[]{:S(2)}) collective-permute-start(f32[32,1,128]{2,1,0:T(1,128)} %get-tuple-element.64), channel_id=1, source_target_pairs={{0,16},{16,32},{32,48},{48,64},{64,80},{80,96},{96,112},{112,0},{1... | collective-permute-start | bytes 49160 | tf_op jit(solution)/shard_map/ppermute | solution.py:19
  20.8 61.2 %collective-permute-start.1 = (f32[32,1,128]{2,1,0:T(1,128)}, f32[32,1,128]{2,1,0:T(1,128)}, u32[]{:S(2)}, u32[]{:S(2)}) collective-permute-start(f32[32,1,128]{2,1,0:T(1,128)} %get-tuple-element.63), channel_id=1, source_target_pairs={{0,112},{16,0},{32,16},{48,32},{64,48},{80,64},{96,80},{112,96},{1... | collective-permute-start | bytes 49160 | tf_op jit(solution)/shard_map/ppermute | solution.py:20
  31.0 51.0 %collective-permute-start.2 = (f32[32,96,1]{1,0,2:T(8,128)}, f32[32,96,1]{1,0,2:T(8,128)}, u32[]{:S(2)}, u32[]{:S(2)}) collective-permute-start(f32[32,96,1]{1,0,2:T(8,128)} %copy.121), channel_id=1, source_target_pairs={{0,1},{1,2},{2,3},{3,4},{4,5},{5,6},{6,7},{7,8},{8,9},{9,10},{10,1... | collective-permute-start | bytes 36872 | tf_op jit(solution)/shard_map/ppermute | solution.py:21
  34.8 47.2 %collective-permute-start.3 = (f32[32,96,1]{1,0,2:T(8,128)}, f32[32,96,1]{1,0,2:T(8,128)}, u32[]{:S(2)}, u32[]{:S(2)}) collective-permute-start(f32[32,96,1]{1,0,2:T(8,128)} %copy.122), channel_id=1, source_target_pairs={{0,15},{1,0},{2,1},{3,2},{4,3},{5,4},{6,5},{7,6},{8,7},{9,8},{10,9... | collective-permute-start | bytes 36872 | tf_op jit(solution)/shard_map/ppermute | solution.py:22
  74.5 5.7 %copy-start.3 = (f32[16,60,6,128]{3,1,2,0:T(8,128)S(1)}, f32[16,60,6,128]{3,1,2,0:T(8,128)}, u32[]{:S(2)}) copy-start(f32[16,60,6,128]{3,1,2,0:T(8,128)} %copy-done.2) | copy-start | bytes 8847364
  95.3 6.9 %collective-permute-start.8 = (f32[54,128]{1,0:T(8,128)S(1)}, f32[54,128]{1,0:T(8,128)S(1)}, u32[]{:S(2)}, u32[]{:S(2)}) collective-permute-start(f32[54,128]{1,0:T(8,128)S(1)} %maximum_bitcast_fusion), channel_id=1, source_target_pairs={{0,1},{1,0},{2,3},{3,2},{4,5},{5,4},{6,7},{7,6},{8,9},{9,8},{10,11... | collective-permute-start | bytes 82952 | tf_op jit(solution)/shard_map/ppermute | solution.py:113
  102.3 2.8 %collective-permute-start.9 = (f32[54,128]{1,0:T(8,128)S(1)}, f32[54,128]{1,0:T(8,128)S(1)}, u32[]{:S(2)}, u32[]{:S(2)}) collective-permute-start(f32[54,128]{1,0:T(8,128)S(1)} %add.101), channel_id=1, source_target_pairs={{0,2},{1,3},{2,0},{3,1},{4,6},{5,7},{6,4},{7,5},{8,10},{9,11},{10,... | collective-permute-start | bytes 82952 | tf_op jit(solution)/shard_map/ppermute | solution.py:113
  105.1 2.7 %collective-permute-start.10 = (f32[54,128]{1,0:T(8,128)S(1)}, f32[54,128]{1,0:T(8,128)S(1)}, u32[]{:S(2)}, u32[]{:S(2)}) collective-permute-start(f32[54,128]{1,0:T(8,128)S(1)} %add.102), channel_id=1, source_target_pairs={{0,4},{1,5},{2,6},{3,7},{4,0},{5,1},{6,2},{7,3},{8,12},{9,13},{10,... | collective-permute-start | bytes 82952 | tf_op jit(solution)/shard_map/ppermute | solution.py:113
  107.8 4.2 %collective-permute-start.11 = (f32[54,128]{1,0:T(8,128)S(1)}, f32[54,128]{1,0:T(8,128)S(1)}, u32[]{:S(2)}, u32[]{:S(2)}) collective-permute-start(f32[54,128]{1,0:T(8,128)S(1)} %add.103), channel_id=1, source_target_pairs={{0,8},{1,9},{2,10},{3,11},{4,12},{5,13},{6,14},{7,15},{8,0},{9,1},... | collective-permute-start | bytes 82952 | tf_op jit(solution)/shard_map/ppermute | solution.py:113
  112.0 8.7 %collective-permute-start.12 = (f32[54,128]{1,0:T(8,128)S(1)}, f32[54,128]{1,0:T(8,128)S(1)}, u32[]{:S(2)}, u32[]{:S(2)}) collective-permute-start(f32[54,128]{1,0:T(8,128)S(1)} %add.104), channel_id=1, source_target_pairs={{0,16},{16,0},{32,48},{48,32},{64,80},{80,64},{96,112},{112,96},{1... | collective-permute-start | bytes 82952 | tf_op jit(solution)/shard_map/ppermute | solution.py:113
  113.1 24.6 %all-to-all-start.1 = ((f32[16,20,6,128]{3,1,2,0:T(8,128)}), f32[16,20,6,128]{3,1,2,0:T(8,128)S(1)}, u32[]{:S(2)}, u32[]{:S(2)}) async-start(f32[16,20,6,128]{3,1,2,0:T(8,128)} %fusion.12), calls=%async_computation.1 | async-start | bytes 2359296 | tf_op jit(solution)/shard_map/all_to_all | solution.py:168
  120.7 3.0 %collective-permute-start.13 = (f32[54,128]{1,0:T(8,128)S(1)}, f32[54,128]{1,0:T(8,128)S(1)}, u32[]{:S(2)}, u32[]{:S(2)}) collective-permute-start(f32[54,128]{1,0:T(8,128)S(1)} %add.105), channel_id=1, source_target_pairs={{0,32},{16,48},{32,0},{48,16},{64,96},{80,112},{96,64},{112,80},{1... | collective-permute-start | bytes 82952 | tf_op jit(solution)/shard_map/ppermute | solution.py:113
  123.7 11.5 %collective-permute-start.14 = (f32[54,128]{1,0:T(8,128)S(1)}, f32[54,128]{1,0:T(8,128)S(1)}, u32[]{:S(2)}, u32[]{:S(2)}) collective-permute-start(f32[54,128]{1,0:T(8,128)S(1)} %add.106), channel_id=1, source_target_pairs={{0,64},{16,80},{32,96},{48,112},{64,0},{80,16},{96,32},{112,48},{1... | collective-permute-start | bytes 82952 | tf_op jit(solution)/shard_map/ppermute | solution.py:113
  129.2 19.2 %collective-permute-start.4 = (f32[10,96,1]{2,1,0:T(8,128)}, f32[10,96,1]{2,1,0:T(8,128)}, u32[]{:S(2)}, u32[]{:S(2)}) collective-permute-start(f32[10,96,1]{2,1,0:T(8,128)} %get-tuple-element.84), channel_id=1, source_target_pairs={{0,15},{1,0},{2,1},{3,2},{4,3},{5,4},{6,5},{7,6},{8,7},{9,8},{10,9... | collective-permute-start | bytes 11528 | tf_op jit(solution)/shard_map/ppermute | solution.py:22
  130.8 17.6 %collective-permute-start.5 = (f32[10,96,1]{2,1,0:T(8,128)}, f32[10,96,1]{2,1,0:T(8,128)}, u32[]{:S(2)}, u32[]{:S(2)}) collective-permute-start(f32[10,96,1]{2,1,0:T(8,128)} %get-tuple-element.83), channel_id=1, source_target_pairs={{0,1},{1,2},{2,3},{3,4},{4,5},{5,6},{6,7},{7,8},{8,9},{9,10},{10,1... | collective-permute-start | bytes 11528 | tf_op jit(solution)/shard_map/ppermute | solution.py:21
  132.2 18.2 %collective-permute-start.6 = (f32[10,1,128]{2,1,0:T(1,128)S(1)}, f32[10,1,128]{2,1,0:T(1,128)S(1)}, u32[]{:S(2)}, u32[]{:S(2)}) collective-permute-start(f32[10,1,128]{2,1,0:T(1,128)S(1)} %get-tuple-element.80), channel_id=1, source_target_pairs={{0,112},{16,0},{32,16},{48,32},{64,48},{80,64},{96,80},{112,96},{1... | collective-permute-start | bytes 15368 | tf_op jit(solution)/shard_map/ppermute | solution.py:20
  134.2 17.5 %collective-permute-start.7 = (f32[10,1,128]{2,1,0:T(1,128)S(1)}, f32[10,1,128]{2,1,0:T(1,128)S(1)}, u32[]{:S(2)}, u32[]{:S(2)}) collective-permute-start(f32[10,1,128]{2,1,0:T(1,128)S(1)} %get-tuple-element.79), channel_id=1, source_target_pairs={{0,16},{16,32},{32,48},{48,64},{64,80},{80,96},{96,112},{112,0},{1... | collective-permute-start | bytes 15368 | tf_op jit(solution)/shard_map/ppermute | solution.py:19
  140.0 11.8 %copy-start.29 = (f32[10,95,128]{2,1,0:T(8,128)S(1)}, f32[10,95,128]{2,1,0:T(8,128)}, u32[]{:S(2)}) copy-start(f32[10,95,128]{2,1,0:T(8,128)} %get-tuple-element.81) | copy-start | bytes 1459204
  140.0 11.8 %copy-start.30 = (f32[10,95,128]{2,1,0:T(8,128)S(1)}, f32[10,95,128]{2,1,0:T(8,128)}, u32[]{:S(2)}) copy-start(f32[10,95,128]{2,1,0:T(8,128)} %get-tuple-element.82) | copy-start | bytes 1459204
  141.4 10.4 %copy-start.27 = (f32[10,96,127]{2,1,0:T(8,128)S(1)}, f32[10,96,127]{2,1,0:T(8,128)}, u32[]{:S(2)}) copy-start(f32[10,96,127]{2,1,0:T(8,128)} %get-tuple-element.85) | copy-start | bytes 1463044
  141.4 10.4 %copy-start.28 = (f32[10,96,127]{2,1,0:T(8,128)S(1)}, f32[10,96,127]{2,1,0:T(8,128)}, u32[]{:S(2)}) copy-start(f32[10,96,127]{2,1,0:T(8,128)} %get-tuple-element.86) | copy-start | bytes 1463044
  (30 other events, 98.3 us)
where the time goes:
time: 155 us; the launch traced here: 154 us
  local copies, waits for them, and re-layouts  60.6 us (39%)
  starting transfers between devices  38.6 us (25%)
  matrix products  20.9 us (13%)
  other arithmetic  18.1 us (12%)
  waiting for transfers between devices  15 us (10%)
    ppermute x7, starting transfers between devices, butterfly_sum(): values = values + lax.ppermute(values, axis, pairs)  10.7 us
    unnamed x78, local copies, waits for them, and re-layouts  9.4 us
    all_to_all x1, starting transfers between devices, on_device(): lax.all_to_all(band_grad, 'lon', split_axis=0, concat_axis=0, tiled=True)  7.55 us
    all_to_all x1, starting transfers between devices, on_device(): lax.all_to_all(chunks.transpose(2, 0, 1, 3), 'lon', split_axis=0, concat_...  6.95 us
    slice x9, local copies, waits for them, and re-layouts, part(): return tuple((piece[lo:hi] for piece in (below, above, left, right)))  6.86 us
    ppermute x2, waiting for transfers between devices, edges(): right = lax.ppermute(block[..., :, :1], 'lon', ring('lon', -1))  6.69 us
    slice x2, local copies, waits for them, and re-layouts, edges(): right = lax.ppermute(block[..., :, :1], 'lon', ring('lon', -1))  6.69 us
    slice x6, local copies, waits for them, and re-layouts, lon_roll(): values[..., :-1]  6.5 us
  transfers between devices with their start and end apart: 17, of which 8 were waited for; matrix products, arithmetic and copies ran while one was open for 47% of the time, Pallas kernels for 0%

commit v1 on v0

--- a/solution.py
+++ b/solution.py
@@ -104,15 +104,17 @@
 LANES = 128
 
 
-def butterfly_sum(values, axes):
-    for axis in axes:
+def butterfly_sum(values, axes, tie=None):
+    for index, axis in enumerate(axes):
+        if index == 1 and tie is not None:
+            values, tie = lax.optimization_barrier((values, tie))
         size = lax.axis_size(axis)
         stride = 1
         while stride < size:
             pairs = [(i, i ^ stride) for i in range(size)]
             values = values + lax.ppermute(values, axis, pairs)
             stride *= 2
-    return values
+    return values, tie
 
 
 def pack(parts):
@@ -164,7 +166,6 @@
     weight_grads, band_grad = network_vjp(weights, band[:, : 2 * levels], band[:, 2 * levels :])
     packed = pack(weight_grads)
     packed, plane_halo = lax.optimization_barrier((packed, plane_halo))
-    summed = unpack(butterfly_sum(packed, ("lon", "lat")), weight_grads)
     returned = lax.all_to_all(band_grad, "lon", split_axis=0, concat_axis=0, tiled=True)
     input_grad = returned.transpose(1, 2, 0, 3).reshape(2 * levels, tile_rows, tile_cols)
     below, above, left, right = plane_halo
@@ -181,7 +182,9 @@
     tracer_term = laplace(tracer_adjoint, part(0, levels), sea_cells, sea_near, *faces)
     first_laplace = laplace(velocity_adjoint, part(levels, 2 * levels), sea_cells, sea_near, *faces)
     scaled = viscosity * first_laplace
-    viscous_term = laplace(scaled, edges(scaled), sea_cells, sea_near, *faces)
+    total, scaled_halo = butterfly_sum(packed, ("lon", "lat"), edges(scaled))
+    summed = unpack(total, weight_grads)
+    viscous_term = laplace(scaled, scaled_halo, sea_cells, sea_near, *faces)
     scale = 1.0 / math.sqrt(tile_rows * lax.axis_size("lat") * tile_cols * lax.axis_size("lon"))
     tracer_grad = tracer_adjoint + tracer_term + input_grad[:levels]
     velocity_grad = velocity_adjoint - viscous_term + input_grad[levels:]

time: 155 us -> 157 us (1.013)
  waiting for transfers between devices: 15 us -> 22.7 us
  starting transfers between devices: 38.6 us -> 33.7 us
    all_to_all x1, waiting for transfers between devices: 0.33 us -> 7.4 us  [on_device(): lax.all_to_all(band_grad, 'lon', split_axis=0, concat_axis=0, tiled=True)]
    ppermute x2, waiting for transfers between devices: 0.01 us -> 6.38 us  [edges(): left = lax.ppermute(block[..., :, -1:], 'lon', ring('lon', 1))]
    ppermute x2, waiting for transfers between devices: 6.69 us -> 2.73 us  [edges(): right = lax.ppermute(block[..., :, :1], 'lon', ring('lon', -1))]
    ppermute x7, starting transfers between devices: 10.7 us -> 7.35 us  [butterfly_sum(): values = values + lax.ppermute(values, axis, pairs)]
    all_to_all x1, starting transfers between devices: 7.55 us -> 4.37 us  [on_device(): lax.all_to_all(band_grad, 'lon', split_axis=0, concat_axis=0, tiled=True)]
    ppermute x2, starting transfers between devices: 5.48 us -> 8.54 us  [edges(): above = lax.ppermute(block[..., :1, :], 'lat', ring('lat', -1))]
    ppermute x2, waiting for transfers between devices: 2.01 us -> 0.01 us  [edges(): above = lax.ppermute(block[..., :1, :], 'lat', ring('lat', -1))]
    ppermute x7, waiting for transfers between devices: 4.58 us -> 6.15 us  [butterfly_sum(): values = values + lax.ppermute(values, axis, pairs)]
  transfers between devices with their start and end apart: 17 -> 17, of which waited for: 8 -> 7; matrix products, arithmetic and copies ran while one was open for 47% -> 44% of each run, Pallas kernels for 0% -> 0%
where the time goes in v1:
time: 157 us; the launch traced here: 156 us
  local copies, waits for them, and re-layouts  60 us (38%)
  starting transfers between devices  33.7 us (21%)
  waiting for transfers between devices  22.7 us (14%)
  matrix products  20.9 us (13%)
  other arithmetic  17 us (11%)
    unnamed x86, local copies, waits for them, and re-layouts  9.58 us
    ppermute x2, starting transfers between devices, edges(): above = lax.ppermute(block[..., :1, :], 'lat', ring('lat', -1))  8.54 us
    all_to_all x1, waiting for transfers between devices, on_device(): lax.all_to_all(band_grad, 'lon', split_axis=0, concat_axis=0, tiled=True)  7.4 us
    ppermute x7, starting transfers between devices, butterfly_sum(): values = values + lax.ppermute(values, axis, pairs)  7.35 us
    all_to_all x1, starting transfers between devices, on_device(): lax.all_to_all(chunks.transpose(2, 0, 1, 3), 'lon', split_axis=0, concat_...  6.95 us
    slice x9, local copies, waits for them, and re-layouts, part(): return tuple((piece[lo:hi] for piece in (below, above, left, right)))  6.89 us
    slice x3, local copies, waits for them, and re-layouts, edges(): right = lax.ppermute(block[..., :, :1], 'lon', ring('lon', -1))  6.88 us
    slice x6, local copies, waits for them, and re-layouts, lon_roll(): values[..., :-1]  6.52 us
  transfers between devices with their start and end apart: 17, of which 7 were waited for; matrix products, arithmetic and copies ran while one was open for 44% of the time, Pallas kernels for 0%

profile of v1, /device:TPU:1, one launch (start us, length us, event | category | flops | bytes accessed | tf_op | source)
XLA Modules:
  0.0 155.6 jit_solution(1690989796440526249)
XLA Ops:
  6.0 2.4 %copy.169 = f32[40,6,16,128]{3,0,1,2:T(8,128)} copy(f32[40,6,16,128]{3,2,1,0:T(8,128)S(1)} %bitcast.76) | data formatting | bytes 3932160 | tf_op jit(solution)/shard_map/reshape | solution.py:164
  8.4 6.9 %all-to-all-start = ((f32[16,40,6,128]{3,1,2,0:T(8,128)}), f32[16,40,6,128]{3,1,2,0:T(8,128)S(1)}, u32[]{:S(2)}, u32[]{:S(2)}) async-start(f32[16,40,6,128]{3,1,2,0:T(8,128)} %bitcast.75), calls=%async_computation | async-start | bytes 3932160 | tf_op jit(solution)/shard_map/all_to_all | solution.py:165
  18.2 2.6 %collective-permute-start = (f32[32,1,128]{2,1,0:T(1,128)}, f32[32,1,128]{2,1,0:T(1,128)}, u32[]{:S(2)}, u32[]{:S(2)}) collective-permute-start(f32[32,1,128]{2,1,0:T(1,128)} %get-tuple-element.74), channel_id=1, source_target_pairs={{0,16},{16,32},{32,48},{48,64},{64,80},{80,96},{96,112},{112,0},{1... | collective-permute-start | bytes 49160 | tf_op jit(solution)/shard_map/ppermute | solution.py:19
  20.8 3.5 %collective-permute-start.1 = (f32[32,1,128]{2,1,0:T(1,128)}, f32[32,1,128]{2,1,0:T(1,128)}, u32[]{:S(2)}, u32[]{:S(2)}) collective-permute-start(f32[32,1,128]{2,1,0:T(1,128)} %get-tuple-element.73), channel_id=1, source_target_pairs={{0,112},{16,0},{32,16},{48,32},{64,48},{80,64},{96,80},{112,96},{1... | collective-permute-start | bytes 49160 | tf_op jit(solution)/shard_map/ppermute | solution.py:20
  24.3 4.2 %fusion.78 = (f32[32,96,1]{2,1,0:T(8,128)}, f32[32,96,1]{2,1,0:T(8,128)}) fusion(f32[32,96,128]{2,1,0:T(8,128)} %bitcast_dynamic-update-slice_fusion), kind=kLoop, calls=%fused_computation.110 | loop fusion | bytes 49152 | tf_op jit(solution)/shard_map/slice | solution.py:22
  28.5 2.5 %copy.121 = f32[32,96,1]{1,0,2:T(8,128)} copy(f32[32,96,1]{2,1,0:T(8,128)} %get-tuple-element.72) | data formatting | bytes 24576 | tf_op jit(solution)/shard_map/slice | solution.py:21
  32.3 2.5 %copy.122 = f32[32,96,1]{1,0,2:T(8,128)} copy(f32[32,96,1]{2,1,0:T(8,128)} %get-tuple-element.71) | data formatting | bytes 24576 | tf_op jit(solution)/shard_map/slice | solution.py:22
  47.6 2.7 %convolution_bitcast_fusion.1 = f32[16,96,6,128]{3,1,2,0:T(8,128)S(1)} fusion(f32[20,96,1,1]{1,0,2,3:T(8,128)} %reshape.78, f32[16,40,6,128]{3,1,2,0:T(8,128)S(1)} %all-to-all-done), kind=kOutput, calls=%fused_computation.10 | convolution fusion | flops 141557760 | bytes 5905920 | tf_op jit(solution)/shard_map/oc,soml->scml/dot_general | solution.py:92
  57.0 4.0 %fusion.9 = (f32[16,32,6,128]{3,1,2,0:T(8,128)S(1)}, f32[16,32,6,128]{3,1,2,0:T(8,128)S(1)}) fusion(f32[16,96,6,128]{3,1,2,0:T(8,128)S(1)} %convolution_bitcast_fusion.1, f32[1,32,6,1]{3,1,2,0:T(8,128)S(1)} %get-tuple-element.52, f32[15,32,6,1]{3,1,2,0:T(8,128)S(1)} %get-tuple-element.54, f32[16,32,6,127]{3,1,2,0:T(8,128)S(1)} %get-tuple-element.56, ...), kind=kOutput, calls=%fused_computation.19 | convolution fusion | flops 237109248 | bytes 12595200 | tf_op jit(solution)/shard_map/oc,scml->soml/dot_general | solution.py:80
  62.2 2.3 %fusion.19 = f32[32,96]{1,0:T(8,128)S(1)} fusion(f32[16,32,6,128]{3,1,2,0:T(8,128)S(1)} %get-tuple-element.126, f32[1,32,6,1]{3,1,2,0:T(8,128)S(1)} %get-tuple-element.82, f32[15,32,6,1]{3,1,2,0:T(8,128)S(1)} %get-tuple-element.84, f32[16,32,6,127]{3,1,2,0:T(8,128)S(1)} %get-tuple-element.86, f32[16,32,6,128]{3,1,2,0:T(8,128)S(1)} %tanh_bitcast_fusion.1, ...), kind=kOutput, calls=%fused_computation.28 | convolution fusion | flops 233570304 | bytes 6303744 | tf_op jit(solution)/shard_map/soml,scml->oc/dot_general | solution.py:94
  66.7 2.6 %fusion.66 = (f32[15,32,6,1]{3,1,2,0:T(8,128)}, f32[15,32,6,1]{3,1,2,0:T(8,128)}) fusion(f32[16,96,6,128]{3,1,2,0:T(8,128)S(1)} %convolution_bitcast_fusion), kind=kLoop, calls=%fused_computation.98 | loop fusion | bytes 46080 | tf_op jit(solution)/shard_map/jit(_roll_static)/slice | solution.py:52
  69.6 2.2 %fusion.67 = (f32[16,32,6,127]{3,1,2,0:T(8,128)}, f32[16,32,6,127]{3,1,2,0:T(8,128)}) fusion(f32[16,96,6,128]{3,1,2,0:T(8,128)S(1)} %convolution_bitcast_fusion), kind=kLoop, calls=%fused_computation.99 | loop fusion | bytes 6242304 | tf_op jit(solution)/shard_map/slice | solution.py:52
  71.9 2.4 %fusion.24 = f32[20,96]{1,0:T(8,128)S(1)} fusion(f32[16,20,6,128]{3,1,2,0:T(8,128)S(1)} %get-tuple-element.63, f32[1,32,6,1]{3,1,2,0:T(8,128)S(1)} %get-tuple-element.76, f32[15,32,6,1]{3,1,2,0:T(8,128)S(1)} %get-tuple-element.78, f32[16,32,6,127]{3,1,2,0:T(8,128)S(1)} %get-tuple-element.80, f32[16,32,6,128]{3,1,2,0:T(8,128)S(1)} %get-tuple-element.127, ...), kind=kOutput, calls=%fused_computation.29 | convolution fusion | flops 148635648 | bytes 5709312 | tf_op jit(solution)/shard_map/soml,scml->oc/dot_general | solution.py:91
  74.6 4.5 %fusion.7 = f32[16,32,6,128]{3,1,2,0:T(8,128)S(1)} fusion(f32[16,96,6,128]{3,1,2,0:T(8,128)} %copy-done, f32[1,32,6,1]{3,1,2,0:T(8,128)S(1)} %get-tuple-element.46, f32[15,32,6,1]{3,1,2,0:T(8,128)} %get-tuple-element.48, f32[16,32,6,127]{3,1,2,0:T(8,128)} %get-tuple-element.50, f32[16,32,6,127]{3,1,2,0:T(8,128)} %get-tuple-element.49, ...), kind=kLoop, calls=%fused_computation.16 | loop fusion | flops 3538944 | bytes 7864320 | tf_op jit(solution)/shard_map/mul | solution.py:96
  82.8 4.7 %convolution_bitcast_fusion.2 = f32[16,60,6,128]{3,1,2,0:T(8,128)} fusion(f32[16,32,6,128]{3,1,2,0:T(8,128)} %copy-done.6, f32[32,60]{0,1:T(8,128)S(1)} %copy-done.39), kind=kOutput, calls=%fused_computation.13 | convolution fusion | flops 141557760 | bytes 4529664 | tf_op jit(solution)/shard_map/oc,soml->scml/dot_general | solution.py:98
  95.4 3.0 %collective-permute-start.4 = (f32[54,128]{1,0:T(8,128)S(1)}, f32[54,128]{1,0:T(8,128)S(1)}, u32[]{:S(2)}, u32[]{:S(2)}) collective-permute-start(f32[54,128]{1,0:T(8,128)S(1)} %maximum_bitcast_fusion), channel_id=1, source_target_pairs={{0,1},{1,0},{2,3},{3,2},{4,5},{5,4},{6,7},{7,6},{8,9},{9,8},{10,11... | collective-permute-start | bytes 82952 | tf_op jit(solution)/shard_map/ppermute | solution.py:115
  98.6 3.3 %fusion.44 = (f32[10,96,128]{2,1,0:T(8,128)S(1)}, f32[10,96,128]{2,1,0:T(8,128)S(1)}, f32[10,96,128]{2,1,0:T(8,128)}, f32[10,96,128]{2,1,0:T(8,128)}, f32[10,96,128]{2,1,0:T(8,128)}) fusion(f32[10,96,128]{2,1,0:T(8,128)S(1)} %copy-done.1, f32[10,96,1]{2,1,0:T(8,128)S(1)} %copy-done.22, f32[10,96,127]{2,1,0:T(8,128)S(1)} %copy-done.14, ...), kind=kLoop, calls=%fused_computation.54 | loop fusion | flops 3563520 | bytes 7618560 | tf_op jit(solution)/shard_map/mul | solution.py:184
  102.6 2.5 %collective-permute-done.5 = f32[54,128]{1,0:T(8,128)S(1)} collective-permute-done((f32[54,128]{1,0:T(8,128)S(1)}, f32[54,128]{1,0:T(8,128)S(1)}, u32[]{:S(2)}, u32[]{:S(2)}) %collective-permute-start.5) | collective-permute-done | bytes 27680 | tf_op jit(solution)/shard_map/ppermute | solution.py:115
  105.7 5.1 %collective-permute-start.9 = (f32[10,1,128]{2,1,0:T(1,128)S(1)}, f32[10,1,128]{2,1,0:T(1,128)S(1)}, u32[]{:S(2)}, u32[]{:S(2)}) collective-permute-start(f32[10,1,128]{2,1,0:T(1,128)S(1)} %get-tuple-element.95), channel_id=1, source_target_pairs={{0,112},{16,0},{32,16},{48,32},{64,48},{80,64},{96,80},{112,96},{1... | collective-permute-start | bytes 15368 | tf_op jit(solution)/shard_map/ppermute | solution.py:20
  113.3 2.5 %collective-permute-start.7 = (f32[54,128]{1,0:T(8,128)S(1)}, f32[54,128]{1,0:T(8,128)S(1)}, u32[]{:S(2)}, u32[]{:S(2)}) collective-permute-start(f32[54,128]{1,0:T(8,128)S(1)} %add.99), channel_id=1, source_target_pairs={{0,8},{1,9},{2,10},{3,11},{4,12},{5,13},{6,14},{7,15},{8,0},{9,1},... | collective-permute-start | bytes 82952 | tf_op jit(solution)/shard_map/ppermute | solution.py:115
  117.6 6.4 %collective-permute-done.10 = f32[10,96,1]{2,1,0:T(8,128)S(1)} collective-permute-done((f32[10,96,1]{2,1,0:T(8,128)S(1)}, f32[10,96,1]{2,1,0:T(8,128)S(1)}, u32[]{:S(2)}, u32[]{:S(2)}) %collective-permute-start.10) | collective-permute-done | bytes 3872 | tf_op jit(solution)/shard_map/ppermute | solution.py:21
  124.0 2.7 %collective-permute-done.11 = f32[10,96,1]{2,1,0:T(8,128)S(1)} collective-permute-done((f32[10,96,1]{2,1,0:T(8,128)S(1)}, f32[10,96,1]{2,1,0:T(8,128)S(1)}, u32[]{:S(2)}, u32[]{:S(2)}) %collective-permute-start.11) | collective-permute-done | bytes 3872 | tf_op jit(solution)/shard_map/ppermute | solution.py:22
  128.6 4.4 %all-to-all-start.1 = ((f32[16,20,6,128]{3,1,2,0:T(8,128)}), f32[16,20,6,128]{3,1,2,0:T(8,128)S(1)}, u32[]{:S(2)}, u32[]{:S(2)}) async-start(f32[16,20,6,128]{3,1,2,0:T(8,128)} %fusion.12), calls=%async_computation.1 | async-start | bytes 2359296 | tf_op jit(solution)/shard_map/all_to_all | solution.py:169
  142.5 7.4 %all-to-all-done.1 = f32[16,20,6,128]{3,1,2,0:T(8,128)S(1)} async-done(((f32[16,20,6,128]{3,1,2,0:T(8,128)}), f32[16,20,6,128]{3,1,2,0:T(8,128)S(1)}, u32[]{:S(2)}, u32[]{:S(2)}) %all-to-all-start.1) | async-done | bytes 983072 | tf_op jit(solution)/shard_map/all_to_all | solution.py:169
  (191 shorter events, 66.9 us)
Async XLA Ops:
  8.4 7.0 %copy-start.38 = (f32[96,128]{1,0:T(8,128)S(1)}, f32[96,128]{1,0:T(8,128)}, u32[]{:S(2)}) copy-start(f32[96,128]{1,0:T(8,128)} %param.16) | copy-start | bytes 147460
  8.4 7.6 %copy-start.37 = (f32[96,128]{1,0:T(8,128)S(1)}, f32[96,128]{1,0:T(8,128)}, u32[]{:S(2)}) copy-start(f32[96,128]{1,0:T(8,128)} %param.17) | copy-start | bytes 147460
  8.4 39.2 %all-to-all-start = ((f32[16,40,6,128]{3,1,2,0:T(8,128)}), f32[16,40,6,128]{3,1,2,0:T(8,128)S(1)}, u32[]{:S(2)}, u32[]{:S(2)}) async-start(f32[16,40,6,128]{3,1,2,0:T(8,128)} %bitcast.75), calls=%async_computation | async-start | bytes 3932160 | tf_op jit(solution)/shard_map/all_to_all | solution.py:165
  18.2 63.8 %collective-permute-start = (f32[32,1,128]{2,1,0:T(1,128)}, f32[32,1,128]{2,1,0:T(1,128)}, u32[]{:S(2)}, u32[]{:S(2)}) collective-permute-start(f32[32,1,128]{2,1,0:T(1,128)} %get-tuple-element.74), channel_id=1, source_target_pairs={{0,16},{16,32},{32,48},{48,64},{64,80},{80,96},{96,112},{112,0},{1... | collective-permute-start | bytes 49160 | tf_op jit(solution)/shard_map/ppermute | solution.py:19
  20.8 61.2 %collective-permute-start.1 = (f32[32,1,128]{2,1,0:T(1,128)}, f32[32,1,128]{2,1,0:T(1,128)}, u32[]{:S(2)}, u32[]{:S(2)}) collective-permute-start(f32[32,1,128]{2,1,0:T(1,128)} %get-tuple-element.73), channel_id=1, source_target_pairs={{0,112},{16,0},{32,16},{48,32},{64,48},{80,64},{96,80},{112,96},{1... | collective-permute-start | bytes 49160 | tf_op jit(solution)/shard_map/ppermute | solution.py:20
  31.0 51.0 %collective-permute-start.2 = (f32[32,96,1]{1,0,2:T(8,128)}, f32[32,96,1]{1,0,2:T(8,128)}, u32[]{:S(2)}, u32[]{:S(2)}) collective-permute-start(f32[32,96,1]{1,0,2:T(8,128)} %copy.121), channel_id=1, source_target_pairs={{0,1},{1,2},{2,3},{3,4},{4,5},{5,6},{6,7},{7,8},{8,9},{9,10},{10,1... | collective-permute-start | bytes 36872 | tf_op jit(solution)/shard_map/ppermute | solution.py:21
  34.8 47.2 %collective-permute-start.3 = (f32[32,96,1]{1,0,2:T(8,128)}, f32[32,96,1]{1,0,2:T(8,128)}, u32[]{:S(2)}, u32[]{:S(2)}) collective-permute-start(f32[32,96,1]{1,0,2:T(8,128)} %copy.122), channel_id=1, source_target_pairs={{0,15},{1,0},{2,1},{3,2},{4,3},{5,4},{6,5},{7,6},{8,7},{9,8},{10,9... | collective-permute-start | bytes 36872 | tf_op jit(solution)/shard_map/ppermute | solution.py:22
  74.6 5.7 %copy-start.3 = (f32[16,60,6,128]{3,1,2,0:T(8,128)S(1)}, f32[16,60,6,128]{3,1,2,0:T(8,128)}, u32[]{:S(2)}) copy-start(f32[16,60,6,128]{3,1,2,0:T(8,128)} %copy-done.2) | copy-start | bytes 8847364
  93.1 5.4 %copy-start.15 = (f32[10,96,127]{2,1,0:T(8,128)S(1)}, f32[10,96,127]{2,1,0:T(8,128)}, u32[]{:S(2)}) copy-start(f32[10,96,127]{2,1,0:T(8,128)} %get-tuple-element.134) | copy-start | bytes 1463044
  93.1 5.4 %copy-start.16 = (f32[10,95,128]{2,1,0:T(8,128)S(1)}, f32[10,95,128]{2,1,0:T(8,128)}, u32[]{:S(2)}) copy-start(f32[10,95,128]{2,1,0:T(8,128)} %get-tuple-element.103) | copy-start | bytes 1459204
  93.1 5.4 %copy-start.17 = (f32[10,95,128]{2,1,0:T(8,128)S(1)}, f32[10,95,128]{2,1,0:T(8,128)}, u32[]{:S(2)}) copy-start(f32[10,95,128]{2,1,0:T(8,128)} %get-tuple-element.104) | copy-start | bytes 1459204
  93.1 5.4 %copy-start.18 = (f32[10,95,128]{2,1,0:T(8,128)S(1)}, f32[10,95,128]{2,1,0:T(8,128)}, u32[]{:S(2)}) copy-start(f32[10,95,128]{2,1,0:T(8,128)} %get-tuple-element.135) | copy-start | bytes 1459204
  95.4 6.9 %collective-permute-start.4 = (f32[54,128]{1,0:T(8,128)S(1)}, f32[54,128]{1,0:T(8,128)S(1)}, u32[]{:S(2)}, u32[]{:S(2)}) collective-permute-start(f32[54,128]{1,0:T(8,128)S(1)} %maximum_bitcast_fusion), channel_id=1, source_target_pairs={{0,1},{1,0},{2,3},{3,2},{4,5},{5,4},{6,7},{7,6},{8,9},{9,8},{10,11... | collective-permute-start | bytes 82952 | tf_op jit(solution)/shard_map/ppermute | solution.py:115
  102.3 2.8 %collective-permute-start.5 = (f32[54,128]{1,0:T(8,128)S(1)}, f32[54,128]{1,0:T(8,128)S(1)}, u32[]{:S(2)}, u32[]{:S(2)}) collective-permute-start(f32[54,128]{1,0:T(8,128)S(1)} %add.97), channel_id=1, source_target_pairs={{0,2},{1,3},{2,0},{3,1},{4,6},{5,7},{6,4},{7,5},{8,10},{9,11},{10,... | collective-permute-start | bytes 82952 | tf_op jit(solution)/shard_map/ppermute | solution.py:115
  105.1 8.1 %collective-permute-start.6 = (f32[54,128]{1,0:T(8,128)S(1)}, f32[54,128]{1,0:T(8,128)S(1)}, u32[]{:S(2)}, u32[]{:S(2)}) collective-permute-start(f32[54,128]{1,0:T(8,128)S(1)} %add.98), channel_id=1, source_target_pairs={{0,4},{1,5},{2,6},{3,7},{4,0},{5,1},{6,2},{7,3},{8,12},{9,13},{10,... | collective-permute-start | bytes 82952 | tf_op jit(solution)/shard_map/ppermute | solution.py:115
  105.6 21.1 %collective-permute-start.8 = (f32[10,1,128]{2,1,0:T(1,128)S(1)}, f32[10,1,128]{2,1,0:T(1,128)S(1)}, u32[]{:S(2)}, u32[]{:S(2)}) collective-permute-start(f32[10,1,128]{2,1,0:T(1,128)S(1)} %get-tuple-element.96), channel_id=1, source_target_pairs={{0,16},{16,32},{32,48},{48,64},{64,80},{80,96},{96,112},{112,0},{1... | collective-permute-start | bytes 15368 | tf_op jit(solution)/shard_map/ppermute | solution.py:19
  105.7 21.0 %collective-permute-start.9 = (f32[10,1,128]{2,1,0:T(1,128)S(1)}, f32[10,1,128]{2,1,0:T(1,128)S(1)}, u32[]{:S(2)}, u32[]{:S(2)}) collective-permute-start(f32[10,1,128]{2,1,0:T(1,128)S(1)} %get-tuple-element.95), channel_id=1, source_target_pairs={{0,112},{16,0},{32,16},{48,32},{64,48},{80,64},{96,80},{112,96},{1... | collective-permute-start | bytes 15368 | tf_op jit(solution)/shard_map/ppermute | solution.py:20
  110.7 13.2 %collective-permute-start.10 = (f32[10,96,1]{2,1,0:T(8,128)S(1)}, f32[10,96,1]{2,1,0:T(8,128)S(1)}, u32[]{:S(2)}, u32[]{:S(2)}) collective-permute-start(f32[10,96,1]{2,1,0:T(8,128)S(1)} %get-tuple-element.94), channel_id=1, source_target_pairs={{0,1},{1,2},{2,3},{3,4},{4,5},{5,6},{6,7},{7,8},{8,9},{9,10},{10,1... | collective-permute-start | bytes 11528 | tf_op jit(solution)/shard_map/ppermute | solution.py:21
  112.9 13.8 %collective-permute-start.11 = (f32[10,96,1]{2,1,0:T(8,128)S(1)}, f32[10,96,1]{2,1,0:T(8,128)S(1)}, u32[]{:S(2)}, u32[]{:S(2)}) collective-permute-start(f32[10,96,1]{2,1,0:T(8,128)S(1)} %get-tuple-element.93), channel_id=1, source_target_pairs={{0,15},{1,0},{2,1},{3,2},{4,3},{5,4},{6,5},{7,6},{8,7},{9,8},{10,9... | collective-permute-start | bytes 11528 | tf_op jit(solution)/shard_map/ppermute | solution.py:22
  113.3 4.3 %collective-permute-start.7 = (f32[54,128]{1,0:T(8,128)S(1)}, f32[54,128]{1,0:T(8,128)S(1)}, u32[]{:S(2)}, u32[]{:S(2)}) collective-permute-start(f32[54,128]{1,0:T(8,128)S(1)} %add.99), channel_id=1, source_target_pairs={{0,8},{1,9},{2,10},{3,11},{4,12},{5,13},{6,14},{7,15},{8,0},{9,1},... | collective-permute-start | bytes 82952 | tf_op jit(solution)/shard_map/ppermute | solution.py:115
  126.7 6.2 %collective-permute-start.12 = (f32[54,128]{1,0:T(8,128)S(1)}, f32[54,128]{1,0:T(8,128)S(1)}, u32[]{:S(2)}, u32[]{:S(2)}) collective-permute-start(f32[54,128]{1,0:T(8,128)S(1)} %add.100), channel_id=1, source_target_pairs={{0,16},{16,0},{32,48},{48,32},{64,80},{80,64},{96,112},{112,96},{1... | collective-permute-start | bytes 82952 | tf_op jit(solution)/shard_map/ppermute | solution.py:115
  128.6 21.4 %all-to-all-start.1 = ((f32[16,20,6,128]{3,1,2,0:T(8,128)}), f32[16,20,6,128]{3,1,2,0:T(8,128)S(1)}, u32[]{:S(2)}, u32[]{:S(2)}) async-start(f32[16,20,6,128]{3,1,2,0:T(8,128)} %fusion.12), calls=%async_computation.1 | async-start | bytes 2359296 | tf_op jit(solution)/shard_map/all_to_all | solution.py:169
  133.0 2.8 %collective-permute-start.13 = (f32[54,128]{1,0:T(8,128)S(1)}, f32[54,128]{1,0:T(8,128)S(1)}, u32[]{:S(2)}, u32[]{:S(2)}) collective-permute-start(f32[54,128]{1,0:T(8,128)S(1)} %add.105), channel_id=1, source_target_pairs={{0,32},{16,48},{32,0},{48,16},{64,96},{80,112},{96,64},{112,80},{1... | collective-permute-start | bytes 82952 | tf_op jit(solution)/shard_map/ppermute | solution.py:115
  135.8 4.5 %collective-permute-start.14 = (f32[54,128]{1,0:T(8,128)S(1)}, f32[54,128]{1,0:T(8,128)S(1)}, u32[]{:S(2)}, u32[]{:S(2)}) collective-permute-start(f32[54,128]{1,0:T(8,128)S(1)} %add.106), channel_id=1, source_target_pairs={{0,64},{16,80},{32,96},{48,112},{64,0},{80,16},{96,32},{112,48},{1... | collective-permute-start | bytes 82952 | tf_op jit(solution)/shard_map/ppermute | solution.py:115
  (34 other events, 92.2 us)

commit v2 on v0

--- a/solution.py
+++ b/solution.py
@@ -162,7 +162,8 @@
     chunks = stacked.reshape(stacked.shape[0], tile_rows // blocks, blocks, tile_cols)
     band = lax.all_to_all(chunks.transpose(2, 0, 1, 3), "lon", split_axis=0, concat_axis=0, tiled=True)
     weight_grads, band_grad = network_vjp(weights, band[:, : 2 * levels], band[:, 2 * levels :])
-    packed = pack(weight_grads)
+    scale = 1.0 / math.sqrt(tile_rows * lax.axis_size("lat") * tile_cols * lax.axis_size("lon"))
+    packed = pack(weight_grads) * scale
     packed, plane_halo = lax.optimization_barrier((packed, plane_halo))
     summed = unpack(butterfly_sum(packed, ("lon", "lat")), weight_grads)
     returned = lax.all_to_all(band_grad, "lon", split_axis=0, concat_axis=0, tiled=True)
@@ -182,10 +183,9 @@
     first_laplace = laplace(velocity_adjoint, part(levels, 2 * levels), sea_cells, sea_near, *faces)
     scaled = viscosity * first_laplace
     viscous_term = laplace(scaled, edges(scaled), sea_cells, sea_near, *faces)
-    scale = 1.0 / math.sqrt(tile_rows * lax.axis_size("lat") * tile_cols * lax.axis_size("lon"))
     tracer_grad = tracer_adjoint + tracer_term + input_grad[:levels]
     velocity_grad = velocity_adjoint - viscous_term + input_grad[levels:]
-    return (tracer_grad, velocity_grad, summed[0] * scale, summed[1] * scale, summed[2] * scale)
+    return (tracer_grad, velocity_grad, summed[0], summed[1], summed[2])
 
 
 def solution(mesh):

time: 155 us -> 165 us (1.065)
  starting transfers between devices: 38.6 us -> 45.7 us
  other arithmetic: 18.1 us -> 22.1 us
  local copies, waits for them, and re-layouts: 60.6 us -> 64.3 us
  waiting for transfers between devices: 15 us -> 11.6 us
  matrix products: 20.9 us -> 19.2 us
    ppermute x7, starting transfers between devices: 10.7 us -> 17 us  [butterfly_sum(): values = values + lax.ppermute(values, axis, pairs)]
    ppermute x2, waiting for transfers between devices: 6.69 us -> 2.41 us  [edges(): right = lax.ppermute(block[..., :, :1], 'lon', ring('lon', -1))]
    ppermute x2, starting transfers between devices: 1.63 us -> 4.82 us  [edges(): right = lax.ppermute(block[..., :, :1], 'lon', ring('lon', -1))]
    ppermute x7, waiting for transfers between devices: 4.58 us -> 7.22 us  [butterfly_sum(): values = values + lax.ppermute(values, axis, pairs)]
    slice x9, local copies, waits for them, and re-layouts: 6.86 us -> 9.29 us  [part(): return tuple((piece[lo:hi] for piece in (below, above, left, right)))]
    add x1, other arithmetic: 1.75 us -> 3.82 us  [unstack_taps(): return first + middle + last]
    slice x12, local copies, waits for them, and re-layouts: 5.45 us -> 7.4 us  [lon_roll(): jnp.roll(values[..., -1:], 1, axis=0)]
    slice x6, local copies, waits for them, and re-layouts: 6.5 us -> 4.72 us  [lon_roll(): values[..., :-1]]
  transfers between devices with their start and end apart: 17 -> 17, of which waited for: 8 -> 8; matrix products, arithmetic and copies ran while one was open for 47% -> 45% of each run, Pallas kernels for 0% -> 0%
where the time goes in v2:
time: 165 us; the launch traced here: 164 us
  local copies, waits for them, and re-layouts  64.3 us (39%)
  starting transfers between devices  45.7 us (28%)
  other arithmetic  22.1 us (13%)
  matrix products  19.2 us (12%)
  waiting for transfers between devices  11.6 us (7%)
    ppermute x7, starting transfers between devices, butterfly_sum(): values = values + lax.ppermute(values, axis, pairs)  17 us
    unnamed x78, local copies, waits for them, and re-layouts  9.35 us
    slice x9, local copies, waits for them, and re-layouts, part(): return tuple((piece[lo:hi] for piece in (below, above, left, right)))  9.29 us
    slice x12, local copies, waits for them, and re-layouts, lon_roll(): jnp.roll(values[..., -1:], 1, axis=0)  7.4 us
    ppermute x7, waiting for transfers between devices, butterfly_sum(): values = values + lax.ppermute(values, axis, pairs)  7.22 us
    all_to_all x1, starting transfers between devices, on_device(): lax.all_to_all(chunks.transpose(2, 0, 1, 3), 'lon', split_axis=0, concat_...  6.95 us
    slice x2, local copies, waits for them, and re-layouts, edges(): right = lax.ppermute(block[..., :, :1], 'lon', ring('lon', -1))  6.69 us
    all_to_all x1, starting transfers between devices, on_device(): lax.all_to_all(band_grad, 'lon', split_axis=0, concat_axis=0, tiled=True)  6.58 us
  transfers between devices with their start and end apart: 17, of which 8 were waited for; matrix products, arithmetic and copies ran while one was open for 45% of the time, Pallas kernels for 0%

profile of v2, /device:TPU:1, one launch (start us, length us, event | category | flops | bytes accessed | tf_op | source)
XLA Modules:
  0.0 164.2 jit_solution(3435147712706336339)
XLA Ops:
  6.0 2.4 %copy.169 = f32[40,6,16,128]{3,0,1,2:T(8,128)} copy(f32[40,6,16,128]{3,2,1,0:T(8,128)S(1)} %bitcast.76) | data formatting | bytes 3932160 | tf_op jit(solution)/shard_map/reshape | solution.py:162
  8.4 6.9 %all-to-all-start = ((f32[16,40,6,128]{3,1,2,0:T(8,128)}), f32[16,40,6,128]{3,1,2,0:T(8,128)S(1)}, u32[]{:S(2)}, u32[]{:S(2)}) async-start(f32[16,40,6,128]{3,1,2,0:T(8,128)} %bitcast.75), calls=%async_computation | async-start | bytes 3932160 | tf_op jit(solution)/shard_map/all_to_all | solution.py:163
  18.2 2.6 %collective-permute-start = (f32[32,1,128]{2,1,0:T(1,128)}, f32[32,1,128]{2,1,0:T(1,128)}, u32[]{:S(2)}, u32[]{:S(2)}) collective-permute-start(f32[32,1,128]{2,1,0:T(1,128)} %get-tuple-element.64), channel_id=1, source_target_pairs={{0,16},{16,32},{32,48},{48,64},{64,80},{80,96},{96,112},{112,0},{1... | collective-permute-start | bytes 49160 | tf_op jit(solution)/shard_map/ppermute | solution.py:19
  20.8 3.5 %collective-permute-start.1 = (f32[32,1,128]{2,1,0:T(1,128)}, f32[32,1,128]{2,1,0:T(1,128)}, u32[]{:S(2)}, u32[]{:S(2)}) collective-permute-start(f32[32,1,128]{2,1,0:T(1,128)} %get-tuple-element.63), channel_id=1, source_target_pairs={{0,112},{16,0},{32,16},{48,32},{64,48},{80,64},{96,80},{112,96},{1... | collective-permute-start | bytes 49160 | tf_op jit(solution)/shard_map/ppermute | solution.py:20
  24.3 4.2 %fusion.79 = (f32[32,96,1]{2,1,0:T(8,128)}, f32[32,96,1]{2,1,0:T(8,128)}) fusion(f32[32,96,128]{2,1,0:T(8,128)} %bitcast_dynamic-update-slice_fusion), kind=kLoop, calls=%fused_computation.108 | loop fusion | bytes 49152 | tf_op jit(solution)/shard_map/slice | solution.py:22
  28.4 2.5 %copy.121 = f32[32,96,1]{1,0,2:T(8,128)} copy(f32[32,96,1]{2,1,0:T(8,128)} %get-tuple-element.62) | data formatting | bytes 24576 | tf_op jit(solution)/shard_map/slice | solution.py:21
  32.3 2.5 %copy.122 = f32[32,96,1]{1,0,2:T(8,128)} copy(f32[32,96,1]{2,1,0:T(8,128)} %get-tuple-element.61) | data formatting | bytes 24576 | tf_op jit(solution)/shard_map/slice | solution.py:22
  47.5 2.7 %convolution_bitcast_fusion.1 = f32[16,96,6,128]{3,1,2,0:T(8,128)S(1)} fusion(f32[20,96,1,1]{1,0,2,3:T(8,128)} %reshape.80, f32[16,40,6,128]{3,1,2,0:T(8,128)S(1)} %all-to-all-done), kind=kOutput, calls=%fused_computation.10 | convolution fusion | flops 141557760 | bytes 5905920 | tf_op jit(solution)/shard_map/oc,soml->scml/dot_general | solution.py:92
  57.0 4.0 %fusion.9 = (f32[16,32,6,128]{3,1,2,0:T(8,128)S(1)}, f32[16,32,6,128]{3,1,2,0:T(8,128)S(1)}) fusion(f32[16,96,6,128]{3,1,2,0:T(8,128)S(1)} %convolution_bitcast_fusion.1, f32[1,32,6,1]{3,1,2,0:T(8,128)S(1)} %get-tuple-element.42, f32[15,32,6,1]{3,1,2,0:T(8,128)S(1)} %get-tuple-element.44, f32[16,32,6,127]{3,1,2,0:T(8,128)S(1)} %get-tuple-element.46, ...), kind=kOutput, calls=%fused_computation.19 | convolution fusion | flops 237109248 | bytes 12595200 | tf_op jit(solution)/shard_map/oc,scml->soml/dot_general | solution.py:80
  62.2 2.3 %fusion.19 = f32[32,96]{1,0:T(8,128)S(1)} fusion(f32[16,32,6,128]{3,1,2,0:T(8,128)S(1)} %get-tuple-element.116, f32[1,32,6,1]{3,1,2,0:T(8,128)S(1)} %get-tuple-element.72, f32[15,32,6,1]{3,1,2,0:T(8,128)S(1)} %get-tuple-element.74, f32[16,32,6,127]{3,1,2,0:T(8,128)S(1)} %get-tuple-element.76, f32[16,32,6,128]{3,1,2,0:T(8,128)S(1)} %tanh_bitcast_fusion.1, ...), kind=kOutput, calls=%fused_computation.28 | convolution fusion | flops 233570304 | bytes 6303744 | tf_op jit(solution)/shard_map/soml,scml->oc/dot_general | solution.py:94
  66.7 2.6 %fusion.67 = (f32[15,32,6,1]{3,1,2,0:T(8,128)}, f32[15,32,6,1]{3,1,2,0:T(8,128)}) fusion(f32[16,96,6,128]{3,1,2,0:T(8,128)S(1)} %convolution_bitcast_fusion), kind=kLoop, calls=%fused_computation.96 | loop fusion | bytes 46080 | tf_op jit(solution)/shard_map/jit(_roll_static)/slice | solution.py:52
  69.6 2.2 %fusion.68 = (f32[16,32,6,127]{3,1,2,0:T(8,128)}, f32[16,32,6,127]{3,1,2,0:T(8,128)}) fusion(f32[16,96,6,128]{3,1,2,0:T(8,128)S(1)} %convolution_bitcast_fusion), kind=kLoop, calls=%fused_computation.97 | loop fusion | bytes 6242304 | tf_op jit(solution)/shard_map/slice | solution.py:52
  71.8 2.4 %fusion.24 = f32[20,96]{1,0:T(8,128)S(1)} fusion(f32[16,20,6,128]{3,1,2,0:T(8,128)S(1)} %get-tuple-element.53, f32[1,32,6,1]{3,1,2,0:T(8,128)S(1)} %get-tuple-element.66, f32[15,32,6,1]{3,1,2,0:T(8,128)S(1)} %get-tuple-element.68, f32[16,32,6,127]{3,1,2,0:T(8,128)S(1)} %get-tuple-element.70, f32[16,32,6,128]{3,1,2,0:T(8,128)S(1)} %get-tuple-element.117, ...), kind=kOutput, calls=%fused_computation.29 | convolution fusion | flops 148635648 | bytes 5709312 | tf_op jit(solution)/shard_map/soml,scml->oc/dot_general | solution.py:91
  74.5 4.5 %fusion.7 = f32[16,32,6,128]{3,1,2,0:T(8,128)S(1)} fusion(f32[16,96,6,128]{3,1,2,0:T(8,128)} %copy-done, f32[1,32,6,1]{3,1,2,0:T(8,128)S(1)} %get-tuple-element.36, f32[15,32,6,1]{3,1,2,0:T(8,128)} %get-tuple-element.38, f32[16,32,6,127]{3,1,2,0:T(8,128)} %get-tuple-element.40, f32[16,32,6,127]{3,1,2,0:T(8,128)} %get-tuple-element.39, ...), kind=kLoop, calls=%fused_computation.16 | loop fusion | flops 3538944 | bytes 7864320 | tf_op jit(solution)/shard_map/mul | solution.py:96
  84.4 3.1 %convolution_bitcast_fusion.2 = f32[16,60,6,128]{3,1,2,0:T(8,128)S(1)} fusion(f32[16,32,6,128]{3,1,2,0:T(8,128)} %copy-done.6, f32[32,60]{0,1:T(8,128)S(1)} %copy-done.26), kind=kOutput, calls=%fused_computation.13 | convolution fusion | flops 141557760 | bytes 4529664 | tf_op jit(solution)/shard_map/oc,soml->scml/dot_general | solution.py:98
  97.0 3.8 %fusion.12 = f32[16,20,6,128]{3,1,2,0:T(8,128)} fusion(f32[16,60,6,128]{3,1,2,0:T(8,128)} %copy-done.4, f32[1,20,6,1]{3,1,2,0:T(8,128)} %get-tuple-element.48, f32[15,20,6,1]{3,1,2,0:T(8,128)} %get-tuple-element.50, f32[16,20,6,127]{3,1,2,0:T(8,128)S(1)} %get-tuple-element.52, f32[16,20,6,127]{3,1,2,0:T(8,128)S(1)} %get-tuple-element.51, ...), kind=kLoop, calls=%fused_computation.25 | loop fusion | flops 1474560 | bytes 3932160 | tf_op jit(solution)/shard_map/add | solution.py:66
  100.9 6.6 %all-to-all-start.1 = ((f32[16,20,6,128]{3,1,2,0:T(8,128)}), f32[16,20,6,128]{3,1,2,0:T(8,128)S(1)}, u32[]{:S(2)}, u32[]{:S(2)}) async-start(f32[16,20,6,128]{3,1,2,0:T(8,128)} %fusion.12), calls=%async_computation.1 | async-start | bytes 2359296 | tf_op jit(solution)/shard_map/all_to_all | solution.py:169
  113.5 8.3 %collective-permute-start.10 = (f32[54,128]{1,0:T(8,128)S(1)}, f32[54,128]{1,0:T(8,128)S(1)}, u32[]{:S(2)}, u32[]{:S(2)}) collective-permute-start(f32[54,128]{1,0:T(8,128)S(1)} %add.102), channel_id=1, source_target_pairs={{0,4},{1,5},{2,6},{3,7},{4,0},{5,1},{6,2},{7,3},{8,12},{9,13},{10,... | collective-permute-start | bytes 82952 | tf_op jit(solution)/shard_map/ppermute | solution.py:113
  121.9 4.7 %fusion.44 = (f32[10,96,128]{2,1,0:T(8,128)S(1)}, f32[10,96,128]{2,1,0:T(8,128)}, f32[10,96,128]{2,1,0:T(8,128)}, f32[10,96,128]{2,1,0:T(8,128)}, f32[10,96,128]{2,1,0:T(8,128)}) fusion(f32[10,96,128]{2,1,0:T(8,128)S(1)} %copy-done.1, f32[10,96,1]{2,1,0:T(8,128)} %copy.130, f32[10,96,127]{2,1,0:T(8,128)} %get-tuple-element.123, ...), kind=kLoop, calls=%fused_computation.54 | loop fusion | flops 3563520 | bytes 7618560 | tf_op jit(solution)/shard_map/mul | solution.py:184
  126.5 5.2 %collective-permute-start.11 = (f32[54,128]{1,0:T(8,128)S(1)}, f32[54,128]{1,0:T(8,128)S(1)}, u32[]{:S(2)}, u32[]{:S(2)}) collective-permute-start(f32[54,128]{1,0:T(8,128)S(1)} %add.103), channel_id=1, source_target_pairs={{0,8},{1,9},{2,10},{3,11},{4,12},{5,13},{6,14},{7,15},{8,0},{9,1},... | collective-permute-start | bytes 82952 | tf_op jit(solution)/shard_map/ppermute | solution.py:113
  134.1 3.1 %collective-permute-done.12 = f32[54,128]{1,0:T(8,128)S(1)} collective-permute-done((f32[54,128]{1,0:T(8,128)S(1)}, f32[54,128]{1,0:T(8,128)S(1)}, u32[]{:S(2)}, u32[]{:S(2)}) %collective-permute-start.12) | collective-permute-done | bytes 27680 | tf_op jit(solution)/shard_map/ppermute | solution.py:113
  143.2 4.8 %collective-permute-start.4 = (f32[10,96,1]{2,1,0:T(8,128)}, f32[10,96,1]{2,1,0:T(8,128)}, u32[]{:S(2)}, u32[]{:S(2)}) collective-permute-start(f32[10,96,1]{2,1,0:T(8,128)} %get-tuple-element.84), channel_id=1, source_target_pairs={{0,15},{1,0},{2,1},{3,2},{4,3},{5,4},{6,5},{7,6},{8,7},{9,8},{10,9... | collective-permute-start | bytes 11528 | tf_op jit(solution)/shard_map/ppermute | solution.py:22
  157.2 2.4 %collective-permute-done.4 = f32[10,96,1]{2,1,0:T(8,128)} collective-permute-done((f32[10,96,1]{2,1,0:T(8,128)}, f32[10,96,1]{2,1,0:T(8,128)}, u32[]{:S(2)}, u32[]{:S(2)}) %collective-permute-start.4) | collective-permute-done | bytes 3872 | tf_op jit(solution)/shard_map/ppermute | solution.py:22
  161.6 2.7 %fusion.53 = f32[10,96,128]{2,1,0:T(8,128)} fusion(f32[10,96,128]{2,1,0:T(8,128)S(1)} %copy-done.1, f32[10,96,128]{2,1,0:T(8,128)S(1)} %copy-done.12, f32[10,96,128]{2,1,0:T(8,128)S(1)} %get-tuple-element.30, f32[10,96,1]{2,1,0:T(8,128)} %collective-permute-done.4, f32[10,96,127]{2,1,0:T(8,128)S(1)} %copy-done.19, f32[10,96,128]{2,1,0:T(8,128)S(1)} %copy-done.11, ...), kind=kLoop, calls=%fused_computation.67 | loop fusion | flops 2088960 | bytes 5898240 | tf_op jit(solution)/shard_map/add | solution.py:187
  (183 shorter events, 72.9 us)
Async XLA Ops:
  8.4 7.6 %copy-start.24 = (f32[96,128]{1,0:T(8,128)S(1)}, f32[96,128]{1,0:T(8,128)}, u32[]{:S(2)}) copy-start(f32[96,128]{1,0:T(8,128)} %param.17) | copy-start | bytes 147460
  8.4 39.2 %all-to-all-start = ((f32[16,40,6,128]{3,1,2,0:T(8,128)}), f32[16,40,6,128]{3,1,2,0:T(8,128)S(1)}, u32[]{:S(2)}, u32[]{:S(2)}) async-start(f32[16,40,6,128]{3,1,2,0:T(8,128)} %bitcast.75), calls=%async_computation | async-start | bytes 3932160 | tf_op jit(solution)/shard_map/all_to_all | solution.py:163
  18.2 64.4 %collective-permute-start = (f32[32,1,128]{2,1,0:T(1,128)}, f32[32,1,128]{2,1,0:T(1,128)}, u32[]{:S(2)}, u32[]{:S(2)}) collective-permute-start(f32[32,1,128]{2,1,0:T(1,128)} %get-tuple-element.64), channel_id=1, source_target_pairs={{0,16},{16,32},{32,48},{48,64},{64,80},{80,96},{96,112},{112,0},{1... | collective-permute-start | bytes 49160 | tf_op jit(solution)/shard_map/ppermute | solution.py:19
  20.8 61.7 %collective-permute-start.1 = (f32[32,1,128]{2,1,0:T(1,128)}, f32[32,1,128]{2,1,0:T(1,128)}, u32[]{:S(2)}, u32[]{:S(2)}) collective-permute-start(f32[32,1,128]{2,1,0:T(1,128)} %get-tuple-element.63), channel_id=1, source_target_pairs={{0,112},{16,0},{32,16},{48,32},{64,48},{80,64},{96,80},{112,96},{1... | collective-permute-start | bytes 49160 | tf_op jit(solution)/shard_map/ppermute | solution.py:20
  31.0 51.6 %collective-permute-start.2 = (f32[32,96,1]{1,0,2:T(8,128)}, f32[32,96,1]{1,0,2:T(8,128)}, u32[]{:S(2)}, u32[]{:S(2)}) collective-permute-start(f32[32,96,1]{1,0,2:T(8,128)} %copy.121), channel_id=1, source_target_pairs={{0,1},{1,2},{2,3},{3,4},{4,5},{5,6},{6,7},{7,8},{8,9},{9,10},{10,1... | collective-permute-start | bytes 36872 | tf_op jit(solution)/shard_map/ppermute | solution.py:21
  34.8 47.8 %collective-permute-start.3 = (f32[32,96,1]{1,0,2:T(8,128)}, f32[32,96,1]{1,0,2:T(8,128)}, u32[]{:S(2)}, u32[]{:S(2)}) collective-permute-start(f32[32,96,1]{1,0,2:T(8,128)} %copy.122), channel_id=1, source_target_pairs={{0,15},{1,0},{2,1},{3,2},{4,3},{5,4},{6,5},{7,6},{8,7},{9,8},{10,9... | collective-permute-start | bytes 36872 | tf_op jit(solution)/shard_map/ppermute | solution.py:22
  100.8 9.5 %copy-start.29 = (f32[10,96,1]{1,0,2:T(8,128)S(1)}, f32[10,96,1]{1,0,2:T(8,128)}, u32[]{:S(2)}) copy-start(f32[10,96,1]{1,0,2:T(8,128)} %get-tuple-element.112) | copy-start | bytes 11524
  100.8 21.0 %copy-start.8 = (s32[10,96,128]{2,1,0:T(8,128)S(1)}, s32[10,96,128]{2,1,0:T(8,128)}, u32[]{:S(2)}) copy-start(s32[10,96,128]{2,1,0:T(8,128)} %param.15) | copy-start | bytes 1474564
  100.9 21.0 %copy-start.28 = (f32[96,128]{1,0:T(8,128)S(1)}, f32[96,128]{1,0:T(8,128)}, u32[]{:S(2)}) copy-start(f32[96,128]{1,0:T(8,128)} %param.18) | copy-start | bytes 147460
  100.9 21.0 %copy-start.32 = (f32[10,1,128]{2,1,0:T(1,128)S(1)}, f32[10,1,128]{2,1,0:T(1,128)}, u32[]{:S(2)}) copy-start(f32[10,1,128]{2,1,0:T(1,128)} %get-tuple-element.105) | copy-start | bytes 15364
  100.9 21.0 %copy-start.33 = (f32[10,1,128]{2,1,0:T(1,128)S(1)}, f32[10,1,128]{2,1,0:T(1,128)}, u32[]{:S(2)}) copy-start(f32[10,1,128]{2,1,0:T(1,128)} %get-tuple-element.106) | copy-start | bytes 15364
  100.9 21.0 %copy-start.34 = (f32[10,1,128]{2,1,0:T(1,128)S(1)}, f32[10,1,128]{2,1,0:T(1,128)}, u32[]{:S(2)}) copy-start(f32[10,1,128]{2,1,0:T(1,128)} %get-tuple-element.108) | copy-start | bytes 15364
  100.9 52.3 %all-to-all-start.1 = ((f32[16,20,6,128]{3,1,2,0:T(8,128)}), f32[16,20,6,128]{3,1,2,0:T(8,128)S(1)}, u32[]{:S(2)}, u32[]{:S(2)}) async-start(f32[16,20,6,128]{3,1,2,0:T(8,128)} %fusion.12), calls=%async_computation.1 | async-start | bytes 2359296 | tf_op jit(solution)/shard_map/all_to_all | solution.py:169
  107.5 1.3 collective-permute-start.8
  108.8 4.7 %collective-permute-start.9 = (f32[54,128]{1,0:T(8,128)S(1)}, f32[54,128]{1,0:T(8,128)S(1)}, u32[]{:S(2)}, u32[]{:S(2)}) collective-permute-start(f32[54,128]{1,0:T(8,128)S(1)} %add.101), channel_id=1, source_target_pairs={{0,2},{1,3},{2,0},{3,1},{4,6},{5,7},{6,4},{7,5},{8,10},{9,11},{10,... | collective-permute-start | bytes 82952 | tf_op jit(solution)/shard_map/ppermute | solution.py:113
  113.5 13.0 %collective-permute-start.10 = (f32[54,128]{1,0:T(8,128)S(1)}, f32[54,128]{1,0:T(8,128)S(1)}, u32[]{:S(2)}, u32[]{:S(2)}) collective-permute-start(f32[54,128]{1,0:T(8,128)S(1)} %add.102), channel_id=1, source_target_pairs={{0,4},{1,5},{2,6},{3,7},{4,0},{5,1},{6,2},{7,3},{8,12},{9,13},{10,... | collective-permute-start | bytes 82952 | tf_op jit(solution)/shard_map/ppermute | solution.py:113
  126.5 6.5 %collective-permute-start.11 = (f32[54,128]{1,0:T(8,128)S(1)}, f32[54,128]{1,0:T(8,128)S(1)}, u32[]{:S(2)}, u32[]{:S(2)}) collective-permute-start(f32[54,128]{1,0:T(8,128)S(1)} %add.103), channel_id=1, source_target_pairs={{0,8},{1,9},{2,10},{3,11},{4,12},{5,13},{6,14},{7,15},{8,0},{9,1},... | collective-permute-start | bytes 82952 | tf_op jit(solution)/shard_map/ppermute | solution.py:113
  133.0 4.2 %collective-permute-start.12 = (f32[54,128]{1,0:T(8,128)S(1)}, f32[54,128]{1,0:T(8,128)S(1)}, u32[]{:S(2)}, u32[]{:S(2)}) collective-permute-start(f32[54,128]{1,0:T(8,128)S(1)} %add.104), channel_id=1, source_target_pairs={{0,16},{16,0},{32,48},{48,32},{64,80},{80,64},{96,112},{112,96},{1... | collective-permute-start | bytes 82952 | tf_op jit(solution)/shard_map/ppermute | solution.py:113
  137.3 3.0 %collective-permute-start.13 = (f32[54,128]{1,0:T(8,128)S(1)}, f32[54,128]{1,0:T(8,128)S(1)}, u32[]{:S(2)}, u32[]{:S(2)}) collective-permute-start(f32[54,128]{1,0:T(8,128)S(1)} %add.105), channel_id=1, source_target_pairs={{0,32},{16,48},{32,0},{48,16},{64,96},{80,112},{96,64},{112,80},{1... | collective-permute-start | bytes 82952 | tf_op jit(solution)/shard_map/ppermute | solution.py:113
  140.3 10.7 %collective-permute-start.14 = (f32[54,128]{1,0:T(8,128)S(1)}, f32[54,128]{1,0:T(8,128)S(1)}, u32[]{:S(2)}, u32[]{:S(2)}) collective-permute-start(f32[54,128]{1,0:T(8,128)S(1)} %add.106), channel_id=1, source_target_pairs={{0,64},{16,80},{32,96},{48,112},{64,0},{80,16},{96,32},{112,48},{1... | collective-permute-start | bytes 82952 | tf_op jit(solution)/shard_map/ppermute | solution.py:113
  143.2 16.4 %collective-permute-start.4 = (f32[10,96,1]{2,1,0:T(8,128)}, f32[10,96,1]{2,1,0:T(8,128)}, u32[]{:S(2)}, u32[]{:S(2)}) collective-permute-start(f32[10,96,1]{2,1,0:T(8,128)} %get-tuple-element.84), channel_id=1, source_target_pairs={{0,15},{1,0},{2,1},{3,2},{4,3},{5,4},{6,5},{7,6},{8,7},{9,8},{10,9... | collective-permute-start | bytes 11528 | tf_op jit(solution)/shard_map/ppermute | solution.py:22
  148.0 11.6 %collective-permute-start.5 = (f32[10,96,1]{2,1,0:T(8,128)}, f32[10,96,1]{2,1,0:T(8,128)}, u32[]{:S(2)}, u32[]{:S(2)}) collective-permute-start(f32[10,96,1]{2,1,0:T(8,128)} %get-tuple-element.83), channel_id=1, source_target_pairs={{0,1},{1,2},{2,3},{3,4},{4,5},{5,6},{6,7},{7,8},{8,9},{9,10},{10,1... | collective-permute-start | bytes 11528 | tf_op jit(solution)/shard_map/ppermute | solution.py:21
  148.0 13.2 %collective-permute-start.6 = (f32[10,1,128]{2,1,0:T(1,128)S(1)}, f32[10,1,128]{2,1,0:T(1,128)S(1)}, u32[]{:S(2)}, u32[]{:S(2)}) collective-permute-start(f32[10,1,128]{2,1,0:T(1,128)S(1)} %get-tuple-element.80), channel_id=1, source_target_pairs={{0,112},{16,0},{32,16},{48,32},{64,48},{80,64},{96,80},{112,96},{1... | collective-permute-start | bytes 15368 | tf_op jit(solution)/shard_map/ppermute | solution.py:20
  149.9 11.7 %collective-permute-start.7 = (f32[10,1,128]{2,1,0:T(1,128)S(1)}, f32[10,1,128]{2,1,0:T(1,128)S(1)}, u32[]{:S(2)}, u32[]{:S(2)}) collective-permute-start(f32[10,1,128]{2,1,0:T(1,128)S(1)} %get-tuple-element.79), channel_id=1, source_target_pairs={{0,16},{16,32},{32,48},{48,64},{64,80},{80,96},{96,112},{112,0},{1... | collective-permute-start | bytes 15368 | tf_op jit(solution)/shard_map/ppermute | solution.py:19
  (30 other events, 97.0 us)

commit v3 on v0

--- a/solution.py
+++ b/solution.py
@@ -109,9 +109,15 @@
         size = lax.axis_size(axis)
         stride = 1
         while stride < size:
-            pairs = [(i, i ^ stride) for i in range(size)]
-            values = values + lax.ppermute(values, axis, pairs)
-            stride *= 2
+            def partner(offset):
+                return lax.ppermute(values, axis, [(i, i ^ offset) for i in range(size)])
+
+            if 4 * stride <= size:
+                values = (values + partner(stride)) + (partner(2 * stride) + partner(3 * stride))
+                stride *= 4
+            else:
+                values = values + partner(stride)
+                stride *= 2
     return values
 
 
@@ -164,7 +170,7 @@
     weight_grads, band_grad = network_vjp(weights, band[:, : 2 * levels], band[:, 2 * levels :])
     packed = pack(weight_grads)
     packed, plane_halo = lax.optimization_barrier((packed, plane_halo))
-    summed = unpack(butterfly_sum(packed, ("lon", "lat")), weight_grads)
+    summed = unpack(butterfly_sum(packed, ("lat", "lon")), weight_grads)
     returned = lax.all_to_all(band_grad, "lon", split_axis=0, concat_axis=0, tiled=True)
     input_grad = returned.transpose(1, 2, 0, 3).reshape(2 * levels, tile_rows, tile_cols)
     below, above, left, right = plane_halo

time: 155 us -> 164 us (1.058)
  local copies, waits for them, and re-layouts: 60.6 us -> 67.1 us
  other arithmetic: 18.1 us -> 21.7 us
  waiting for transfers between devices: 15 us -> 12.5 us
  starting transfers between devices: 38.6 us -> 40.6 us
    ppermute x2, waiting for transfers between devices: 6.69 us -> 0.01 us  [edges(): right = lax.ppermute(block[..., :, :1], 'lon', ring('lon', -1))]
    ppermute x7 -> x10, starting transfers between devices: 10.7 us -> 16.9 us  [partner(): return lax.ppermute(values, axis, [(i, i ^ offset) for i in range(size)])]
    ppermute x7 -> x10, waiting for transfers between devices: 4.58 us -> 10 us  [partner(): return lax.ppermute(values, axis, [(i, i ^ offset) for i in range(size)])]
    slice x9, local copies, waits for them, and re-layouts: 6.86 us -> 10.9 us  [part(): return tuple((piece[lo:hi] for piece in (below, above, left, right)))]
    all_to_all x1, starting transfers between devices: 7.55 us -> 4.01 us  [on_device(): lax.all_to_all(band_grad, 'lon', split_axis=0, concat_axis=0, tiled=True)]
    add x1, other arithmetic: 1.75 us -> 3.99 us  [unstack_taps(): return first + middle + last]
    ppermute x2, waiting for transfers between devices: 2.01 us -> 0.01 us  [edges(): above = lax.ppermute(block[..., :1, :], 'lat', ring('lat', -1))]
    slice x12, local copies, waits for them, and re-layouts: 5.45 us -> 7.38 us  [lon_roll(): jnp.roll(values[..., -1:], 1, axis=0)]
  transfers between devices with their start and end apart: 17 -> 20, of which waited for: 8 -> 3; matrix products, arithmetic and copies ran while one was open for 47% -> 52% of each run, Pallas kernels for 0% -> 0%
where the time goes in v3:
time: 164 us; the launch traced here: 163 us
  local copies, waits for them, and re-layouts  67.1 us (41%)
  starting transfers between devices  40.6 us (25%)
  other arithmetic  21.7 us (13%)
  matrix products  19.3 us (12%)
  waiting for transfers between devices  12.5 us (8%)
    ppermute x10, starting transfers between devices, partner(): return lax.ppermute(values, axis, [(i, i ^ offset) for i in range(size)])  16.9 us
    slice x9, local copies, waits for them, and re-layouts, part(): return tuple((piece[lo:hi] for piece in (below, above, left, right)))  10.9 us
    ppermute x10, waiting for transfers between devices, partner(): return lax.ppermute(values, axis, [(i, i ^ offset) for i in range(size)])  10 us
    unnamed x96, local copies, waits for them, and re-layouts  9.43 us
    slice x12, local copies, waits for them, and re-layouts, lon_roll(): jnp.roll(values[..., -1:], 1, axis=0)  7.38 us
    all_to_all x1, starting transfers between devices, on_device(): lax.all_to_all(chunks.transpose(2, 0, 1, 3), 'lon', split_axis=0, concat_...  6.95 us
    ppermute x2, starting transfers between devices, edges(): above = lax.ppermute(block[..., :1, :], 'lat', ring('lat', -1))  6.72 us
    slice x2, local copies, waits for them, and re-layouts, edges(): right = lax.ppermute(block[..., :, :1], 'lon', ring('lon', -1))  6.63 us
  transfers between devices with their start and end apart: 20, of which 3 were waited for; matrix products, arithmetic and copies ran while one was open for 52% of the time, Pallas kernels for 0%

profile of v3, /device:TPU:1, one launch (start us, length us, event | category | flops | bytes accessed | tf_op | source)
XLA Modules:
  0.0 162.7 jit_solution(3668996313581596145)
XLA Ops:
  6.0 2.4 %copy.169 = f32[40,6,16,128]{3,0,1,2:T(8,128)} copy(f32[40,6,16,128]{3,2,1,0:T(8,128)S(1)} %bitcast.76) | data formatting | bytes 3932160 | tf_op jit(solution)/shard_map/reshape | solution.py:168
  8.4 6.9 %all-to-all-start = ((f32[16,40,6,128]{3,1,2,0:T(8,128)}), f32[16,40,6,128]{3,1,2,0:T(8,128)S(1)}, u32[]{:S(2)}, u32[]{:S(2)}) async-start(f32[16,40,6,128]{3,1,2,0:T(8,128)} %bitcast.75), calls=%async_computation | async-start | bytes 3932160 | tf_op jit(solution)/shard_map/all_to_all | solution.py:169
  18.2 2.6 %collective-permute-start = (f32[32,1,128]{2,1,0:T(1,128)}, f32[32,1,128]{2,1,0:T(1,128)}, u32[]{:S(2)}, u32[]{:S(2)}) collective-permute-start(f32[32,1,128]{2,1,0:T(1,128)} %get-tuple-element.64), channel_id=1, source_target_pairs={{0,16},{16,32},{32,48},{48,64},{64,80},{80,96},{96,112},{112,0},{1... | collective-permute-start | bytes 49160 | tf_op jit(solution)/shard_map/ppermute | solution.py:19
  20.8 3.5 %collective-permute-start.1 = (f32[32,1,128]{2,1,0:T(1,128)}, f32[32,1,128]{2,1,0:T(1,128)}, u32[]{:S(2)}, u32[]{:S(2)}) collective-permute-start(f32[32,1,128]{2,1,0:T(1,128)} %get-tuple-element.63), channel_id=1, source_target_pairs={{0,112},{16,0},{32,16},{48,32},{64,48},{80,64},{96,80},{112,96},{1... | collective-permute-start | bytes 49160 | tf_op jit(solution)/shard_map/ppermute | solution.py:20
  24.3 4.1 %fusion.78 = (f32[32,96,1]{2,1,0:T(8,128)}, f32[32,96,1]{2,1,0:T(8,128)}) fusion(f32[32,96,128]{2,1,0:T(8,128)} %bitcast_dynamic-update-slice_fusion), kind=kLoop, calls=%fused_computation.113 | loop fusion | bytes 49152 | tf_op jit(solution)/shard_map/slice | solution.py:22
  28.4 2.5 %copy.121 = f32[32,96,1]{1,0,2:T(8,128)} copy(f32[32,96,1]{2,1,0:T(8,128)} %get-tuple-element.62) | data formatting | bytes 24576 | tf_op jit(solution)/shard_map/slice | solution.py:21
  32.2 2.5 %copy.122 = f32[32,96,1]{1,0,2:T(8,128)} copy(f32[32,96,1]{2,1,0:T(8,128)} %get-tuple-element.61) | data formatting | bytes 24576 | tf_op jit(solution)/shard_map/slice | solution.py:22
  47.5 2.7 %convolution_bitcast_fusion.1 = f32[16,96,6,128]{3,1,2,0:T(8,128)S(1)} fusion(f32[20,96,1,1]{1,0,2,3:T(8,128)} %reshape.78, f32[16,40,6,128]{3,1,2,0:T(8,128)S(1)} %all-to-all-done), kind=kOutput, calls=%fused_computation.10 | convolution fusion | flops 141557760 | bytes 5905920 | tf_op jit(solution)/shard_map/oc,soml->scml/dot_general | solution.py:92
  56.9 4.0 %fusion.9 = (f32[16,32,6,128]{3,1,2,0:T(8,128)S(1)}, f32[16,32,6,128]{3,1,2,0:T(8,128)S(1)}) fusion(f32[16,96,6,128]{3,1,2,0:T(8,128)S(1)} %convolution_bitcast_fusion.1, f32[1,32,6,1]{3,1,2,0:T(8,128)S(1)} %get-tuple-element.42, f32[15,32,6,1]{3,1,2,0:T(8,128)S(1)} %get-tuple-element.44, f32[16,32,6,127]{3,1,2,0:T(8,128)S(1)} %get-tuple-element.46, ...), kind=kOutput, calls=%fused_computation.19 | convolution fusion | flops 237109248 | bytes 12595200 | tf_op jit(solution)/shard_map/oc,scml->soml/dot_general | solution.py:80
  62.1 2.3 %fusion.19 = f32[32,96]{1,0:T(8,128)S(1)} fusion(f32[16,32,6,128]{3,1,2,0:T(8,128)S(1)} %get-tuple-element.116, f32[1,32,6,1]{3,1,2,0:T(8,128)S(1)} %get-tuple-element.72, f32[15,32,6,1]{3,1,2,0:T(8,128)S(1)} %get-tuple-element.74, f32[16,32,6,127]{3,1,2,0:T(8,128)S(1)} %get-tuple-element.76, f32[16,32,6,128]{3,1,2,0:T(8,128)S(1)} %tanh_bitcast_fusion.1, ...), kind=kOutput, calls=%fused_computation.28 | convolution fusion | flops 233570304 | bytes 6303744 | tf_op jit(solution)/shard_map/soml,scml->oc/dot_general | solution.py:94
  66.6 2.6 %fusion.66 = (f32[15,32,6,1]{3,1,2,0:T(8,128)}, f32[15,32,6,1]{3,1,2,0:T(8,128)}) fusion(f32[16,96,6,128]{3,1,2,0:T(8,128)S(1)} %convolution_bitcast_fusion), kind=kLoop, calls=%fused_computation.101 | loop fusion | bytes 46080 | tf_op jit(solution)/shard_map/jit(_roll_static)/slice | solution.py:52
  71.8 2.4 %fusion.24 = f32[20,96]{1,0:T(8,128)S(1)} fusion(f32[16,20,6,128]{3,1,2,0:T(8,128)S(1)} %get-tuple-element.53, f32[1,32,6,1]{3,1,2,0:T(8,128)S(1)} %get-tuple-element.66, f32[15,32,6,1]{3,1,2,0:T(8,128)S(1)} %get-tuple-element.68, f32[16,32,6,127]{3,1,2,0:T(8,128)S(1)} %get-tuple-element.70, f32[16,32,6,128]{3,1,2,0:T(8,128)S(1)} %get-tuple-element.117, ...), kind=kOutput, calls=%fused_computation.29 | convolution fusion | flops 148635648 | bytes 5709312 | tf_op jit(solution)/shard_map/soml,scml->oc/dot_general | solution.py:91
  74.5 4.5 %fusion.7 = f32[16,32,6,128]{3,1,2,0:T(8,128)S(1)} fusion(f32[16,96,6,128]{3,1,2,0:T(8,128)} %copy-done, f32[1,32,6,1]{3,1,2,0:T(8,128)S(1)} %get-tuple-element.36, f32[15,32,6,1]{3,1,2,0:T(8,128)} %get-tuple-element.38, f32[16,32,6,127]{3,1,2,0:T(8,128)} %get-tuple-element.40, f32[16,32,6,127]{3,1,2,0:T(8,128)} %get-tuple-element.39, ...), kind=kLoop, calls=%fused_computation.16 | loop fusion | flops 3538944 | bytes 7864320 | tf_op jit(solution)/shard_map/mul | solution.py:96
  84.4 3.1 %convolution_bitcast_fusion.2 = f32[16,60,6,128]{3,1,2,0:T(8,128)S(1)} fusion(f32[16,32,6,128]{3,1,2,0:T(8,128)} %copy-done.6, f32[32,60]{0,1:T(8,128)S(1)} %copy-done.38), kind=kOutput, calls=%fused_computation.13 | convolution fusion | flops 141557760 | bytes 4529664 | tf_op jit(solution)/shard_map/oc,soml->scml/dot_general | solution.py:98
  92.2 2.3 %collective-permute-start.8 = (f32[54,128]{1,0:T(8,128)}, f32[54,128]{1,0:T(8,128)}, u32[]{:S(2)}, u32[]{:S(2)}) collective-permute-start(f32[54,128]{1,0:T(8,128)} %maximum_bitcast_fusion), channel_id=1, source_target_pairs={{0,16},{16,0},{32,48},{48,32},{64,80},{80,64},{96,112},{112,96},{1... | collective-permute-start | bytes 82952 | tf_op jit(solution)/shard_map/ppermute | solution.py:113
  107.2 4.0 %fusion.12 = f32[16,20,6,128]{3,1,2,0:T(8,128)} fusion(f32[16,60,6,128]{3,1,2,0:T(8,128)} %copy-done.4, f32[1,20,6,1]{3,1,2,0:T(8,128)} %get-tuple-element.48, f32[15,20,6,1]{3,1,2,0:T(8,128)} %get-tuple-element.50, f32[16,20,6,127]{3,1,2,0:T(8,128)S(1)} %get-tuple-element.52, f32[16,20,6,127]{3,1,2,0:T(8,128)S(1)} %get-tuple-element.51, ...), kind=kLoop, calls=%fused_computation.25 | loop fusion | flops 1474560 | bytes 3932160 | tf_op jit(solution)/shard_map/add | solution.py:66
  115.1 2.3 %collective-permute-start.11 = (f32[54,128]{1,0:T(8,128)S(1)}, f32[54,128]{1,0:T(8,128)S(1)}, u32[]{:S(2)}, u32[]{:S(2)}) collective-permute-start(f32[54,128]{1,0:T(8,128)S(1)} %add_add_fusion.2), channel_id=1, source_target_pairs={{0,64},{16,80},{32,96},{48,112},{64,0},{80,16},{96,32},{112,48},{1... | collective-permute-start | bytes 82952 | tf_op jit(solution)/shard_map/ppermute | solution.py:113
  121.2 4.8 %collective-permute-start.14 = (f32[54,128]{1,0:T(8,128)S(1)}, f32[54,128]{1,0:T(8,128)S(1)}, u32[]{:S(2)}, u32[]{:S(2)}) collective-permute-start(f32[54,128]{1,0:T(8,128)S(1)} %add.113), channel_id=1, source_target_pairs={{0,3},{1,2},{2,1},{3,0},{4,7},{5,6},{6,5},{7,4},{8,11},{9,10},{10,... | collective-permute-start | bytes 82952 | tf_op jit(solution)/shard_map/ppermute | solution.py:113
  127.0 4.0 %all-to-all-start.1 = ((f32[16,20,6,128]{3,1,2,0:T(8,128)}), f32[16,20,6,128]{3,1,2,0:T(8,128)S(1)}, u32[]{:S(2)}, u32[]{:S(2)}) async-start(f32[16,20,6,128]{3,1,2,0:T(8,128)} %fusion.12), calls=%async_computation.1 | async-start | bytes 2359296 | tf_op jit(solution)/shard_map/all_to_all | solution.py:174
  131.0 3.0 %collective-permute-start.16 = (f32[54,128]{1,0:T(8,128)S(1)}, f32[54,128]{1,0:T(8,128)S(1)}, u32[]{:S(2)}, u32[]{:S(2)}) collective-permute-start(f32[54,128]{1,0:T(8,128)S(1)} %add_add_fusion.1), channel_id=1, source_target_pairs={{0,8},{1,9},{2,10},{3,11},{4,12},{5,13},{6,14},{7,15},{8,0},{9,1},... | collective-permute-start | bytes 82952 | tf_op jit(solution)/shard_map/ppermute | solution.py:113
  139.0 9.1 %collective-permute-done.16 = f32[54,128]{1,0:T(8,128)S(1)} collective-permute-done((f32[54,128]{1,0:T(8,128)S(1)}, f32[54,128]{1,0:T(8,128)S(1)}, u32[]{:S(2)}, u32[]{:S(2)}) %collective-permute-start.16) | collective-permute-done | bytes 27680 | tf_op jit(solution)/shard_map/ppermute | solution.py:113
  148.1 3.2 %collective-permute-start.6 = (f32[10,1,128]{2,1,0:T(1,128)S(1)}, f32[10,1,128]{2,1,0:T(1,128)S(1)}, u32[]{:S(2)}, u32[]{:S(2)}) collective-permute-start(f32[10,1,128]{2,1,0:T(1,128)S(1)} %get-tuple-element.80), channel_id=1, source_target_pairs={{0,112},{16,0},{32,16},{48,32},{64,48},{80,64},{96,80},{112,96},{1... | collective-permute-start | bytes 15368 | tf_op jit(solution)/shard_map/ppermute | solution.py:20
  157.6 2.4 %collective-permute-done.7 = f32[10,1,128]{2,1,0:T(1,128)S(1)} collective-permute-done((f32[10,1,128]{2,1,0:T(1,128)S(1)}, f32[10,1,128]{2,1,0:T(1,128)S(1)}, u32[]{:S(2)}, u32[]{:S(2)}) %collective-permute-start.7) | collective-permute-done | bytes 5152 | tf_op jit(solution)/shard_map/ppermute | solution.py:19
  160.0 2.6 %fusion.53 = f32[10,96,128]{2,1,0:T(8,128)} fusion(f32[10,96,128]{2,1,0:T(8,128)S(1)} %copy-done.1, f32[10,96,128]{2,1,0:T(8,128)S(1)} %copy-done.11, f32[10,96,128]{2,1,0:T(8,128)S(1)} %get-tuple-element.30, f32[10,96,1]{2,1,0:T(8,128)} %collective-permute-done.4, f32[10,96,127]{2,1,0:T(8,128)S(1)} %copy-done.31, f32[10,96,128]{2,1,0:T(8,128)S(1)} %copy-done.10, ...), kind=kLoop, calls=%fused_computation.67 | loop fusion | flops 2088960 | bytes 5898240 | tf_op jit(solution)/shard_map/add | solution.py:193
  (204 shorter events, 77.2 us)
Async XLA Ops:
  8.4 7.0 %copy-start.37 = (f32[96,128]{1,0:T(8,128)S(1)}, f32[96,128]{1,0:T(8,128)}, u32[]{:S(2)}) copy-start(f32[96,128]{1,0:T(8,128)} %param.16) | copy-start | bytes 147460
  8.4 7.6 %copy-start.36 = (f32[96,128]{1,0:T(8,128)S(1)}, f32[96,128]{1,0:T(8,128)}, u32[]{:S(2)}) copy-start(f32[96,128]{1,0:T(8,128)} %param.17) | copy-start | bytes 147460
  8.4 39.1 %all-to-all-start = ((f32[16,40,6,128]{3,1,2,0:T(8,128)}), f32[16,40,6,128]{3,1,2,0:T(8,128)S(1)}, u32[]{:S(2)}, u32[]{:S(2)}) async-start(f32[16,40,6,128]{3,1,2,0:T(8,128)} %bitcast.75), calls=%async_computation | async-start | bytes 3932160 | tf_op jit(solution)/shard_map/all_to_all | solution.py:169
  18.2 64.3 %collective-permute-start = (f32[32,1,128]{2,1,0:T(1,128)}, f32[32,1,128]{2,1,0:T(1,128)}, u32[]{:S(2)}, u32[]{:S(2)}) collective-permute-start(f32[32,1,128]{2,1,0:T(1,128)} %get-tuple-element.64), channel_id=1, source_target_pairs={{0,16},{16,32},{32,48},{48,64},{64,80},{80,96},{96,112},{112,0},{1... | collective-permute-start | bytes 49160 | tf_op jit(solution)/shard_map/ppermute | solution.py:19
  20.8 61.7 %collective-permute-start.1 = (f32[32,1,128]{2,1,0:T(1,128)}, f32[32,1,128]{2,1,0:T(1,128)}, u32[]{:S(2)}, u32[]{:S(2)}) collective-permute-start(f32[32,1,128]{2,1,0:T(1,128)} %get-tuple-element.63), channel_id=1, source_target_pairs={{0,112},{16,0},{32,16},{48,32},{64,48},{80,64},{96,80},{112,96},{1... | collective-permute-start | bytes 49160 | tf_op jit(solution)/shard_map/ppermute | solution.py:20
  30.9 51.6 %collective-permute-start.2 = (f32[32,96,1]{1,0,2:T(8,128)}, f32[32,96,1]{1,0,2:T(8,128)}, u32[]{:S(2)}, u32[]{:S(2)}) collective-permute-start(f32[32,96,1]{1,0,2:T(8,128)} %copy.121), channel_id=1, source_target_pairs={{0,1},{1,2},{2,3},{3,4},{4,5},{5,6},{6,7},{7,8},{8,9},{9,10},{10,1... | collective-permute-start | bytes 36872 | tf_op jit(solution)/shard_map/ppermute | solution.py:21
  34.7 47.8 %collective-permute-start.3 = (f32[32,96,1]{1,0,2:T(8,128)}, f32[32,96,1]{1,0,2:T(8,128)}, u32[]{:S(2)}, u32[]{:S(2)}) collective-permute-start(f32[32,96,1]{1,0,2:T(8,128)} %copy.122), channel_id=1, source_target_pairs={{0,15},{1,0},{2,1},{3,2},{4,3},{5,4},{6,5},{7,6},{8,7},{9,8},{10,9... | collective-permute-start | bytes 36872 | tf_op jit(solution)/shard_map/ppermute | solution.py:22
  74.5 5.7 %copy-start.3 = (f32[16,60,6,128]{3,1,2,0:T(8,128)S(1)}, f32[16,60,6,128]{3,1,2,0:T(8,128)}, u32[]{:S(2)}) copy-start(f32[16,60,6,128]{3,1,2,0:T(8,128)} %copy-done.2) | copy-start | bytes 8847364
  90.3 23.9 %collective-permute-start.9 = (f32[54,128]{1,0:T(8,128)}, f32[54,128]{1,0:T(8,128)}, u32[]{:S(2)}, u32[]{:S(2)}) collective-permute-start(f32[54,128]{1,0:T(8,128)} %maximum_bitcast_fusion), channel_id=1, source_target_pairs={{0,32},{16,48},{32,0},{48,16},{64,96},{80,112},{96,64},{112,80},{1... | collective-permute-start | bytes 82952 | tf_op jit(solution)/shard_map/ppermute | solution.py:113
  90.7 23.6 %collective-permute-start.10 = (f32[54,128]{1,0:T(8,128)}, f32[54,128]{1,0:T(8,128)}, u32[]{:S(2)}, u32[]{:S(2)}) collective-permute-start(f32[54,128]{1,0:T(8,128)} %maximum_bitcast_fusion), channel_id=1, source_target_pairs={{0,48},{16,32},{32,16},{48,0},{64,112},{80,96},{96,80},{112,64},{1... | collective-permute-start | bytes 82952 | tf_op jit(solution)/shard_map/ppermute | solution.py:113
  92.2 22.0 %collective-permute-start.8 = (f32[54,128]{1,0:T(8,128)}, f32[54,128]{1,0:T(8,128)}, u32[]{:S(2)}, u32[]{:S(2)}) collective-permute-start(f32[54,128]{1,0:T(8,128)} %maximum_bitcast_fusion), channel_id=1, source_target_pairs={{0,16},{16,0},{32,48},{48,32},{64,80},{80,64},{96,112},{112,96},{1... | collective-permute-start | bytes 82952 | tf_op jit(solution)/shard_map/ppermute | solution.py:113
  115.1 4.3 %collective-permute-start.11 = (f32[54,128]{1,0:T(8,128)S(1)}, f32[54,128]{1,0:T(8,128)S(1)}, u32[]{:S(2)}, u32[]{:S(2)}) collective-permute-start(f32[54,128]{1,0:T(8,128)S(1)} %add_add_fusion.2), channel_id=1, source_target_pairs={{0,64},{16,80},{32,96},{48,112},{64,0},{80,16},{96,32},{112,48},{1... | collective-permute-start | bytes 82952 | tf_op jit(solution)/shard_map/ppermute | solution.py:113
  119.4 11.6 %collective-permute-start.13 = (f32[54,128]{1,0:T(8,128)S(1)}, f32[54,128]{1,0:T(8,128)S(1)}, u32[]{:S(2)}, u32[]{:S(2)}) collective-permute-start(f32[54,128]{1,0:T(8,128)S(1)} %add.113), channel_id=1, source_target_pairs={{0,2},{1,3},{2,0},{3,1},{4,6},{5,7},{6,4},{7,5},{8,10},{9,11},{10,... | collective-permute-start | bytes 82952 | tf_op jit(solution)/shard_map/ppermute | solution.py:113
  121.2 9.8 %collective-permute-start.14 = (f32[54,128]{1,0:T(8,128)S(1)}, f32[54,128]{1,0:T(8,128)S(1)}, u32[]{:S(2)}, u32[]{:S(2)}) collective-permute-start(f32[54,128]{1,0:T(8,128)S(1)} %add.113), channel_id=1, source_target_pairs={{0,3},{1,2},{2,1},{3,0},{4,7},{5,6},{6,5},{7,4},{8,11},{9,10},{10,... | collective-permute-start | bytes 82952 | tf_op jit(solution)/shard_map/ppermute | solution.py:113
  125.9 5.1 %collective-permute-start.12 = (f32[54,128]{1,0:T(8,128)S(1)}, f32[54,128]{1,0:T(8,128)S(1)}, u32[]{:S(2)}, u32[]{:S(2)}) collective-permute-start(f32[54,128]{1,0:T(8,128)S(1)} %add.113), channel_id=1, source_target_pairs={{0,1},{1,0},{2,3},{3,2},{4,5},{5,4},{6,7},{7,6},{8,9},{9,8},{10,11... | collective-permute-start | bytes 82952 | tf_op jit(solution)/shard_map/ppermute | solution.py:113
  127.0 26.6 %all-to-all-start.1 = ((f32[16,20,6,128]{3,1,2,0:T(8,128)}), f32[16,20,6,128]{3,1,2,0:T(8,128)S(1)}, u32[]{:S(2)}, u32[]{:S(2)}) async-start(f32[16,20,6,128]{3,1,2,0:T(8,128)} %fusion.12), calls=%async_computation.1 | async-start | bytes 2359296 | tf_op jit(solution)/shard_map/all_to_all | solution.py:174
  131.0 17.1 %collective-permute-start.16 = (f32[54,128]{1,0:T(8,128)S(1)}, f32[54,128]{1,0:T(8,128)S(1)}, u32[]{:S(2)}, u32[]{:S(2)}) collective-permute-start(f32[54,128]{1,0:T(8,128)S(1)} %add_add_fusion.1), channel_id=1, source_target_pairs={{0,8},{1,9},{2,10},{3,11},{4,12},{5,13},{6,14},{7,15},{8,0},{9,1},... | collective-permute-start | bytes 82952 | tf_op jit(solution)/shard_map/ppermute | solution.py:113
  134.0 17.3 %collective-permute-start.17 = (f32[54,128]{1,0:T(8,128)S(1)}, f32[54,128]{1,0:T(8,128)S(1)}, u32[]{:S(2)}, u32[]{:S(2)}) collective-permute-start(f32[54,128]{1,0:T(8,128)S(1)} %add_add_fusion.1), channel_id=1, source_target_pairs={{0,12},{1,13},{2,14},{3,15},{4,8},{5,9},{6,10},{7,11},{8,4},{9,5},... | collective-permute-start | bytes 82952 | tf_op jit(solution)/shard_map/ppermute | solution.py:113
  134.9 16.5 %collective-permute-start.15 = (f32[54,128]{1,0:T(8,128)S(1)}, f32[54,128]{1,0:T(8,128)S(1)}, u32[]{:S(2)}, u32[]{:S(2)}) collective-permute-start(f32[54,128]{1,0:T(8,128)S(1)} %add_add_fusion.1), channel_id=1, source_target_pairs={{0,4},{1,5},{2,6},{3,7},{4,0},{5,1},{6,2},{7,3},{8,12},{9,13},{10,... | collective-permute-start | bytes 82952 | tf_op jit(solution)/shard_map/ppermute | solution.py:113
  136.9 20.6 %collective-permute-start.4 = (f32[10,96,1]{2,1,0:T(8,128)}, f32[10,96,1]{2,1,0:T(8,128)}, u32[]{:S(2)}, u32[]{:S(2)}) collective-permute-start(f32[10,96,1]{2,1,0:T(8,128)} %get-tuple-element.84), channel_id=1, source_target_pairs={{0,15},{1,0},{2,1},{3,2},{4,3},{5,4},{6,5},{7,6},{8,7},{9,8},{10,9... | collective-permute-start | bytes 11528 | tf_op jit(solution)/shard_map/ppermute | solution.py:22
  137.9 19.7 %collective-permute-start.5 = (f32[10,96,1]{2,1,0:T(8,128)}, f32[10,96,1]{2,1,0:T(8,128)}, u32[]{:S(2)}, u32[]{:S(2)}) collective-permute-start(f32[10,96,1]{2,1,0:T(8,128)} %get-tuple-element.83), channel_id=1, source_target_pairs={{0,1},{1,2},{2,3},{3,4},{4,5},{5,6},{6,7},{7,8},{8,9},{9,10},{10,1... | collective-permute-start | bytes 11528 | tf_op jit(solution)/shard_map/ppermute | solution.py:21
  148.1 9.5 %collective-permute-start.6 = (f32[10,1,128]{2,1,0:T(1,128)S(1)}, f32[10,1,128]{2,1,0:T(1,128)S(1)}, u32[]{:S(2)}, u32[]{:S(2)}) collective-permute-start(f32[10,1,128]{2,1,0:T(1,128)S(1)} %get-tuple-element.80), channel_id=1, source_target_pairs={{0,112},{16,0},{32,16},{48,32},{64,48},{80,64},{96,80},{112,96},{1... | collective-permute-start | bytes 15368 | tf_op jit(solution)/shard_map/ppermute | solution.py:20
  151.3 8.7 %collective-permute-start.7 = (f32[10,1,128]{2,1,0:T(1,128)S(1)}, f32[10,1,128]{2,1,0:T(1,128)S(1)}, u32[]{:S(2)}, u32[]{:S(2)}) collective-permute-start(f32[10,1,128]{2,1,0:T(1,128)S(1)} %get-tuple-element.79), channel_id=1, source_target_pairs={{0,16},{16,32},{32,48},{48,64},{64,80},{80,96},{96,112},{112,0},{1... | collective-permute-start | bytes 15368 | tf_op jit(solution)/shard_map/ppermute | solution.py:19
  155.8 4.2 %copy-start.33 = (f32[10,95,128]{2,1,0:T(8,128)S(1)}, f32[10,95,128]{2,1,0:T(8,128)}, u32[]{:S(2)}) copy-start(f32[10,95,128]{2,1,0:T(8,128)} %get-tuple-element.82) | copy-start | bytes 1459204
  (42 other events, 126.9 us)

commit v4 on v0

--- a/solution.py
+++ b/solution.py
@@ -95,24 +95,31 @@
     back = jnp.einsum("oc,soml->scml", flats[1], second_delta, precision=highest)
     first_delta = unstack_taps(back, first.shape[1]) * (1.0 - first * first)
     first_grad = jnp.einsum("soml,scml->oc", first_delta, in_stack, precision=highest)
-    back = jnp.einsum("oc,soml->scml", flats[0], first_delta, precision=highest)
-    input_grad = unstack_taps(back, values.shape[1])
     grads = (kernel_of(first_grad, taps), kernel_of(middle_grad, taps), kernel_of(last_grad, taps))
-    return grads, input_grad
+    return grads, first_delta
+
+
+def input_pullback(weights, first_delta, channels):
+    back = jnp.einsum("oc,soml->scml", flat_kernel(weights[0]), first_delta, precision=highest)
+    return unstack_taps(back, channels)
 
 
 LANES = 128
 
 
-def butterfly_sum(values, axes):
+def butterfly_sum(values, axes, tie):
+    first = True
     for axis in axes:
         size = lax.axis_size(axis)
         stride = 1
         while stride < size:
             pairs = [(i, i ^ stride) for i in range(size)]
             values = values + lax.ppermute(values, axis, pairs)
+            if first:
+                values, tie = lax.optimization_barrier((values, tie))
+                first = False
             stride *= 2
-    return values
+    return values, tie
 
 
 def pack(parts):
@@ -161,10 +168,12 @@
     blocks = lax.axis_size("lon")
     chunks = stacked.reshape(stacked.shape[0], tile_rows // blocks, blocks, tile_cols)
     band = lax.all_to_all(chunks.transpose(2, 0, 1, 3), "lon", split_axis=0, concat_axis=0, tiled=True)
-    weight_grads, band_grad = network_vjp(weights, band[:, : 2 * levels], band[:, 2 * levels :])
+    weight_grads, first_delta = network_vjp(weights, band[:, : 2 * levels], band[:, 2 * levels :])
     packed = pack(weight_grads)
     packed, plane_halo = lax.optimization_barrier((packed, plane_halo))
-    summed = unpack(butterfly_sum(packed, ("lon", "lat")), weight_grads)
+    total, first_delta = butterfly_sum(packed, ("lon", "lat"), first_delta)
+    summed = unpack(total, weight_grads)
+    band_grad = input_pullback(weights, first_delta, 2 * levels)
     returned = lax.all_to_all(band_grad, "lon", split_axis=0, concat_axis=0, tiled=True)
     input_grad = returned.transpose(1, 2, 0, 3).reshape(2 * levels, tile_rows, tile_cols)
     below, above, left, right = plane_halo

time: 155 us -> 153 us (0.987)
  matrix products: 20.9 us -> 17.5 us
  waiting for transfers between devices: 15 us -> 17.1 us
  local copies, waits for them, and re-layouts: 60.6 us -> 58.7 us
    dot_general x1, matrix products: 4.68 us -> 1.38 us  [input_pullback(): jnp.einsum('oc,soml->scml', flat_kernel(weights[0]), first_delta, precisi...]
    ppermute x7, waiting for transfers between devices: 4.58 us -> 6.66 us  [butterfly_sum(): values = values + lax.ppermute(values, axis, pairs)]
    slice x6, local copies, waits for them, and re-layouts: 6.5 us -> 4.71 us  [lon_roll(): values[..., :-1]]
    unnamed x78 -> x62, local copies, waits for them, and re-layouts: 9.4 us -> 9.37 us
  transfers between devices with their start and end apart: 17 -> 17, of which waited for: 8 -> 8; matrix products, arithmetic and copies ran while one was open for 47% -> 48% of each run, Pallas kernels for 0% -> 0%
where the time goes in v4:
time: 153 us; the launch traced here: 152 us
  local copies, waits for them, and re-layouts  58.7 us (38%)
  starting transfers between devices  38 us (25%)
  other arithmetic  19.1 us (12%)
  matrix products  17.5 us (11%)
  waiting for transfers between devices  17.1 us (11%)
    ppermute x7, starting transfers between devices, butterfly_sum(): values = values + lax.ppermute(values, axis, pairs)  10.6 us
    unnamed x62, local copies, waits for them, and re-layouts  9.37 us
    all_to_all x1, starting transfers between devices, on_device(): lax.all_to_all(band_grad, 'lon', split_axis=0, concat_axis=0, tiled=True)  7.02 us
    all_to_all x1, starting transfers between devices, on_device(): lax.all_to_all(chunks.transpose(2, 0, 1, 3), 'lon', split_axis=0, concat_...  6.95 us
    slice x9, local copies, waits for them, and re-layouts, part(): return tuple((piece[lo:hi] for piece in (below, above, left, right)))  6.86 us
    ppermute x2, waiting for transfers between devices, edges(): right = lax.ppermute(block[..., :, :1], 'lon', ring('lon', -1))  6.7 us
    slice x2, local copies, waits for them, and re-layouts, edges(): right = lax.ppermute(block[..., :, :1], 'lon', ring('lon', -1))  6.68 us
    ppermute x7, waiting for transfers between devices, butterfly_sum(): values = values + lax.ppermute(values, axis, pairs)  6.66 us
  transfers between devices with their start and end apart: 17, of which 8 were waited for; matrix products, arithmetic and copies ran while one was open for 48% of the time, Pallas kernels for 0%

profile of v4, /device:TPU:1, one launch (start us, length us, event | category | flops | bytes accessed | tf_op | source)
XLA Modules:
  0.0 151.6 jit_solution(3409780356665606869)
XLA Ops:
  6.0 2.4 %copy.169 = f32[40,6,16,128]{3,0,1,2:T(8,128)} copy(f32[40,6,16,128]{3,2,1,0:T(8,128)S(1)} %bitcast.76) | data formatting | bytes 3932160 | tf_op jit(solution)/shard_map/reshape | solution.py:169
  8.4 6.9 %all-to-all-start = ((f32[16,40,6,128]{3,1,2,0:T(8,128)}), f32[16,40,6,128]{3,1,2,0:T(8,128)S(1)}, u32[]{:S(2)}, u32[]{:S(2)}) async-start(f32[16,40,6,128]{3,1,2,0:T(8,128)} %bitcast.75), calls=%async_computation | async-start | bytes 3932160 | tf_op jit(solution)/shard_map/all_to_all | solution.py:170
  18.2 2.6 %collective-permute-start = (f32[32,1,128]{2,1,0:T(1,128)}, f32[32,1,128]{2,1,0:T(1,128)}, u32[]{:S(2)}, u32[]{:S(2)}) collective-permute-start(f32[32,1,128]{2,1,0:T(1,128)} %get-tuple-element.68), channel_id=1, source_target_pairs={{0,16},{16,32},{32,48},{48,64},{64,80},{80,96},{96,112},{112,0},{1... | collective-permute-start | bytes 49160 | tf_op jit(solution)/shard_map/ppermute | solution.py:19
  20.8 3.5 %collective-permute-start.1 = (f32[32,1,128]{2,1,0:T(1,128)}, f32[32,1,128]{2,1,0:T(1,128)}, u32[]{:S(2)}, u32[]{:S(2)}) collective-permute-start(f32[32,1,128]{2,1,0:T(1,128)} %get-tuple-element.67), channel_id=1, source_target_pairs={{0,112},{16,0},{32,16},{48,32},{64,48},{80,64},{96,80},{112,96},{1... | collective-permute-start | bytes 49160 | tf_op jit(solution)/shard_map/ppermute | solution.py:20
  24.3 4.2 %fusion.78 = (f32[32,96,1]{2,1,0:T(8,128)}, f32[32,96,1]{2,1,0:T(8,128)}) fusion(f32[32,96,128]{2,1,0:T(8,128)} %bitcast_dynamic-update-slice_fusion), kind=kLoop, calls=%fused_computation.110 | loop fusion | bytes 49152 | tf_op jit(solution)/shard_map/slice | solution.py:22
  28.5 2.5 %copy.121 = f32[32,96,1]{1,0,2:T(8,128)} copy(f32[32,96,1]{2,1,0:T(8,128)} %get-tuple-element.66) | data formatting | bytes 24576 | tf_op jit(solution)/shard_map/slice | solution.py:21
  32.3 2.5 %copy.122 = f32[32,96,1]{1,0,2:T(8,128)} copy(f32[32,96,1]{2,1,0:T(8,128)} %get-tuple-element.65) | data formatting | bytes 24576 | tf_op jit(solution)/shard_map/slice | solution.py:22
  47.5 2.7 %convolution_bitcast_fusion.1 = f32[16,96,6,128]{3,1,2,0:T(8,128)S(1)} fusion(f32[20,96,1,1]{1,0,2,3:T(8,128)} %reshape.79, f32[16,40,6,128]{3,1,2,0:T(8,128)S(1)} %all-to-all-done), kind=kOutput, calls=%fused_computation.10 | convolution fusion | flops 141557760 | bytes 5905920 | tf_op jit(solution)/shard_map/oc,soml->scml/dot_general | solution.py:92
  56.9 4.0 %fusion.9 = (f32[16,32,6,128]{3,1,2,0:T(8,128)S(1)}, f32[16,32,6,128]{3,1,2,0:T(8,128)S(1)}) fusion(f32[16,96,6,128]{3,1,2,0:T(8,128)S(1)} %convolution_bitcast_fusion.1, f32[1,32,6,1]{3,1,2,0:T(8,128)S(1)} %get-tuple-element.46, f32[15,32,6,1]{3,1,2,0:T(8,128)S(1)} %get-tuple-element.48, f32[16,32,6,127]{3,1,2,0:T(8,128)S(1)} %get-tuple-element.50, ...), kind=kOutput, calls=%fused_computation.19 | convolution fusion | flops 237109248 | bytes 12595200 | tf_op jit(solution)/shard_map/oc,scml->soml/dot_general | solution.py:80
  62.1 2.3 %fusion.19 = f32[32,96]{1,0:T(8,128)S(1)} fusion(f32[16,32,6,128]{3,1,2,0:T(8,128)S(1)} %get-tuple-element.120, f32[1,32,6,1]{3,1,2,0:T(8,128)S(1)} %get-tuple-element.76, f32[15,32,6,1]{3,1,2,0:T(8,128)S(1)} %get-tuple-element.78, f32[16,32,6,127]{3,1,2,0:T(8,128)S(1)} %get-tuple-element.80, f32[16,32,6,128]{3,1,2,0:T(8,128)S(1)} %tanh_bitcast_fusion.1, ...), kind=kOutput, calls=%fused_computation.28 | convolution fusion | flops 233570304 | bytes 6303744 | tf_op jit(solution)/shard_map/soml,scml->oc/dot_general | solution.py:94
  64.5 2.0 %convolution_bitcast_fusion = f32[16,96,6,128]{3,1,2,0:T(8,128)S(1)} fusion(f32[16,32,6,128]{3,1,2,0:T(8,128)S(1)} %get-tuple-element.120, f32[32,96,1,1]{1,0,2,3:T(8,128)S(1)} %reshape.81), kind=kOutput, calls=%fused_computation.9 | convolution fusion | flops 226492416 | bytes 6303744 | tf_op jit(solution)/shard_map/oc,soml->scml/dot_general | solution.py:95
  66.6 2.6 %fusion.66 = (f32[15,32,6,1]{3,1,2,0:T(8,128)}, f32[15,32,6,1]{3,1,2,0:T(8,128)}) fusion(f32[16,96,6,128]{3,1,2,0:T(8,128)S(1)} %convolution_bitcast_fusion), kind=kLoop, calls=%fused_computation.98 | loop fusion | bytes 46080 | tf_op jit(solution)/shard_map/jit(_roll_static)/slice | solution.py:52
  69.6 2.2 %fusion.67 = (f32[16,32,6,127]{3,1,2,0:T(8,128)}, f32[16,32,6,127]{3,1,2,0:T(8,128)}) fusion(f32[16,96,6,128]{3,1,2,0:T(8,128)S(1)} %convolution_bitcast_fusion), kind=kLoop, calls=%fused_computation.99 | loop fusion | bytes 6242304 | tf_op jit(solution)/shard_map/slice | solution.py:52
  71.8 2.4 %fusion.24 = f32[20,96]{1,0:T(8,128)S(1)} fusion(f32[16,20,6,128]{3,1,2,0:T(8,128)S(1)} %get-tuple-element.57, f32[1,32,6,1]{3,1,2,0:T(8,128)S(1)} %get-tuple-element.70, f32[15,32,6,1]{3,1,2,0:T(8,128)S(1)} %get-tuple-element.72, f32[16,32,6,127]{3,1,2,0:T(8,128)S(1)} %get-tuple-element.74, f32[16,32,6,128]{3,1,2,0:T(8,128)S(1)} %get-tuple-element.121, ...), kind=kOutput, calls=%fused_computation.29 | convolution fusion | flops 148635648 | bytes 5709312 | tf_op jit(solution)/shard_map/soml,scml->oc/dot_general | solution.py:91
  74.5 4.5 %fusion.7 = f32[16,32,6,128]{3,1,2,0:T(8,128)S(1)} fusion(f32[16,96,6,128]{3,1,2,0:T(8,128)} %copy-done, f32[1,32,6,1]{3,1,2,0:T(8,128)S(1)} %get-tuple-element.40, f32[15,32,6,1]{3,1,2,0:T(8,128)} %get-tuple-element.42, f32[16,32,6,127]{3,1,2,0:T(8,128)} %get-tuple-element.44, f32[16,32,6,127]{3,1,2,0:T(8,128)} %get-tuple-element.43, ...), kind=kLoop, calls=%fused_computation.16 | loop fusion | flops 3538944 | bytes 7864320 | tf_op jit(solution)/shard_map/mul | solution.py:96
  88.3 2.9 %collective-permute-start.4 = (f32[54,128]{1,0:T(8,128)S(1)}, f32[54,128]{1,0:T(8,128)S(1)}, u32[]{:S(2)}, u32[]{:S(2)}) collective-permute-start(f32[54,128]{1,0:T(8,128)S(1)} %maximum_bitcast_fusion), channel_id=1, source_target_pairs={{0,1},{1,0},{2,3},{3,2},{4,5},{5,4},{6,7},{7,6},{8,9},{9,8},{10,11... | collective-permute-start | bytes 82952 | tf_op jit(solution)/shard_map/ppermute | solution.py:117
  91.4 4.3 %fusion.44 = (f32[10,96,128]{2,1,0:T(8,128)S(1)}, f32[10,96,128]{2,1,0:T(8,128)S(1)}, f32[10,96,128]{2,1,0:T(8,128)}, f32[10,96,128]{2,1,0:T(8,128)}, f32[10,96,128]{2,1,0:T(8,128)}) fusion(f32[10,96,128]{2,1,0:T(8,128)S(1)} %copy-done.1, f32[10,96,1]{2,1,0:T(8,128)} %copy.130, f32[10,96,127]{2,1,0:T(8,128)} %get-tuple-element.127, ...), kind=kLoop, calls=%fused_computation.54 | loop fusion | flops 3563520 | bytes 7618560 | tf_op jit(solution)/shard_map/mul | solution.py:192
  99.8 2.3 %collective-permute-done.9 = f32[54,128]{1,0:T(8,128)S(1)} collective-permute-done((f32[54,128]{1,0:T(8,128)S(1)}, f32[54,128]{1,0:T(8,128)S(1)}, u32[]{:S(2)}, u32[]{:S(2)}) %collective-permute-start.9) | collective-permute-done | bytes 27680 | tf_op jit(solution)/shard_map/ppermute | solution.py:117
  106.9 2.2 %collective-permute-done.11 = f32[54,128]{1,0:T(8,128)S(1)} collective-permute-done((f32[54,128]{1,0:T(8,128)S(1)}, f32[54,128]{1,0:T(8,128)S(1)}, u32[]{:S(2)}, u32[]{:S(2)}) %collective-permute-start.11) | collective-permute-done | bytes 27680 | tf_op jit(solution)/shard_map/ppermute | solution.py:117
  110.8 7.0 %all-to-all-start.1 = ((f32[16,20,6,128]{3,1,2,0:T(8,128)}), f32[16,20,6,128]{3,1,2,0:T(8,128)S(1)}, u32[]{:S(2)}, u32[]{:S(2)}) async-start(f32[16,20,6,128]{3,1,2,0:T(8,128)} %fusion.12), calls=%async_computation.1 | async-start | bytes 2359296 | tf_op jit(solution)/shard_map/all_to_all | solution.py:177
  120.8 3.4 %collective-permute-start.14 = (f32[54,128]{1,0:T(8,128)S(1)}, f32[54,128]{1,0:T(8,128)S(1)}, u32[]{:S(2)}, u32[]{:S(2)}) collective-permute-start(f32[54,128]{1,0:T(8,128)S(1)} %add.106), channel_id=1, source_target_pairs={{0,64},{16,80},{32,96},{48,112},{64,0},{80,16},{96,32},{112,48},{1... | collective-permute-start | bytes 82952 | tf_op jit(solution)/shard_map/ppermute | solution.py:117
  138.8 6.7 %collective-permute-done.5 = f32[10,96,1]{2,1,0:T(8,128)} collective-permute-done((f32[10,96,1]{2,1,0:T(8,128)}, f32[10,96,1]{2,1,0:T(8,128)}, u32[]{:S(2)}, u32[]{:S(2)}) %collective-permute-start.5) | collective-permute-done | bytes 3872 | tf_op jit(solution)/shard_map/ppermute | solution.py:22
  145.5 2.1 %collective-permute-done.7 = f32[10,1,128]{2,1,0:T(1,128)S(1)} collective-permute-done((f32[10,1,128]{2,1,0:T(1,128)S(1)}, f32[10,1,128]{2,1,0:T(1,128)S(1)}, u32[]{:S(2)}, u32[]{:S(2)}) %collective-permute-start.7) | collective-permute-done | bytes 5152 | tf_op jit(solution)/shard_map/ppermute | solution.py:20
  148.9 2.6 %fusion.53 = f32[10,96,128]{2,1,0:T(8,128)} fusion(f32[10,96,128]{2,1,0:T(8,128)S(1)} %copy-done.1, f32[10,96,128]{2,1,0:T(8,128)S(1)} %copy-done.11, f32[10,96,128]{2,1,0:T(8,128)S(1)} %get-tuple-element.34, f32[10,96,1]{2,1,0:T(8,128)} %collective-permute-done.5, f32[10,96,127]{2,1,0:T(8,128)S(1)} %copy-done.20, f32[10,96,128]{2,1,0:T(8,128)S(1)} %copy-done.10, ...), kind=kLoop, calls=%fused_computation.67 | loop fusion | flops 2088960 | bytes 5898240 | tf_op jit(solution)/shard_map/add | solution.py:196
  (167 shorter events, 69.3 us)
Async XLA Ops:
  8.4 39.1 %all-to-all-start = ((f32[16,40,6,128]{3,1,2,0:T(8,128)}), f32[16,40,6,128]{3,1,2,0:T(8,128)S(1)}, u32[]{:S(2)}, u32[]{:S(2)}) async-start(f32[16,40,6,128]{3,1,2,0:T(8,128)} %bitcast.75), calls=%async_computation | async-start | bytes 3932160 | tf_op jit(solution)/shard_map/all_to_all | solution.py:170
  18.2 63.7 %collective-permute-start = (f32[32,1,128]{2,1,0:T(1,128)}, f32[32,1,128]{2,1,0:T(1,128)}, u32[]{:S(2)}, u32[]{:S(2)}) collective-permute-start(f32[32,1,128]{2,1,0:T(1,128)} %get-tuple-element.68), channel_id=1, source_target_pairs={{0,16},{16,32},{32,48},{48,64},{64,80},{80,96},{96,112},{112,0},{1... | collective-permute-start | bytes 49160 | tf_op jit(solution)/shard_map/ppermute | solution.py:19
  20.8 61.1 %collective-permute-start.1 = (f32[32,1,128]{2,1,0:T(1,128)}, f32[32,1,128]{2,1,0:T(1,128)}, u32[]{:S(2)}, u32[]{:S(2)}) collective-permute-start(f32[32,1,128]{2,1,0:T(1,128)} %get-tuple-element.67), channel_id=1, source_target_pairs={{0,112},{16,0},{32,16},{48,32},{64,48},{80,64},{96,80},{112,96},{1... | collective-permute-start | bytes 49160 | tf_op jit(solution)/shard_map/ppermute | solution.py:20
  31.0 50.9 %collective-permute-start.2 = (f32[32,96,1]{1,0,2:T(8,128)}, f32[32,96,1]{1,0,2:T(8,128)}, u32[]{:S(2)}, u32[]{:S(2)}) collective-permute-start(f32[32,96,1]{1,0,2:T(8,128)} %copy.121), channel_id=1, source_target_pairs={{0,1},{1,2},{2,3},{3,4},{4,5},{5,6},{6,7},{7,8},{8,9},{9,10},{10,1... | collective-permute-start | bytes 36872 | tf_op jit(solution)/shard_map/ppermute | solution.py:21
  34.8 47.1 %collective-permute-start.3 = (f32[32,96,1]{1,0,2:T(8,128)}, f32[32,96,1]{1,0,2:T(8,128)}, u32[]{:S(2)}, u32[]{:S(2)}) collective-permute-start(f32[32,96,1]{1,0,2:T(8,128)} %copy.122), channel_id=1, source_target_pairs={{0,15},{1,0},{2,1},{3,2},{4,3},{5,4},{6,5},{7,6},{8,7},{9,8},{10,9... | collective-permute-start | bytes 36872 | tf_op jit(solution)/shard_map/ppermute | solution.py:22
  81.6 9.7 %copy-start.8 = (s32[10,96,128]{2,1,0:T(8,128)S(1)}, s32[10,96,128]{2,1,0:T(8,128)}, u32[]{:S(2)}) copy-start(s32[10,96,128]{2,1,0:T(8,128)} %param.15) | copy-start | bytes 1474564
  81.7 9.7 %copy-start.12 = (f32[10,96,127]{2,1,0:T(8,128)S(1)}, f32[10,96,127]{2,1,0:T(8,128)}, u32[]{:S(2)}) copy-start(f32[10,96,127]{2,1,0:T(8,128)} %get-tuple-element.95) | copy-start | bytes 1463044
  81.7 9.7 %copy-start.28 = (f32[96,128]{1,0:T(8,128)S(1)}, f32[96,128]{1,0:T(8,128)}, u32[]{:S(2)}) copy-start(f32[96,128]{1,0:T(8,128)} %param.18) | copy-start | bytes 147460
  88.3 9.6 %collective-permute-start.4 = (f32[54,128]{1,0:T(8,128)S(1)}, f32[54,128]{1,0:T(8,128)S(1)}, u32[]{:S(2)}, u32[]{:S(2)}) collective-permute-start(f32[54,128]{1,0:T(8,128)S(1)} %maximum_bitcast_fusion), channel_id=1, source_target_pairs={{0,1},{1,0},{2,3},{3,2},{4,5},{5,4},{6,7},{7,6},{8,9},{9,8},{10,11... | collective-permute-start | bytes 82952 | tf_op jit(solution)/shard_map/ppermute | solution.py:117
  99.3 2.8 %collective-permute-start.9 = (f32[54,128]{1,0:T(8,128)S(1)}, f32[54,128]{1,0:T(8,128)S(1)}, u32[]{:S(2)}, u32[]{:S(2)}) collective-permute-start(f32[54,128]{1,0:T(8,128)S(1)} %add.91), channel_id=1, source_target_pairs={{0,2},{1,3},{2,0},{3,1},{4,6},{5,7},{6,4},{7,5},{8,10},{9,11},{10,... | collective-permute-start | bytes 82952 | tf_op jit(solution)/shard_map/ppermute | solution.py:117
  102.1 2.7 %collective-permute-start.10 = (f32[54,128]{1,0:T(8,128)S(1)}, f32[54,128]{1,0:T(8,128)S(1)}, u32[]{:S(2)}, u32[]{:S(2)}) collective-permute-start(f32[54,128]{1,0:T(8,128)S(1)} %add.102), channel_id=1, source_target_pairs={{0,4},{1,5},{2,6},{3,7},{4,0},{5,1},{6,2},{7,3},{8,12},{9,13},{10,... | collective-permute-start | bytes 82952 | tf_op jit(solution)/shard_map/ppermute | solution.py:117
  104.8 4.2 %collective-permute-start.11 = (f32[54,128]{1,0:T(8,128)S(1)}, f32[54,128]{1,0:T(8,128)S(1)}, u32[]{:S(2)}, u32[]{:S(2)}) collective-permute-start(f32[54,128]{1,0:T(8,128)S(1)} %add.103), channel_id=1, source_target_pairs={{0,8},{1,9},{2,10},{3,11},{4,12},{5,13},{6,14},{7,15},{8,0},{9,1},... | collective-permute-start | bytes 82952 | tf_op jit(solution)/shard_map/ppermute | solution.py:117
  109.1 8.8 %collective-permute-start.12 = (f32[54,128]{1,0:T(8,128)S(1)}, f32[54,128]{1,0:T(8,128)S(1)}, u32[]{:S(2)}, u32[]{:S(2)}) collective-permute-start(f32[54,128]{1,0:T(8,128)S(1)} %add.104), channel_id=1, source_target_pairs={{0,16},{16,0},{32,48},{48,32},{64,80},{80,64},{96,112},{112,96},{1... | collective-permute-start | bytes 82952 | tf_op jit(solution)/shard_map/ppermute | solution.py:117
  110.8 24.1 %all-to-all-start.1 = ((f32[16,20,6,128]{3,1,2,0:T(8,128)}), f32[16,20,6,128]{3,1,2,0:T(8,128)S(1)}, u32[]{:S(2)}, u32[]{:S(2)}) async-start(f32[16,20,6,128]{3,1,2,0:T(8,128)} %fusion.12), calls=%async_computation.1 | async-start | bytes 2359296 | tf_op jit(solution)/shard_map/all_to_all | solution.py:177
  117.9 3.0 %collective-permute-start.13 = (f32[54,128]{1,0:T(8,128)S(1)}, f32[54,128]{1,0:T(8,128)S(1)}, u32[]{:S(2)}, u32[]{:S(2)}) collective-permute-start(f32[54,128]{1,0:T(8,128)S(1)} %add.105), channel_id=1, source_target_pairs={{0,32},{16,48},{32,0},{48,16},{64,96},{80,112},{96,64},{112,80},{1... | collective-permute-start | bytes 82952 | tf_op jit(solution)/shard_map/ppermute | solution.py:117
  120.8 11.5 %collective-permute-start.14 = (f32[54,128]{1,0:T(8,128)S(1)}, f32[54,128]{1,0:T(8,128)S(1)}, u32[]{:S(2)}, u32[]{:S(2)}) collective-permute-start(f32[54,128]{1,0:T(8,128)S(1)} %add.106), channel_id=1, source_target_pairs={{0,64},{16,80},{32,96},{48,112},{64,0},{80,16},{96,32},{112,48},{1... | collective-permute-start | bytes 82952 | tf_op jit(solution)/shard_map/ppermute | solution.py:117
  126.3 19.2 %collective-permute-start.5 = (f32[10,96,1]{2,1,0:T(8,128)}, f32[10,96,1]{2,1,0:T(8,128)}, u32[]{:S(2)}, u32[]{:S(2)}) collective-permute-start(f32[10,96,1]{2,1,0:T(8,128)} %get-tuple-element.88), channel_id=1, source_target_pairs={{0,15},{1,0},{2,1},{3,2},{4,3},{5,4},{6,5},{7,6},{8,7},{9,8},{10,9... | collective-permute-start | bytes 11528 | tf_op jit(solution)/shard_map/ppermute | solution.py:22
  128.0 17.6 %collective-permute-start.6 = (f32[10,96,1]{2,1,0:T(8,128)}, f32[10,96,1]{2,1,0:T(8,128)}, u32[]{:S(2)}, u32[]{:S(2)}) collective-permute-start(f32[10,96,1]{2,1,0:T(8,128)} %get-tuple-element.87), channel_id=1, source_target_pairs={{0,1},{1,2},{2,3},{3,4},{4,5},{5,6},{6,7},{7,8},{8,9},{9,10},{10,1... | collective-permute-start | bytes 11528 | tf_op jit(solution)/shard_map/ppermute | solution.py:21
  129.4 18.2 %collective-permute-start.7 = (f32[10,1,128]{2,1,0:T(1,128)S(1)}, f32[10,1,128]{2,1,0:T(1,128)S(1)}, u32[]{:S(2)}, u32[]{:S(2)}) collective-permute-start(f32[10,1,128]{2,1,0:T(1,128)S(1)} %get-tuple-element.84), channel_id=1, source_target_pairs={{0,112},{16,0},{32,16},{48,32},{64,48},{80,64},{96,80},{112,96},{1... | collective-permute-start | bytes 15368 | tf_op jit(solution)/shard_map/ppermute | solution.py:20
  131.4 17.5 %collective-permute-start.8 = (f32[10,1,128]{2,1,0:T(1,128)S(1)}, f32[10,1,128]{2,1,0:T(1,128)S(1)}, u32[]{:S(2)}, u32[]{:S(2)}) collective-permute-start(f32[10,1,128]{2,1,0:T(1,128)S(1)} %get-tuple-element.83), channel_id=1, source_target_pairs={{0,16},{16,32},{32,48},{48,64},{64,80},{80,96},{96,112},{112,0},{1... | collective-permute-start | bytes 15368 | tf_op jit(solution)/shard_map/ppermute | solution.py:19
  137.1 11.8 %copy-start.21 = (f32[10,95,128]{2,1,0:T(8,128)S(1)}, f32[10,95,128]{2,1,0:T(8,128)}, u32[]{:S(2)}) copy-start(f32[10,95,128]{2,1,0:T(8,128)} %get-tuple-element.85) | copy-start | bytes 1459204
  137.1 11.8 %copy-start.22 = (f32[10,95,128]{2,1,0:T(8,128)S(1)}, f32[10,95,128]{2,1,0:T(8,128)}, u32[]{:S(2)}) copy-start(f32[10,95,128]{2,1,0:T(8,128)} %get-tuple-element.86) | copy-start | bytes 1459204
  138.5 10.4 %copy-start.19 = (f32[10,96,127]{2,1,0:T(8,128)S(1)}, f32[10,96,127]{2,1,0:T(8,128)}, u32[]{:S(2)}) copy-start(f32[10,96,127]{2,1,0:T(8,128)} %get-tuple-element.89) | copy-start | bytes 1463044
  138.5 10.4 %copy-start.20 = (f32[10,96,127]{2,1,0:T(8,128)S(1)}, f32[10,96,127]{2,1,0:T(8,128)}, u32[]{:S(2)}) copy-start(f32[10,96,127]{2,1,0:T(8,128)} %get-tuple-element.90) | copy-start | bytes 1463044
  (22 other events, 58.2 us)

commit v5 on v4

--- a/solution.py
+++ b/solution.py
@@ -107,19 +107,21 @@
 LANES = 128
 
 
-def butterfly_sum(values, axes, tie):
-    first = True
+def butterfly_sum(values, axes, tie, late):
+    rounds = []
     for axis in axes:
-        size = lax.axis_size(axis)
         stride = 1
-        while stride < size:
-            pairs = [(i, i ^ stride) for i in range(size)]
-            values = values + lax.ppermute(values, axis, pairs)
-            if first:
-                values, tie = lax.optimization_barrier((values, tie))
-                first = False
+        while stride < lax.axis_size(axis):
+            rounds.append((axis, stride))
             stride *= 2
-    return values, tie
+    for index, (axis, stride) in enumerate(rounds):
+        if index == len(rounds) - 1:
+            values, late = lax.optimization_barrier((values, late))
+        pairs = [(i, i ^ stride) for i in range(lax.axis_size(axis))]
+        values = values + lax.ppermute(values, axis, pairs)
+        if index == 0:
+            values, tie = lax.optimization_barrier((values, tie))
+    return values, tie, late
 
 
 def pack(parts):
@@ -171,11 +173,7 @@
     weight_grads, first_delta = network_vjp(weights, band[:, : 2 * levels], band[:, 2 * levels :])
     packed = pack(weight_grads)
     packed, plane_halo = lax.optimization_barrier((packed, plane_halo))
-    total, first_delta = butterfly_sum(packed, ("lon", "lat"), first_delta)
-    summed = unpack(total, weight_grads)
-    band_grad = input_pullback(weights, first_delta, 2 * levels)
-    returned = lax.all_to_all(band_grad, "lon", split_axis=0, concat_axis=0, tiled=True)
-    input_grad = returned.transpose(1, 2, 0, 3).reshape(2 * levels, tile_rows, tile_cols)
+
     below, above, left, right = plane_halo
     below = below * row_inside(-1)
     above = above * row_inside(1)
@@ -190,7 +188,12 @@
     tracer_term = laplace(tracer_adjoint, part(0, levels), sea_cells, sea_near, *faces)
     first_laplace = laplace(velocity_adjoint, part(levels, 2 * levels), sea_cells, sea_near, *faces)
     scaled = viscosity * first_laplace
-    viscous_term = laplace(scaled, edges(scaled), sea_cells, sea_near, *faces)
+    total, first_delta, scaled_halo = butterfly_sum(packed, ("lon", "lat"), first_delta, edges(scaled))
+    summed = unpack(total, weight_grads)
+    band_grad = input_pullback(weights, first_delta, 2 * levels)
+    returned = lax.all_to_all(band_grad, "lon", split_axis=0, concat_axis=0, tiled=True)
+    input_grad = returned.transpose(1, 2, 0, 3).reshape(2 * levels, tile_rows, tile_cols)
+    viscous_term = laplace(scaled, scaled_halo, sea_cells, sea_near, *faces)
     scale = 1.0 / math.sqrt(tile_rows * lax.axis_size("lat") * tile_cols * lax.axis_size("lon"))
     tracer_grad = tracer_adjoint + tracer_term + input_grad[:levels]
     velocity_grad = velocity_adjoint - viscous_term + input_grad[levels:]

time: 153 us -> 156 us (1.020)
  waiting for transfers between devices: 17.1 us -> 19.8 us
    ppermute x2, waiting for transfers between devices: 6.7 us -> 0.01 us  [edges(): right = lax.ppermute(block[..., :, :1], 'lon', ring('lon', -1))]
    all_to_all x1, waiting for transfers between devices: 0.31 us -> 6.97 us  [on_device(): lax.all_to_all(band_grad, 'lon', split_axis=0, concat_axis=0, tiled=True)]
    ppermute x7, waiting for transfers between devices: 6.66 us -> 12.8 us  [butterfly_sum(): values = values + lax.ppermute(values, axis, pairs)]
    ppermute x2, starting transfers between devices: 5.48 us -> 8.54 us  [edges(): above = lax.ppermute(block[..., :1, :], 'lat', ring('lat', -1))]
    all_to_all x1, starting transfers between devices: 7.02 us -> 9.48 us  [on_device(): lax.all_to_all(band_grad, 'lon', split_axis=0, concat_axis=0, tiled=True)]
    ppermute x2, waiting for transfers between devices: 2.08 us -> 0.01 us  [edges(): above = lax.ppermute(block[..., :1, :], 'lat', ring('lat', -1))]
    slice x2 -> x1, local copies, waits for them, and re-layouts: 3.63 us -> 2.5 us  [edges(): left = lax.ppermute(block[..., :, -1:], 'lon', ring('lon', 1))]
    slice x2 -> x3, local copies, waits for them, and re-layouts: 6.68 us -> 7.75 us  [edges(): right = lax.ppermute(block[..., :, :1], 'lon', ring('lon', -1))]
  transfers between devices with their start and end apart: 17 -> 17, of which waited for: 8 -> 5; matrix products, arithmetic and copies ran while one was open for 48% -> 47% of each run, Pallas kernels for 0% -> 0%
where the time goes in v5:
time: 156 us; the launch traced here: 155 us
  local copies, waits for them, and re-layouts  58.5 us (38%)
  starting transfers between devices  39.2 us (25%)
  waiting for transfers between devices  19.8 us (13%)
  other arithmetic  19.1 us (12%)
  matrix products  17.5 us (11%)
    ppermute x7, waiting for transfers between devices, butterfly_sum(): values = values + lax.ppermute(values, axis, pairs)  12.8 us
    ppermute x7, starting transfers between devices, butterfly_sum(): values = values + lax.ppermute(values, axis, pairs)  9.67 us
    all_to_all x1, starting transfers between devices, on_device(): lax.all_to_all(band_grad, 'lon', split_axis=0, concat_axis=0, tiled=True)  9.48 us
    unnamed x62, local copies, waits for them, and re-layouts  9.1 us
    ppermute x2, starting transfers between devices, edges(): above = lax.ppermute(block[..., :1, :], 'lat', ring('lat', -1))  8.54 us
    slice x3, local copies, waits for them, and re-layouts, edges(): right = lax.ppermute(block[..., :, :1], 'lon', ring('lon', -1))  7.75 us
    all_to_all x1, waiting for transfers between devices, on_device(): lax.all_to_all(band_grad, 'lon', split_axis=0, concat_axis=0, tiled=True)  6.97 us
    all_to_all x1, starting transfers between devices, on_device(): lax.all_to_all(chunks.transpose(2, 0, 1, 3), 'lon', split_axis=0, concat_...  6.95 us
  transfers between devices with their start and end apart: 17, of which 5 were waited for; matrix products, arithmetic and copies ran while one was open for 47% of the time, Pallas kernels for 0%

profile of v5, /device:TPU:1, one launch (start us, length us, event | category | flops | bytes accessed | tf_op | source)
XLA Modules:
  0.0 155.4 jit_solution(16563077078509980842)
XLA Ops:
  0.7 2.0 %constant_dynamic-update-slice_fusion.2 = f32[32,96,128]{2,1,0:T(8,128)} fusion(f32[10,96,128]{2,1,0:T(8,128)} %param.13), kind=kLoop, calls=%fused_computation.87 | loop fusion | bytes 983040
  6.0 2.4 %copy.169 = f32[40,6,16,128]{3,0,1,2:T(8,128)} copy(f32[40,6,16,128]{3,2,1,0:T(8,128)S(1)} %bitcast.76) | data formatting | bytes 3932160 | tf_op jit(solution)/shard_map/reshape | solution.py:171
  8.4 6.9 %all-to-all-start = ((f32[16,40,6,128]{3,1,2,0:T(8,128)}), f32[16,40,6,128]{3,1,2,0:T(8,128)S(1)}, u32[]{:S(2)}, u32[]{:S(2)}) async-start(f32[16,40,6,128]{3,1,2,0:T(8,128)} %bitcast.75), calls=%async_computation | async-start | bytes 3932160 | tf_op jit(solution)/shard_map/all_to_all | solution.py:172
  18.2 2.6 %collective-permute-start = (f32[32,1,128]{2,1,0:T(1,128)}, f32[32,1,128]{2,1,0:T(1,128)}, u32[]{:S(2)}, u32[]{:S(2)}) collective-permute-start(f32[32,1,128]{2,1,0:T(1,128)} %get-tuple-element.78), channel_id=1, source_target_pairs={{0,16},{16,32},{32,48},{48,64},{64,80},{80,96},{96,112},{112,0},{1... | collective-permute-start | bytes 49160 | tf_op jit(solution)/shard_map/ppermute | solution.py:19
  20.8 3.5 %collective-permute-start.1 = (f32[32,1,128]{2,1,0:T(1,128)}, f32[32,1,128]{2,1,0:T(1,128)}, u32[]{:S(2)}, u32[]{:S(2)}) collective-permute-start(f32[32,1,128]{2,1,0:T(1,128)} %get-tuple-element.77), channel_id=1, source_target_pairs={{0,112},{16,0},{32,16},{48,32},{64,48},{80,64},{96,80},{112,96},{1... | collective-permute-start | bytes 49160 | tf_op jit(solution)/shard_map/ppermute | solution.py:20
  24.3 4.2 %fusion.78 = (f32[32,96,1]{2,1,0:T(8,128)}, f32[32,96,1]{2,1,0:T(8,128)}) fusion(f32[32,96,128]{2,1,0:T(8,128)} %bitcast_dynamic-update-slice_fusion), kind=kLoop, calls=%fused_computation.110 | loop fusion | bytes 49152 | tf_op jit(solution)/shard_map/slice | solution.py:22
  28.5 2.5 %copy.121 = f32[32,96,1]{1,0,2:T(8,128)} copy(f32[32,96,1]{2,1,0:T(8,128)} %get-tuple-element.76) | data formatting | bytes 24576 | tf_op jit(solution)/shard_map/slice | solution.py:21
  32.3 2.5 %copy.122 = f32[32,96,1]{1,0,2:T(8,128)} copy(f32[32,96,1]{2,1,0:T(8,128)} %get-tuple-element.75) | data formatting | bytes 24576 | tf_op jit(solution)/shard_map/slice | solution.py:22
  47.5 2.7 %convolution_bitcast_fusion.1 = f32[16,96,6,128]{3,1,2,0:T(8,128)S(1)} fusion(f32[20,96,1,1]{1,0,2,3:T(8,128)} %reshape.79, f32[16,40,6,128]{3,1,2,0:T(8,128)S(1)} %all-to-all-done), kind=kOutput, calls=%fused_computation.10 | convolution fusion | flops 141557760 | bytes 5905920 | tf_op jit(solution)/shard_map/oc,soml->scml/dot_general | solution.py:92
  56.9 4.0 %fusion.9 = (f32[16,32,6,128]{3,1,2,0:T(8,128)S(1)}, f32[16,32,6,128]{3,1,2,0:T(8,128)S(1)}) fusion(f32[16,96,6,128]{3,1,2,0:T(8,128)S(1)} %convolution_bitcast_fusion.1, f32[1,32,6,1]{3,1,2,0:T(8,128)S(1)} %get-tuple-element.56, f32[15,32,6,1]{3,1,2,0:T(8,128)S(1)} %get-tuple-element.58, f32[16,32,6,127]{3,1,2,0:T(8,128)S(1)} %get-tuple-element.60, ...), kind=kOutput, calls=%fused_computation.19 | convolution fusion | flops 237109248 | bytes 12595200 | tf_op jit(solution)/shard_map/oc,scml->soml/dot_general | solution.py:80
  62.1 2.3 %fusion.19 = f32[32,96]{1,0:T(8,128)S(1)} fusion(f32[16,32,6,128]{3,1,2,0:T(8,128)S(1)} %get-tuple-element.130, f32[1,32,6,1]{3,1,2,0:T(8,128)S(1)} %get-tuple-element.86, f32[15,32,6,1]{3,1,2,0:T(8,128)S(1)} %get-tuple-element.88, f32[16,32,6,127]{3,1,2,0:T(8,128)S(1)} %get-tuple-element.90, f32[16,32,6,128]{3,1,2,0:T(8,128)S(1)} %tanh_bitcast_fusion.1, ...), kind=kOutput, calls=%fused_computation.28 | convolution fusion | flops 233570304 | bytes 6303744 | tf_op jit(solution)/shard_map/soml,scml->oc/dot_general | solution.py:94
  64.5 2.0 %convolution_bitcast_fusion = f32[16,96,6,128]{3,1,2,0:T(8,128)S(1)} fusion(f32[16,32,6,128]{3,1,2,0:T(8,128)S(1)} %get-tuple-element.130, f32[32,96,1,1]{1,0,2,3:T(8,128)S(1)} %reshape.81), kind=kOutput, calls=%fused_computation.9 | convolution fusion | flops 226492416 | bytes 6303744 | tf_op jit(solution)/shard_map/oc,soml->scml/dot_general | solution.py:95
  66.6 2.6 %fusion.66 = (f32[15,32,6,1]{3,1,2,0:T(8,128)}, f32[15,32,6,1]{3,1,2,0:T(8,128)}) fusion(f32[16,96,6,128]{3,1,2,0:T(8,128)S(1)} %convolution_bitcast_fusion), kind=kLoop, calls=%fused_computation.98 | loop fusion | bytes 46080 | tf_op jit(solution)/shard_map/jit(_roll_static)/slice | solution.py:52
  69.6 2.2 %fusion.67 = (f32[16,32,6,127]{3,1,2,0:T(8,128)}, f32[16,32,6,127]{3,1,2,0:T(8,128)}) fusion(f32[16,96,6,128]{3,1,2,0:T(8,128)S(1)} %convolution_bitcast_fusion), kind=kLoop, calls=%fused_computation.99 | loop fusion | bytes 6242304 | tf_op jit(solution)/shard_map/slice | solution.py:52
  71.8 2.4 %fusion.24 = f32[20,96]{1,0:T(8,128)S(1)} fusion(f32[16,20,6,128]{3,1,2,0:T(8,128)S(1)} %get-tuple-element.67, f32[1,32,6,1]{3,1,2,0:T(8,128)S(1)} %get-tuple-element.80, f32[15,32,6,1]{3,1,2,0:T(8,128)S(1)} %get-tuple-element.82, f32[16,32,6,127]{3,1,2,0:T(8,128)S(1)} %get-tuple-element.84, f32[16,32,6,128]{3,1,2,0:T(8,128)S(1)} %get-tuple-element.131, ...), kind=kOutput, calls=%fused_computation.29 | convolution fusion | flops 148635648 | bytes 5709312 | tf_op jit(solution)/shard_map/soml,scml->oc/dot_general | solution.py:91
  74.5 4.5 %fusion.7 = f32[16,32,6,128]{3,1,2,0:T(8,128)S(1)} fusion(f32[16,96,6,128]{3,1,2,0:T(8,128)} %copy-done, f32[1,32,6,1]{3,1,2,0:T(8,128)S(1)} %get-tuple-element.50, f32[15,32,6,1]{3,1,2,0:T(8,128)} %get-tuple-element.52, f32[16,32,6,127]{3,1,2,0:T(8,128)} %get-tuple-element.54, f32[16,32,6,127]{3,1,2,0:T(8,128)} %get-tuple-element.53, ...), kind=kLoop, calls=%fused_computation.16 | loop fusion | flops 3538944 | bytes 7864320 | tf_op jit(solution)/shard_map/mul | solution.py:96
  88.3 2.9 %collective-permute-start.4 = (f32[54,128]{1,0:T(8,128)S(1)}, f32[54,128]{1,0:T(8,128)S(1)}, u32[]{:S(2)}, u32[]{:S(2)}) collective-permute-start(f32[54,128]{1,0:T(8,128)S(1)} %maximum_bitcast_fusion), channel_id=1, source_target_pairs={{0,1},{1,0},{2,3},{3,2},{4,5},{5,4},{6,7},{7,6},{8,9},{9,8},{10,11... | collective-permute-start | bytes 82952 | tf_op jit(solution)/shard_map/ppermute | solution.py:121
  91.4 4.3 %fusion.44 = (f32[10,96,128]{2,1,0:T(8,128)S(1)}, f32[10,96,128]{2,1,0:T(8,128)S(1)}, f32[10,96,128]{2,1,0:T(8,128)}, f32[10,96,128]{2,1,0:T(8,128)}, f32[10,96,128]{2,1,0:T(8,128)}) fusion(f32[10,96,128]{2,1,0:T(8,128)S(1)} %copy-done.1, f32[10,96,1]{2,1,0:T(8,128)} %copy.130, f32[10,96,127]{2,1,0:T(8,128)} %get-tuple-element.137, ...), kind=kLoop, calls=%fused_computation.54 | loop fusion | flops 3563520 | bytes 7618560 | tf_op jit(solution)/shard_map/mul | solution.py:190
  96.9 5.1 %collective-permute-start.11 = (f32[10,1,128]{2,1,0:T(1,128)S(1)}, f32[10,1,128]{2,1,0:T(1,128)S(1)}, u32[]{:S(2)}, u32[]{:S(2)}) collective-permute-start(f32[10,1,128]{2,1,0:T(1,128)S(1)} %get-tuple-element.99), channel_id=1, source_target_pairs={{0,112},{16,0},{32,16},{48,32},{64,48},{80,64},{96,80},{112,96},{1... | collective-permute-start | bytes 15368 | tf_op jit(solution)/shard_map/ppermute | solution.py:20
  105.9 8.0 %collective-permute-done.5 = f32[54,128]{1,0:T(8,128)S(1)} collective-permute-done((f32[54,128]{1,0:T(8,128)S(1)}, f32[54,128]{1,0:T(8,128)S(1)}, u32[]{:S(2)}, u32[]{:S(2)}) %collective-permute-start.5) | collective-permute-done | bytes 27680 | tf_op jit(solution)/shard_map/ppermute | solution.py:121
  116.6 2.2 %collective-permute-start.7 = (f32[54,128]{1,0:T(8,128)S(1)}, f32[54,128]{1,0:T(8,128)S(1)}, u32[]{:S(2)}, u32[]{:S(2)}) collective-permute-start(f32[54,128]{1,0:T(8,128)S(1)} %add.99), channel_id=1, source_target_pairs={{0,8},{1,9},{2,10},{3,11},{4,12},{5,13},{6,14},{7,15},{8,0},{9,1},... | collective-permute-start | bytes 82952 | tf_op jit(solution)/shard_map/ppermute | solution.py:121
  122.6 9.5 %all-to-all-start.1 = ((f32[16,20,6,128]{3,1,2,0:T(8,128)}), f32[16,20,6,128]{3,1,2,0:T(8,128)S(1)}, u32[]{:S(2)}, u32[]{:S(2)}) async-start(f32[16,20,6,128]{3,1,2,0:T(8,128)} %fusion.12), calls=%async_computation.1 | async-start | bytes 2359296 | tf_op jit(solution)/shard_map/all_to_all | solution.py:194
  142.1 7.0 %all-to-all-done.1 = f32[16,20,6,128]{3,1,2,0:T(8,128)S(1)} async-done(((f32[16,20,6,128]{3,1,2,0:T(8,128)}), f32[16,20,6,128]{3,1,2,0:T(8,128)S(1)}, u32[]{:S(2)}, u32[]{:S(2)}) %all-to-all-start.1) | async-done | bytes 983072 | tf_op jit(solution)/shard_map/all_to_all | solution.py:194
  152.8 2.6 %fusion.53 = f32[10,96,128]{2,1,0:T(8,128)} fusion(f32[10,96,128]{2,1,0:T(8,128)S(1)} %copy-done.1, f32[10,96,128]{2,1,0:T(8,128)S(1)} %copy-done.11, f32[10,96,128]{2,1,0:T(8,128)S(1)} %get-tuple-element.44, f32[10,96,1]{2,1,0:T(8,128)} %collective-permute-done.13, f32[10,96,127]{2,1,0:T(8,128)S(1)} %copy-done.20, f32[10,96,128]{2,1,0:T(8,128)S(1)} %copy-done.10, ...), kind=kLoop, calls=%fused_computation.67 | loop fusion | flops 2088960 | bytes 5898240 | tf_op jit(solution)/shard_map/add | solution.py:199
  (167 shorter events, 63.2 us)
Async XLA Ops:
  8.4 7.0 %copy-start.26 = (f32[96,128]{1,0:T(8,128)S(1)}, f32[96,128]{1,0:T(8,128)}, u32[]{:S(2)}) copy-start(f32[96,128]{1,0:T(8,128)} %param.16) | copy-start | bytes 147460
  8.4 7.6 %copy-start.25 = (f32[96,128]{1,0:T(8,128)S(1)}, f32[96,128]{1,0:T(8,128)}, u32[]{:S(2)}) copy-start(f32[96,128]{1,0:T(8,128)} %param.17) | copy-start | bytes 147460
  8.4 39.1 %all-to-all-start = ((f32[16,40,6,128]{3,1,2,0:T(8,128)}), f32[16,40,6,128]{3,1,2,0:T(8,128)S(1)}, u32[]{:S(2)}, u32[]{:S(2)}) async-start(f32[16,40,6,128]{3,1,2,0:T(8,128)} %bitcast.75), calls=%async_computation | async-start | bytes 3932160 | tf_op jit(solution)/shard_map/all_to_all | solution.py:172
  18.2 63.7 %collective-permute-start = (f32[32,1,128]{2,1,0:T(1,128)}, f32[32,1,128]{2,1,0:T(1,128)}, u32[]{:S(2)}, u32[]{:S(2)}) collective-permute-start(f32[32,1,128]{2,1,0:T(1,128)} %get-tuple-element.78), channel_id=1, source_target_pairs={{0,16},{16,32},{32,48},{48,64},{64,80},{80,96},{96,112},{112,0},{1... | collective-permute-start | bytes 49160 | tf_op jit(solution)/shard_map/ppermute | solution.py:19
  20.8 61.1 %collective-permute-start.1 = (f32[32,1,128]{2,1,0:T(1,128)}, f32[32,1,128]{2,1,0:T(1,128)}, u32[]{:S(2)}, u32[]{:S(2)}) collective-permute-start(f32[32,1,128]{2,1,0:T(1,128)} %get-tuple-element.77), channel_id=1, source_target_pairs={{0,112},{16,0},{32,16},{48,32},{64,48},{80,64},{96,80},{112,96},{1... | collective-permute-start | bytes 49160 | tf_op jit(solution)/shard_map/ppermute | solution.py:20
  31.0 50.9 %collective-permute-start.2 = (f32[32,96,1]{1,0,2:T(8,128)}, f32[32,96,1]{1,0,2:T(8,128)}, u32[]{:S(2)}, u32[]{:S(2)}) collective-permute-start(f32[32,96,1]{1,0,2:T(8,128)} %copy.121), channel_id=1, source_target_pairs={{0,1},{1,2},{2,3},{3,4},{4,5},{5,6},{6,7},{7,8},{8,9},{9,10},{10,1... | collective-permute-start | bytes 36872 | tf_op jit(solution)/shard_map/ppermute | solution.py:21
  34.8 47.1 %collective-permute-start.3 = (f32[32,96,1]{1,0,2:T(8,128)}, f32[32,96,1]{1,0,2:T(8,128)}, u32[]{:S(2)}, u32[]{:S(2)}) collective-permute-start(f32[32,96,1]{1,0,2:T(8,128)} %copy.122), channel_id=1, source_target_pairs={{0,15},{1,0},{2,1},{3,2},{4,3},{5,4},{6,5},{7,6},{8,7},{9,8},{10,9... | collective-permute-start | bytes 36872 | tf_op jit(solution)/shard_map/ppermute | solution.py:22
  74.5 5.6 %copy-start.3 = (f32[16,60,6,128]{3,1,2,0:T(8,128)S(1)}, f32[16,60,6,128]{3,1,2,0:T(8,128)}, u32[]{:S(2)}) copy-start(f32[16,60,6,128]{3,1,2,0:T(8,128)} %copy-done.2) | copy-start | bytes 8847364
  81.6 9.7 %copy-start.8 = (s32[10,96,128]{2,1,0:T(8,128)S(1)}, s32[10,96,128]{2,1,0:T(8,128)}, u32[]{:S(2)}) copy-start(s32[10,96,128]{2,1,0:T(8,128)} %param.15) | copy-start | bytes 1474564
  81.7 9.7 %copy-start.12 = (f32[10,96,127]{2,1,0:T(8,128)S(1)}, f32[10,96,127]{2,1,0:T(8,128)}, u32[]{:S(2)}) copy-start(f32[10,96,127]{2,1,0:T(8,128)} %get-tuple-element.105) | copy-start | bytes 1463044
  81.7 9.7 %copy-start.28 = (f32[96,128]{1,0:T(8,128)S(1)}, f32[96,128]{1,0:T(8,128)}, u32[]{:S(2)}) copy-start(f32[96,128]{1,0:T(8,128)} %param.18) | copy-start | bytes 147460
  88.3 14.2 %collective-permute-start.4 = (f32[54,128]{1,0:T(8,128)S(1)}, f32[54,128]{1,0:T(8,128)S(1)}, u32[]{:S(2)}, u32[]{:S(2)}) collective-permute-start(f32[54,128]{1,0:T(8,128)S(1)} %maximum_bitcast_fusion), channel_id=1, source_target_pairs={{0,1},{1,0},{2,3},{3,2},{4,5},{5,4},{6,7},{7,6},{8,9},{9,8},{10,11... | collective-permute-start | bytes 82952 | tf_op jit(solution)/shard_map/ppermute | solution.py:121
  95.7 6.8 %copy-start.6 = (f32[16,32,6,128]{3,1,2,0:T(8,128)S(1)}, f32[16,32,6,128]{3,1,2,0:T(8,128)}, u32[]{:S(2)}) copy-start(f32[16,32,6,128]{3,1,2,0:T(8,128)} %copy-done.5) | copy-start | bytes 4718596
  96.8 38.1 %collective-permute-start.10 = (f32[10,1,128]{2,1,0:T(1,128)S(1)}, f32[10,1,128]{2,1,0:T(1,128)S(1)}, u32[]{:S(2)}, u32[]{:S(2)}) collective-permute-start(f32[10,1,128]{2,1,0:T(1,128)S(1)} %get-tuple-element.100), channel_id=1, source_target_pairs={{0,16},{16,32},{32,48},{48,64},{64,80},{80,96},{96,112},{112,0},{1... | collective-permute-start | bytes 15368 | tf_op jit(solution)/shard_map/ppermute | solution.py:19
  96.9 38.1 %collective-permute-start.11 = (f32[10,1,128]{2,1,0:T(1,128)S(1)}, f32[10,1,128]{2,1,0:T(1,128)S(1)}, u32[]{:S(2)}, u32[]{:S(2)}) collective-permute-start(f32[10,1,128]{2,1,0:T(1,128)S(1)} %get-tuple-element.99), channel_id=1, source_target_pairs={{0,112},{16,0},{32,16},{48,32},{64,48},{80,64},{96,80},{112,96},{1... | collective-permute-start | bytes 15368 | tf_op jit(solution)/shard_map/ppermute | solution.py:20
  101.9 33.0 %collective-permute-start.12 = (f32[10,96,1]{2,1,0:T(8,128)}, f32[10,96,1]{2,1,0:T(8,128)}, u32[]{:S(2)}, u32[]{:S(2)}) collective-permute-start(f32[10,96,1]{2,1,0:T(8,128)} %get-tuple-element.98), channel_id=1, source_target_pairs={{0,1},{1,2},{2,3},{3,4},{4,5},{5,6},{6,7},{7,8},{8,9},{9,10},{10,1... | collective-permute-start | bytes 11528 | tf_op jit(solution)/shard_map/ppermute | solution.py:21
  101.9 33.0 %collective-permute-start.13 = (f32[10,96,1]{2,1,0:T(8,128)}, f32[10,96,1]{2,1,0:T(8,128)}, u32[]{:S(2)}, u32[]{:S(2)}) collective-permute-start(f32[10,96,1]{2,1,0:T(8,128)} %get-tuple-element.97), channel_id=1, source_target_pairs={{0,15},{1,0},{2,1},{3,2},{4,3},{5,4},{6,5},{7,6},{8,7},{9,8},{10,9... | collective-permute-start | bytes 11528 | tf_op jit(solution)/shard_map/ppermute | solution.py:22
  103.9 10.0 %collective-permute-start.5 = (f32[54,128]{1,0:T(8,128)S(1)}, f32[54,128]{1,0:T(8,128)S(1)}, u32[]{:S(2)}, u32[]{:S(2)}) collective-permute-start(f32[54,128]{1,0:T(8,128)S(1)} %add.91), channel_id=1, source_target_pairs={{0,2},{1,3},{2,0},{3,1},{4,6},{5,7},{6,4},{7,5},{8,10},{9,11},{10,... | collective-permute-start | bytes 82952 | tf_op jit(solution)/shard_map/ppermute | solution.py:121
  113.9 2.7 %collective-permute-start.6 = (f32[54,128]{1,0:T(8,128)S(1)}, f32[54,128]{1,0:T(8,128)S(1)}, u32[]{:S(2)}, u32[]{:S(2)}) collective-permute-start(f32[54,128]{1,0:T(8,128)S(1)} %add.98), channel_id=1, source_target_pairs={{0,4},{1,5},{2,6},{3,7},{4,0},{5,1},{6,2},{7,3},{8,12},{9,13},{10,... | collective-permute-start | bytes 82952 | tf_op jit(solution)/shard_map/ppermute | solution.py:121
  116.6 4.2 %collective-permute-start.7 = (f32[54,128]{1,0:T(8,128)S(1)}, f32[54,128]{1,0:T(8,128)S(1)}, u32[]{:S(2)}, u32[]{:S(2)}) collective-permute-start(f32[54,128]{1,0:T(8,128)S(1)} %add.99), channel_id=1, source_target_pairs={{0,8},{1,9},{2,10},{3,11},{4,12},{5,13},{6,14},{7,15},{8,0},{9,1},... | collective-permute-start | bytes 82952 | tf_op jit(solution)/shard_map/ppermute | solution.py:121
  120.8 11.2 %collective-permute-start.8 = (f32[54,128]{1,0:T(8,128)S(1)}, f32[54,128]{1,0:T(8,128)S(1)}, u32[]{:S(2)}, u32[]{:S(2)}) collective-permute-start(f32[54,128]{1,0:T(8,128)S(1)} %add.100), channel_id=1, source_target_pairs={{0,16},{16,0},{32,48},{48,32},{64,80},{80,64},{96,112},{112,96},{1... | collective-permute-start | bytes 82952 | tf_op jit(solution)/shard_map/ppermute | solution.py:121
  122.6 26.5 %all-to-all-start.1 = ((f32[16,20,6,128]{3,1,2,0:T(8,128)}), f32[16,20,6,128]{3,1,2,0:T(8,128)S(1)}, u32[]{:S(2)}, u32[]{:S(2)}) async-start(f32[16,20,6,128]{3,1,2,0:T(8,128)} %fusion.12), calls=%async_computation.1 | async-start | bytes 2359296 | tf_op jit(solution)/shard_map/all_to_all | solution.py:194
  132.1 2.8 %collective-permute-start.9 = (f32[54,128]{1,0:T(8,128)S(1)}, f32[54,128]{1,0:T(8,128)S(1)}, u32[]{:S(2)}, u32[]{:S(2)}) collective-permute-start(f32[54,128]{1,0:T(8,128)S(1)} %add.101), channel_id=1, source_target_pairs={{0,32},{16,48},{32,0},{48,16},{64,96},{80,112},{96,64},{112,80},{1... | collective-permute-start | bytes 82952 | tf_op jit(solution)/shard_map/ppermute | solution.py:121
  134.9 4.9 %collective-permute-start.14 = (f32[54,128]{1,0:T(8,128)S(1)}, f32[54,128]{1,0:T(8,128)S(1)}, u32[]{:S(2)}, u32[]{:S(2)}) collective-permute-start(f32[54,128]{1,0:T(8,128)S(1)} %add.102), channel_id=1, source_target_pairs={{0,64},{16,80},{32,96},{48,112},{64,0},{80,16},{96,32},{112,48},{1... | collective-permute-start | bytes 82952 | tf_op jit(solution)/shard_map/ppermute | solution.py:121
  (22 other events, 41.1 us)

commit v6 on v4

--- a/solution.py
+++ b/solution.py
@@ -171,7 +171,7 @@
     weight_grads, first_delta = network_vjp(weights, band[:, : 2 * levels], band[:, 2 * levels :])
     packed = pack(weight_grads)
     packed, plane_halo = lax.optimization_barrier((packed, plane_halo))
-    total, first_delta = butterfly_sum(packed, ("lon", "lat"), first_delta)
+    total, first_delta = butterfly_sum(packed, ("lat", "lon"), first_delta)
     summed = unpack(total, weight_grads)
     band_grad = input_pullback(weights, first_delta, 2 * levels)
     returned = lax.all_to_all(band_grad, "lon", split_axis=0, concat_axis=0, tiled=True)

time: 153 us -> 159 us (1.039)
  waiting for transfers between devices: 17.1 us -> 21.1 us
  starting transfers between devices: 38 us -> 40.8 us
    ppermute x7, waiting for transfers between devices: 6.66 us -> 15.4 us  [butterfly_sum(): values = values + lax.ppermute(values, axis, pairs)]
    ppermute x2, waiting for transfers between devices: 6.7 us -> 1.56 us  [edges(): right = lax.ppermute(block[..., :, :1], 'lon', ring('lon', -1))]
    ppermute x7, starting transfers between devices: 10.6 us -> 14.4 us  [butterfly_sum(): values = values + lax.ppermute(values, axis, pairs)]
    ppermute x2, starting transfers between devices: 5.48 us -> 7.94 us  [edges(): above = lax.ppermute(block[..., :1, :], 'lat', ring('lat', -1))]
    all_to_all x1, starting transfers between devices: 7.02 us -> 5.22 us  [on_device(): lax.all_to_all(band_grad, 'lon', split_axis=0, concat_axis=0, tiled=True)]
  transfers between devices with their start and end apart: 17 -> 17, of which waited for: 8 -> 7; matrix products, arithmetic and copies ran while one was open for 48% -> 46% of each run, Pallas kernels for 0% -> 0%
where the time goes in v6:
time: 159 us; the launch traced here: 158 us
  local copies, waits for them, and re-layouts  58.7 us (37%)
  starting transfers between devices  40.8 us (26%)
  waiting for transfers between devices  21.1 us (13%)
  other arithmetic  19.1 us (12%)
  matrix products  17.5 us (11%)
    ppermute x7, waiting for transfers between devices, butterfly_sum(): values = values + lax.ppermute(values, axis, pairs)  15.4 us
    ppermute x7, starting transfers between devices, butterfly_sum(): values = values + lax.ppermute(values, axis, pairs)  14.4 us
    unnamed x62, local copies, waits for them, and re-layouts  9.37 us
    ppermute x2, starting transfers between devices, edges(): above = lax.ppermute(block[..., :1, :], 'lat', ring('lat', -1))  7.94 us
    all_to_all x1, starting transfers between devices, on_device(): lax.all_to_all(chunks.transpose(2, 0, 1, 3), 'lon', split_axis=0, concat_...  6.95 us
    slice x9, local copies, waits for them, and re-layouts, part(): return tuple((piece[lo:hi] for piece in (below, above, left, right)))  6.86 us
    slice x2, local copies, waits for them, and re-layouts, edges(): right = lax.ppermute(block[..., :, :1], 'lon', ring('lon', -1))  6.68 us
    slice x12, local copies, waits for them, and re-layouts, lon_roll(): jnp.roll(values[..., -1:], 1, axis=0)  5.48 us
  transfers between devices with their start and end apart: 17, of which 7 were waited for; matrix products, arithmetic and copies ran while one was open for 46% of the time, Pallas kernels for 0%

profile of v6, /device:TPU:1, one launch (start us, length us, event | category | flops | bytes accessed | tf_op | source)
XLA Modules:
  0.0 158.4 jit_solution(12049872469211343752)
XLA Ops:
  6.0 2.4 %copy.169 = f32[40,6,16,128]{3,0,1,2:T(8,128)} copy(f32[40,6,16,128]{3,2,1,0:T(8,128)S(1)} %bitcast.76) | data formatting | bytes 3932160 | tf_op jit(solution)/shard_map/reshape | solution.py:169
  8.4 6.9 %all-to-all-start = ((f32[16,40,6,128]{3,1,2,0:T(8,128)}), f32[16,40,6,128]{3,1,2,0:T(8,128)S(1)}, u32[]{:S(2)}, u32[]{:S(2)}) async-start(f32[16,40,6,128]{3,1,2,0:T(8,128)} %bitcast.75), calls=%async_computation | async-start | bytes 3932160 | tf_op jit(solution)/shard_map/all_to_all | solution.py:170
  18.2 2.6 %collective-permute-start = (f32[32,1,128]{2,1,0:T(1,128)}, f32[32,1,128]{2,1,0:T(1,128)}, u32[]{:S(2)}, u32[]{:S(2)}) collective-permute-start(f32[32,1,128]{2,1,0:T(1,128)} %get-tuple-element.68), channel_id=1, source_target_pairs={{0,16},{16,32},{32,48},{48,64},{64,80},{80,96},{96,112},{112,0},{1... | collective-permute-start | bytes 49160 | tf_op jit(solution)/shard_map/ppermute | solution.py:19
  20.8 3.5 %collective-permute-start.1 = (f32[32,1,128]{2,1,0:T(1,128)}, f32[32,1,128]{2,1,0:T(1,128)}, u32[]{:S(2)}, u32[]{:S(2)}) collective-permute-start(f32[32,1,128]{2,1,0:T(1,128)} %get-tuple-element.67), channel_id=1, source_target_pairs={{0,112},{16,0},{32,16},{48,32},{64,48},{80,64},{96,80},{112,96},{1... | collective-permute-start | bytes 49160 | tf_op jit(solution)/shard_map/ppermute | solution.py:20
  24.3 4.2 %fusion.78 = (f32[32,96,1]{2,1,0:T(8,128)}, f32[32,96,1]{2,1,0:T(8,128)}) fusion(f32[32,96,128]{2,1,0:T(8,128)} %bitcast_dynamic-update-slice_fusion), kind=kLoop, calls=%fused_computation.110 | loop fusion | bytes 49152 | tf_op jit(solution)/shard_map/slice | solution.py:22
  28.5 2.5 %copy.121 = f32[32,96,1]{1,0,2:T(8,128)} copy(f32[32,96,1]{2,1,0:T(8,128)} %get-tuple-element.66) | data formatting | bytes 24576 | tf_op jit(solution)/shard_map/slice | solution.py:21
  32.3 2.5 %copy.122 = f32[32,96,1]{1,0,2:T(8,128)} copy(f32[32,96,1]{2,1,0:T(8,128)} %get-tuple-element.65) | data formatting | bytes 24576 | tf_op jit(solution)/shard_map/slice | solution.py:22
  47.5 2.7 %convolution_bitcast_fusion.1 = f32[16,96,6,128]{3,1,2,0:T(8,128)S(1)} fusion(f32[20,96,1,1]{1,0,2,3:T(8,128)} %reshape.79, f32[16,40,6,128]{3,1,2,0:T(8,128)S(1)} %all-to-all-done), kind=kOutput, calls=%fused_computation.10 | convolution fusion | flops 141557760 | bytes 5905920 | tf_op jit(solution)/shard_map/oc,soml->scml/dot_general | solution.py:92
  56.9 4.0 %fusion.9 = (f32[16,32,6,128]{3,1,2,0:T(8,128)S(1)}, f32[16,32,6,128]{3,1,2,0:T(8,128)S(1)}) fusion(f32[16,96,6,128]{3,1,2,0:T(8,128)S(1)} %convolution_bitcast_fusion.1, f32[1,32,6,1]{3,1,2,0:T(8,128)S(1)} %get-tuple-element.46, f32[15,32,6,1]{3,1,2,0:T(8,128)S(1)} %get-tuple-element.48, f32[16,32,6,127]{3,1,2,0:T(8,128)S(1)} %get-tuple-element.50, ...), kind=kOutput, calls=%fused_computation.19 | convolution fusion | flops 237109248 | bytes 12595200 | tf_op jit(solution)/shard_map/oc,scml->soml/dot_general | solution.py:80
  62.1 2.3 %fusion.19 = f32[32,96]{1,0:T(8,128)S(1)} fusion(f32[16,32,6,128]{3,1,2,0:T(8,128)S(1)} %get-tuple-element.120, f32[1,32,6,1]{3,1,2,0:T(8,128)S(1)} %get-tuple-element.76, f32[15,32,6,1]{3,1,2,0:T(8,128)S(1)} %get-tuple-element.78, f32[16,32,6,127]{3,1,2,0:T(8,128)S(1)} %get-tuple-element.80, f32[16,32,6,128]{3,1,2,0:T(8,128)S(1)} %tanh_bitcast_fusion.1, ...), kind=kOutput, calls=%fused_computation.28 | convolution fusion | flops 233570304 | bytes 6303744 | tf_op jit(solution)/shard_map/soml,scml->oc/dot_general | solution.py:94
  64.5 2.0 %convolution_bitcast_fusion = f32[16,96,6,128]{3,1,2,0:T(8,128)S(1)} fusion(f32[16,32,6,128]{3,1,2,0:T(8,128)S(1)} %get-tuple-element.120, f32[32,96,1,1]{1,0,2,3:T(8,128)S(1)} %reshape.81), kind=kOutput, calls=%fused_computation.9 | convolution fusion | flops 226492416 | bytes 6303744 | tf_op jit(solution)/shard_map/oc,soml->scml/dot_general | solution.py:95
  66.6 2.6 %fusion.66 = (f32[15,32,6,1]{3,1,2,0:T(8,128)}, f32[15,32,6,1]{3,1,2,0:T(8,128)}) fusion(f32[16,96,6,128]{3,1,2,0:T(8,128)S(1)} %convolution_bitcast_fusion), kind=kLoop, calls=%fused_computation.98 | loop fusion | bytes 46080 | tf_op jit(solution)/shard_map/jit(_roll_static)/slice | solution.py:52
  69.6 2.2 %fusion.67 = (f32[16,32,6,127]{3,1,2,0:T(8,128)}, f32[16,32,6,127]{3,1,2,0:T(8,128)}) fusion(f32[16,96,6,128]{3,1,2,0:T(8,128)S(1)} %convolution_bitcast_fusion), kind=kLoop, calls=%fused_computation.99 | loop fusion | bytes 6242304 | tf_op jit(solution)/shard_map/slice | solution.py:52
  71.8 2.4 %fusion.24 = f32[20,96]{1,0:T(8,128)S(1)} fusion(f32[16,20,6,128]{3,1,2,0:T(8,128)S(1)} %get-tuple-element.57, f32[1,32,6,1]{3,1,2,0:T(8,128)S(1)} %get-tuple-element.70, f32[15,32,6,1]{3,1,2,0:T(8,128)S(1)} %get-tuple-element.72, f32[16,32,6,127]{3,1,2,0:T(8,128)S(1)} %get-tuple-element.74, f32[16,32,6,128]{3,1,2,0:T(8,128)S(1)} %get-tuple-element.121, ...), kind=kOutput, calls=%fused_computation.29 | convolution fusion | flops 148635648 | bytes 5709312 | tf_op jit(solution)/shard_map/soml,scml->oc/dot_general | solution.py:91
  74.5 4.5 %fusion.7 = f32[16,32,6,128]{3,1,2,0:T(8,128)S(1)} fusion(f32[16,96,6,128]{3,1,2,0:T(8,128)} %copy-done, f32[1,32,6,1]{3,1,2,0:T(8,128)S(1)} %get-tuple-element.40, f32[15,32,6,1]{3,1,2,0:T(8,128)} %get-tuple-element.42, f32[16,32,6,127]{3,1,2,0:T(8,128)} %get-tuple-element.44, f32[16,32,6,127]{3,1,2,0:T(8,128)} %get-tuple-element.43, ...), kind=kLoop, calls=%fused_computation.16 | loop fusion | flops 3538944 | bytes 7864320 | tf_op jit(solution)/shard_map/mul | solution.py:96
  88.8 4.3 %fusion.44 = (f32[10,96,128]{2,1,0:T(8,128)S(1)}, f32[10,96,128]{2,1,0:T(8,128)S(1)}, f32[10,96,128]{2,1,0:T(8,128)}, f32[10,96,128]{2,1,0:T(8,128)}, f32[10,96,128]{2,1,0:T(8,128)}) fusion(f32[10,96,128]{2,1,0:T(8,128)S(1)} %copy-done.1, f32[10,96,1]{2,1,0:T(8,128)} %copy.130, f32[10,96,127]{2,1,0:T(8,128)} %get-tuple-element.127, ...), kind=kLoop, calls=%fused_computation.54 | loop fusion | flops 3563520 | bytes 7618560 | tf_op jit(solution)/shard_map/mul | solution.py:192
  99.7 3.4 %collective-permute-start.10 = (f32[54,128]{1,0:T(8,128)S(1)}, f32[54,128]{1,0:T(8,128)S(1)}, u32[]{:S(2)}, u32[]{:S(2)}) collective-permute-start(f32[54,128]{1,0:T(8,128)S(1)} %add.102), channel_id=1, source_target_pairs={{0,64},{16,80},{32,96},{48,112},{64,0},{80,16},{96,32},{112,48},{1... | collective-permute-start | bytes 82952 | tf_op jit(solution)/shard_map/ppermute | solution.py:117
  104.4 4.7 %collective-permute-start.11 = (f32[54,128]{1,0:T(8,128)S(1)}, f32[54,128]{1,0:T(8,128)S(1)}, u32[]{:S(2)}, u32[]{:S(2)}) collective-permute-start(f32[54,128]{1,0:T(8,128)S(1)} %add.103), channel_id=1, source_target_pairs={{0,1},{1,0},{2,3},{3,2},{4,5},{5,4},{6,7},{7,6},{8,9},{9,8},{10,11... | collective-permute-start | bytes 82952 | tf_op jit(solution)/shard_map/ppermute | solution.py:117
  111.8 5.2 %all-to-all-start.1 = ((f32[16,20,6,128]{3,1,2,0:T(8,128)}), f32[16,20,6,128]{3,1,2,0:T(8,128)S(1)}, u32[]{:S(2)}, u32[]{:S(2)}) async-start(f32[16,20,6,128]{3,1,2,0:T(8,128)} %fusion.12), calls=%async_computation.1 | async-start | bytes 2359296 | tf_op jit(solution)/shard_map/all_to_all | solution.py:177
  119.4 12.8 %collective-permute-done.13 = f32[54,128]{1,0:T(8,128)S(1)} collective-permute-done((f32[54,128]{1,0:T(8,128)S(1)}, f32[54,128]{1,0:T(8,128)S(1)}, u32[]{:S(2)}, u32[]{:S(2)}) %collective-permute-start.13) | collective-permute-done | bytes 27680 | tf_op jit(solution)/shard_map/ppermute | solution.py:117
  132.3 2.7 %collective-permute-start.14 = (f32[54,128]{1,0:T(8,128)S(1)}, f32[54,128]{1,0:T(8,128)S(1)}, u32[]{:S(2)}, u32[]{:S(2)}) collective-permute-start(f32[54,128]{1,0:T(8,128)S(1)} %add.106), channel_id=1, source_target_pairs={{0,8},{1,9},{2,10},{3,11},{4,12},{5,13},{6,14},{7,15},{8,0},{9,1},... | collective-permute-start | bytes 82952 | tf_op jit(solution)/shard_map/ppermute | solution.py:117
  139.4 4.5 %collective-permute-start.7 = (f32[10,1,128]{2,1,0:T(1,128)S(1)}, f32[10,1,128]{2,1,0:T(1,128)S(1)}, u32[]{:S(2)}, u32[]{:S(2)}) collective-permute-start(f32[10,1,128]{2,1,0:T(1,128)S(1)} %get-tuple-element.84), channel_id=1, source_target_pairs={{0,112},{16,0},{32,16},{48,32},{64,48},{80,64},{96,80},{112,96},{1... | collective-permute-start | bytes 15368 | tf_op jit(solution)/shard_map/ppermute | solution.py:20
  151.6 2.5 %collective-permute-done.7 = f32[10,1,128]{2,1,0:T(1,128)S(1)} collective-permute-done((f32[10,1,128]{2,1,0:T(1,128)S(1)}, f32[10,1,128]{2,1,0:T(1,128)S(1)}, u32[]{:S(2)}, u32[]{:S(2)}) %collective-permute-start.7) | collective-permute-done | bytes 5152 | tf_op jit(solution)/shard_map/ppermute | solution.py:20
  155.8 2.6 %fusion.53 = f32[10,96,128]{2,1,0:T(8,128)} fusion(f32[10,96,128]{2,1,0:T(8,128)S(1)} %copy-done.1, f32[10,96,128]{2,1,0:T(8,128)S(1)} %copy-done.11, f32[10,96,128]{2,1,0:T(8,128)S(1)} %get-tuple-element.34, f32[10,96,1]{2,1,0:T(8,128)} %collective-permute-done.5, f32[10,96,127]{2,1,0:T(8,128)S(1)} %copy-done.20, f32[10,96,128]{2,1,0:T(8,128)S(1)} %copy-done.10, ...), kind=kLoop, calls=%fused_computation.67 | loop fusion | flops 2088960 | bytes 5898240 | tf_op jit(solution)/shard_map/add | solution.py:196
  (167 shorter events, 66.9 us)
Async XLA Ops:
  8.4 7.0 %copy-start.26 = (f32[96,128]{1,0:T(8,128)S(1)}, f32[96,128]{1,0:T(8,128)}, u32[]{:S(2)}) copy-start(f32[96,128]{1,0:T(8,128)} %param.16) | copy-start | bytes 147460
  8.4 7.6 %copy-start.25 = (f32[96,128]{1,0:T(8,128)S(1)}, f32[96,128]{1,0:T(8,128)}, u32[]{:S(2)}) copy-start(f32[96,128]{1,0:T(8,128)} %param.17) | copy-start | bytes 147460
  8.4 39.1 %all-to-all-start = ((f32[16,40,6,128]{3,1,2,0:T(8,128)}), f32[16,40,6,128]{3,1,2,0:T(8,128)S(1)}, u32[]{:S(2)}, u32[]{:S(2)}) async-start(f32[16,40,6,128]{3,1,2,0:T(8,128)} %bitcast.75), calls=%async_computation | async-start | bytes 3932160 | tf_op jit(solution)/shard_map/all_to_all | solution.py:170
  18.2 63.7 %collective-permute-start = (f32[32,1,128]{2,1,0:T(1,128)}, f32[32,1,128]{2,1,0:T(1,128)}, u32[]{:S(2)}, u32[]{:S(2)}) collective-permute-start(f32[32,1,128]{2,1,0:T(1,128)} %get-tuple-element.68), channel_id=1, source_target_pairs={{0,16},{16,32},{32,48},{48,64},{64,80},{80,96},{96,112},{112,0},{1... | collective-permute-start | bytes 49160 | tf_op jit(solution)/shard_map/ppermute | solution.py:19
  20.8 61.1 %collective-permute-start.1 = (f32[32,1,128]{2,1,0:T(1,128)}, f32[32,1,128]{2,1,0:T(1,128)}, u32[]{:S(2)}, u32[]{:S(2)}) collective-permute-start(f32[32,1,128]{2,1,0:T(1,128)} %get-tuple-element.67), channel_id=1, source_target_pairs={{0,112},{16,0},{32,16},{48,32},{64,48},{80,64},{96,80},{112,96},{1... | collective-permute-start | bytes 49160 | tf_op jit(solution)/shard_map/ppermute | solution.py:20
  31.0 50.9 %collective-permute-start.2 = (f32[32,96,1]{1,0,2:T(8,128)}, f32[32,96,1]{1,0,2:T(8,128)}, u32[]{:S(2)}, u32[]{:S(2)}) collective-permute-start(f32[32,96,1]{1,0,2:T(8,128)} %copy.121), channel_id=1, source_target_pairs={{0,1},{1,2},{2,3},{3,4},{4,5},{5,6},{6,7},{7,8},{8,9},{9,10},{10,1... | collective-permute-start | bytes 36872 | tf_op jit(solution)/shard_map/ppermute | solution.py:21
  34.8 47.1 %collective-permute-start.3 = (f32[32,96,1]{1,0,2:T(8,128)}, f32[32,96,1]{1,0,2:T(8,128)}, u32[]{:S(2)}, u32[]{:S(2)}) collective-permute-start(f32[32,96,1]{1,0,2:T(8,128)} %copy.122), channel_id=1, source_target_pairs={{0,15},{1,0},{2,1},{3,2},{4,3},{5,4},{6,5},{7,6},{8,7},{9,8},{10,9... | collective-permute-start | bytes 36872 | tf_op jit(solution)/shard_map/ppermute | solution.py:22
  81.6 7.2 %copy-start.8 = (s32[10,96,128]{2,1,0:T(8,128)S(1)}, s32[10,96,128]{2,1,0:T(8,128)}, u32[]{:S(2)}) copy-start(s32[10,96,128]{2,1,0:T(8,128)} %param.15) | copy-start | bytes 1474564
  81.7 7.2 %copy-start.12 = (f32[10,96,127]{2,1,0:T(8,128)S(1)}, f32[10,96,127]{2,1,0:T(8,128)}, u32[]{:S(2)}) copy-start(f32[10,96,127]{2,1,0:T(8,128)} %get-tuple-element.95) | copy-start | bytes 1463044
  81.7 7.2 %copy-start.28 = (f32[96,128]{1,0:T(8,128)S(1)}, f32[96,128]{1,0:T(8,128)}, u32[]{:S(2)}) copy-start(f32[96,128]{1,0:T(8,128)} %param.18) | copy-start | bytes 147460
  88.3 7.1 %collective-permute-start.4 = (f32[54,128]{1,0:T(8,128)S(1)}, f32[54,128]{1,0:T(8,128)S(1)}, u32[]{:S(2)}, u32[]{:S(2)}) collective-permute-start(f32[54,128]{1,0:T(8,128)S(1)} %maximum_bitcast_fusion), channel_id=1, source_target_pairs={{0,16},{16,0},{32,48},{48,32},{64,80},{80,64},{96,112},{112,96},{1... | collective-permute-start | bytes 82952 | tf_op jit(solution)/shard_map/ppermute | solution.py:117
  96.8 3.0 %collective-permute-start.9 = (f32[54,128]{1,0:T(8,128)S(1)}, f32[54,128]{1,0:T(8,128)S(1)}, u32[]{:S(2)}, u32[]{:S(2)}) collective-permute-start(f32[54,128]{1,0:T(8,128)S(1)} %add.91), channel_id=1, source_target_pairs={{0,32},{16,48},{32,0},{48,16},{64,96},{80,112},{96,64},{112,80},{1... | collective-permute-start | bytes 82952 | tf_op jit(solution)/shard_map/ppermute | solution.py:117
  99.7 4.7 %collective-permute-start.10 = (f32[54,128]{1,0:T(8,128)S(1)}, f32[54,128]{1,0:T(8,128)S(1)}, u32[]{:S(2)}, u32[]{:S(2)}) collective-permute-start(f32[54,128]{1,0:T(8,128)S(1)} %add.102), channel_id=1, source_target_pairs={{0,64},{16,80},{32,96},{48,112},{64,0},{80,16},{96,32},{112,48},{1... | collective-permute-start | bytes 82952 | tf_op jit(solution)/shard_map/ppermute | solution.py:117
  104.4 5.6 %collective-permute-start.11 = (f32[54,128]{1,0:T(8,128)S(1)}, f32[54,128]{1,0:T(8,128)S(1)}, u32[]{:S(2)}, u32[]{:S(2)}) collective-permute-start(f32[54,128]{1,0:T(8,128)S(1)} %add.103), channel_id=1, source_target_pairs={{0,1},{1,0},{2,3},{3,2},{4,5},{5,4},{6,7},{7,6},{8,9},{9,8},{10,11... | collective-permute-start | bytes 82952 | tf_op jit(solution)/shard_map/ppermute | solution.py:117
  110.0 7.0 %collective-permute-start.12 = (f32[54,128]{1,0:T(8,128)S(1)}, f32[54,128]{1,0:T(8,128)S(1)}, u32[]{:S(2)}, u32[]{:S(2)}) collective-permute-start(f32[54,128]{1,0:T(8,128)S(1)} %add.104), channel_id=1, source_target_pairs={{0,2},{1,3},{2,0},{3,1},{4,6},{5,7},{6,4},{7,5},{8,10},{9,11},{10,... | collective-permute-start | bytes 82952 | tf_op jit(solution)/shard_map/ppermute | solution.py:117
  111.8 34.3 %all-to-all-start.1 = ((f32[16,20,6,128]{3,1,2,0:T(8,128)}), f32[16,20,6,128]{3,1,2,0:T(8,128)S(1)}, u32[]{:S(2)}, u32[]{:S(2)}) async-start(f32[16,20,6,128]{3,1,2,0:T(8,128)} %fusion.12), calls=%async_computation.1 | async-start | bytes 2359296 | tf_op jit(solution)/shard_map/all_to_all | solution.py:177
  117.0 15.3 %collective-permute-start.13 = (f32[54,128]{1,0:T(8,128)S(1)}, f32[54,128]{1,0:T(8,128)S(1)}, u32[]{:S(2)}, u32[]{:S(2)}) collective-permute-start(f32[54,128]{1,0:T(8,128)S(1)} %add.105), channel_id=1, source_target_pairs={{0,4},{1,5},{2,6},{3,7},{4,0},{5,1},{6,2},{7,3},{8,12},{9,13},{10,... | collective-permute-start | bytes 82952 | tf_op jit(solution)/shard_map/ppermute | solution.py:117
  132.3 11.6 %collective-permute-start.14 = (f32[54,128]{1,0:T(8,128)S(1)}, f32[54,128]{1,0:T(8,128)S(1)}, u32[]{:S(2)}, u32[]{:S(2)}) collective-permute-start(f32[54,128]{1,0:T(8,128)S(1)} %add.106), channel_id=1, source_target_pairs={{0,8},{1,9},{2,10},{3,11},{4,12},{5,13},{6,14},{7,15},{8,0},{9,1},... | collective-permute-start | bytes 82952 | tf_op jit(solution)/shard_map/ppermute | solution.py:117
  137.0 14.6 %collective-permute-start.5 = (f32[10,96,1]{2,1,0:T(8,128)}, f32[10,96,1]{2,1,0:T(8,128)}, u32[]{:S(2)}, u32[]{:S(2)}) collective-permute-start(f32[10,96,1]{2,1,0:T(8,128)} %get-tuple-element.88), channel_id=1, source_target_pairs={{0,15},{1,0},{2,1},{3,2},{4,3},{5,4},{6,5},{7,6},{8,7},{9,8},{10,9... | collective-permute-start | bytes 11528 | tf_op jit(solution)/shard_map/ppermute | solution.py:22
  138.5 13.1 %collective-permute-start.6 = (f32[10,96,1]{2,1,0:T(8,128)}, f32[10,96,1]{2,1,0:T(8,128)}, u32[]{:S(2)}, u32[]{:S(2)}) collective-permute-start(f32[10,96,1]{2,1,0:T(8,128)} %get-tuple-element.87), channel_id=1, source_target_pairs={{0,1},{1,2},{2,3},{3,4},{4,5},{5,6},{6,7},{7,8},{8,9},{9,10},{10,1... | collective-permute-start | bytes 11528 | tf_op jit(solution)/shard_map/ppermute | solution.py:21
  139.4 14.7 %collective-permute-start.7 = (f32[10,1,128]{2,1,0:T(1,128)S(1)}, f32[10,1,128]{2,1,0:T(1,128)S(1)}, u32[]{:S(2)}, u32[]{:S(2)}) collective-permute-start(f32[10,1,128]{2,1,0:T(1,128)S(1)} %get-tuple-element.84), channel_id=1, source_target_pairs={{0,112},{16,0},{32,16},{48,32},{64,48},{80,64},{96,80},{112,96},{1... | collective-permute-start | bytes 15368 | tf_op jit(solution)/shard_map/ppermute | solution.py:20
  143.8 11.9 %collective-permute-start.8 = (f32[10,1,128]{2,1,0:T(1,128)S(1)}, f32[10,1,128]{2,1,0:T(1,128)S(1)}, u32[]{:S(2)}, u32[]{:S(2)}) collective-permute-start(f32[10,1,128]{2,1,0:T(1,128)S(1)} %get-tuple-element.83), channel_id=1, source_target_pairs={{0,16},{16,32},{32,48},{48,64},{64,80},{80,96},{96,112},{112,0},{1... | collective-permute-start | bytes 15368 | tf_op jit(solution)/shard_map/ppermute | solution.py:19
  148.3 7.4 %copy-start.21 = (f32[10,95,128]{2,1,0:T(8,128)S(1)}, f32[10,95,128]{2,1,0:T(8,128)}, u32[]{:S(2)}) copy-start(f32[10,95,128]{2,1,0:T(8,128)} %get-tuple-element.85) | copy-start | bytes 1459204
  148.3 7.4 %copy-start.22 = (f32[10,95,128]{2,1,0:T(8,128)S(1)}, f32[10,95,128]{2,1,0:T(8,128)}, u32[]{:S(2)}) copy-start(f32[10,95,128]{2,1,0:T(8,128)} %get-tuple-element.86) | copy-start | bytes 1459204
  (22 other events, 55.7 us)
